TPU v7x, 32 devices: a whole 2x2x4 slice. The times are simulated.
32 devices in a mesh: comp: 4 (over y, x), band: 8 (over z, core).
Axes of the slice: x: 2, y: 2, z: 4, core: 2. Of those that a mesh axis runs over, the one named last changes fastest.
Arguments:
- estimate: float32 [512, 256], P('band'), may hold values from -6 to 6
- residual: float32 [512, 256], P('band'), may hold values from -50 to 50
- direction: float32 [512, 256], P('band'), may hold values from -50 to 50
- kernels: bfloat16 [32, 65, 65], P('comp'), may hold values from -0.015625 to 0.015625
- weight_maps: bfloat16 [32, 512, 256], P('comp', 'band'), may hold values from -6 to 6
- filters_in: float32 [64, 3, 3], replicated, may hold values from -2 to 2
- biases: float32 [64], replicated, may hold values from -3 to 3
- filters_out: float32 [64, 3, 3], replicated, may hold values from -0.25 to 0.25
Outputs:
- estimate_next: float32 [512, 256], P('band')
- residual_next: float32 [512, 256], P('band')
- direction_next: float32 [512, 256], P('band')
- denoised: float32 [512, 256], P('band', 'comp')
All inputs are finite; a program needn't handle non-finite values.
Results may differ from a plain program's by a relative error of at most 0.0024.
Values may be sent and summed in bfloat16 or wider, within the bound.
No kernel may reach another device: no remote copies, remote signals or barrier semaphores. Data moves between devices by JAX's collectives and lax.ppermute only.
A program may use at most 64 MiB of HBM per device.

v0:
```python
import jax
import jax.numpy as jnp
from jax import lax
from jax.sharding import PartitionSpec as P

damping = 0.5


def with_halo(array, sides, width):
    for axis, dim in sides:
        count, length = (lax.axis_size(axis), array.shape[dim])
        up = [(i, (i + 1) % count) for i in range(count - 1)]
        down = [(j, i) for i, j in up]
        last = lax.slice_in_dim(array, length - width, length, axis=dim)
        first = lax.slice_in_dim(array, 0, width, axis=dim)
        before = lax.ppermute(last, axis, up)
        after = lax.ppermute(first, axis, down)
        array = jnp.concatenate([before, array, after], axis=dim)
    return array


def denoise(estimate_next, filters_in, biases, filters_out):
    rows, width = estimate_next.shape
    framed = with_halo(estimate_next, (("band", 0),), 2)
    columns = width // lax.axis_size("comp")
    start = lax.axis_index("comp") * columns
    padded = jnp.pad(framed, ((0, 0), (2, 2)))
    tile = lax.dynamic_slice_in_dim(padded, start, columns + 4, 1)
    taps = jnp.stack(
        [tile[a : a + rows + 2, b : b + columns + 2] for a in range(3) for b in range(3)]
    )
    channels = filters_in.shape[0]
    features = jnp.einsum(
        "ct,tij->cij", filters_in.reshape(channels, 9), taps, precision=lax.Precision.HIGHEST
    )
    features = jax.nn.relu(features + biases[:, None, None])
    total_rows = rows * lax.axis_size("band")
    global_rows = lax.axis_index("band") * rows - 1 + jnp.arange(rows + 2)
    global_cols = start - 1 + jnp.arange(columns + 2)
    inside_rows = (global_rows >= 0) & (global_rows < total_rows)
    inside_cols = (global_cols >= 0) & (global_cols < width)
    inside = (inside_rows[:, None] & inside_cols[None, :]).astype(jnp.float32)
    features = features * inside[None]
    spread = jnp.einsum(
        "ct,cij->tij", filters_out.reshape(channels, 9), features, precision=lax.Precision.HIGHEST
    )
    mixed = sum(
        (spread[a * 3 + b, a : a + rows, b : b + columns] for a in range(3) for b in range(3))
    )
    return tile[2 : 2 + rows, 2 : 2 + columns] - mixed


def correlate(source, taps):
    span = taps.shape[0]
    half = (span - 1) // 2
    source_rows, width = source.shape
    out_rows = source_rows - span + 1
    count = width // 128
    framed = jnp.pad(source, ((0, 0), (half, 128 - half)))
    lower = framed[:, :width].reshape(source_rows, count, 128)
    upper = framed[:, 128 : width + 128].reshape(source_rows, count, 128)
    blocks = jnp.concatenate([lower, upper], axis=2)
    offsets = jnp.arange(span)[:, None] + jnp.arange(out_rows)[None, :]
    stacked = blocks[offsets]
    spacing = jnp.arange(256)[:, None] - jnp.arange(128)[None, :]
    valid = (spacing >= 0) & (spacing < span)
    toeplitz = jnp.where(
        valid[None], taps[:, jnp.clip(spacing, 0, span - 1)], jnp.zeros((), taps.dtype)
    )
    result = jnp.einsum("arnu,auv->rnv", stacked, toeplitz, preferred_element_type=jnp.float32)
    return result.reshape(out_rows, width)


def blur_all(sources, kernels, out_rows, width):

    def add_one(total, pair):
        source, taps = pair
        return (total + correlate(source, taps), None)

    result, unused = lax.scan(
        add_one, jnp.zeros((out_rows, width), jnp.float32), (sources, kernels)
    )
    return result


def per_device(
    estimate, residual, direction, kernels, weight_maps, filters_in, biases, filters_out
):
    rows, width = direction.shape
    half = (kernels.shape[1] - 1) // 2
    maps_wide = weight_maps.astype(jnp.float32)
    shaped = (maps_wide * direction[None]).astype(jnp.bfloat16)
    padded = with_halo(shaped, (("band", 1),), half)
    partial_value = blur_all(padded, kernels, rows, width)
    image = lax.psum(partial_value, "comp").astype(jnp.bfloat16)
    edged = with_halo(image, (("band", 0),), half)
    flipped = kernels[:, ::-1, ::-1]

    def add_back(total, pair):
        taps, weights = pair
        return (total + weights * correlate(edged, taps), None)

    local_sum, unused = lax.scan(
        add_back, jnp.zeros((rows, width), jnp.float32), (flipped, maps_wide)
    )
    normal = lax.psum(local_sum, "comp")
    curved = normal + damping * direction
    old, product, cross, square = lax.psum(
        (
            jnp.sum(residual * residual),
            jnp.sum(direction * curved),
            jnp.sum(residual * curved),
            jnp.sum(curved * curved),
        ),
        "band",
    )
    alpha = old / product
    residual_next = residual - alpha * curved
    new = old - 2.0 * alpha * cross + alpha * alpha * square
    estimate_next = estimate + alpha * direction
    direction_next = residual_next + new / old * direction
    denoised = denoise(estimate_next, filters_in, biases, filters_out)
    return (estimate_next, residual_next, direction_next, denoised)


def solution(mesh):
    return jax.shard_map(
        per_device,
        mesh=mesh,
        in_specs=(
            P("band", None),
            P("band", None),
            P("band", None),
            P("comp", None, None),
            P("comp", "band", None),
            P(),
            P(),
            P(),
        ),
        out_specs=(P("band", None), P("band", None), P("band", None), P("band", "comp")),
        check_vma=False,
    )
```

profile of v0, /device:TPU:0, one launch (start us, length us, event | category | flops | bytes accessed | tf_op | source)
XLA Modules:
  0.0 2489.0 jit_solution(3234788113476659042)
XLA Ops:
  16.2 1176.3 %while.26 = (s32[]{:T(128)}, f32[64,256]{1,0:T(8,128)S(1)}, bf16[8,128,256]{2,1,0:T(8,128)(2,1)S(1)}, bf16[8,65,65]{1,2,0:T(8,128)(2,1)S(1)}, s32[]{:T(128)}, /*index=5*/s32[]{:T(128)}) while((s32[]{:T(128)}, f32[64,256]{1,0:T(8,128)S(1)}, bf16[8,128,256]{2,1,0:T(8,128)(2,1)S(1)}, bf16[8,65,65]{1,2,0:T(8,128)(2,1)S(1)}, s32[]{:T(128)}, ...), condition=%wide.region_3.4_spmd.clone, body=%wide.region_2.3_spmd.clone.sunk | while | flops 548033792 | bytes 35641176 | solution.py:80
  16.6 16.3 gather_fusion.1
  32.9 114.9 %gather_fusion = bf16[32768,65]{1,0:T(8,128)(2,1)} fusion(bf16[65,65]{0,1:T(8,128)(2,1)S(1)} %dynamic-slice_bitcast_fusion.6, s32[32768]{0:T(1024)S(1)} %fusion.82), kind=kCustom, calls=%fused_computation.1.clone.clone.1 | custom fusion | bytes 8650752 | tf_op jit(solution)/shard_map/while/body/eval_jaxpr/gather | solution.py:68
  147.8 10.6 copy.46
  163.6 16.3 gather_fusion.1
  180.0 114.9 %gather_fusion = bf16[32768,65]{1,0:T(8,128)(2,1)} fusion(bf16[65,65]{0,1:T(8,128)(2,1)S(1)} %dynamic-slice_bitcast_fusion.6, s32[32768]{0:T(1024)S(1)} %fusion.82), kind=kCustom, calls=%fused_computation.1.clone.clone.1 | custom fusion | bytes 8650752 | tf_op jit(solution)/shard_map/while/body/eval_jaxpr/gather | solution.py:68
  294.9 10.6 copy.46
  310.7 16.3 gather_fusion.1
  327.0 114.9 %gather_fusion = bf16[32768,65]{1,0:T(8,128)(2,1)} fusion(bf16[65,65]{0,1:T(8,128)(2,1)S(1)} %dynamic-slice_bitcast_fusion.6, s32[32768]{0:T(1024)S(1)} %fusion.82), kind=kCustom, calls=%fused_computation.1.clone.clone.1 | custom fusion | bytes 8650752 | tf_op jit(solution)/shard_map/while/body/eval_jaxpr/gather | solution.py:68
  441.9 10.6 copy.46
  457.7 16.3 gather_fusion.1
  474.0 114.9 %gather_fusion = bf16[32768,65]{1,0:T(8,128)(2,1)} fusion(bf16[65,65]{0,1:T(8,128)(2,1)S(1)} %dynamic-slice_bitcast_fusion.6, s32[32768]{0:T(1024)S(1)} %fusion.82), kind=kCustom, calls=%fused_computation.1.clone.clone.1 | custom fusion | bytes 8650752 | tf_op jit(solution)/shard_map/while/body/eval_jaxpr/gather | solution.py:68
  588.9 10.6 copy.46
  604.8 16.3 gather_fusion.1
  621.1 114.9 %gather_fusion = bf16[32768,65]{1,0:T(8,128)(2,1)} fusion(bf16[65,65]{0,1:T(8,128)(2,1)S(1)} %dynamic-slice_bitcast_fusion.6, s32[32768]{0:T(1024)S(1)} %fusion.82), kind=kCustom, calls=%fused_computation.1.clone.clone.1 | custom fusion | bytes 8650752 | tf_op jit(solution)/shard_map/while/body/eval_jaxpr/gather | solution.py:68
  736.0 10.6 copy.46
  751.8 16.3 gather_fusion.1
  768.1 114.9 %gather_fusion = bf16[32768,65]{1,0:T(8,128)(2,1)} fusion(bf16[65,65]{0,1:T(8,128)(2,1)S(1)} %dynamic-slice_bitcast_fusion.6, s32[32768]{0:T(1024)S(1)} %fusion.82), kind=kCustom, calls=%fused_computation.1.clone.clone.1 | custom fusion | bytes 8650752 | tf_op jit(solution)/shard_map/while/body/eval_jaxpr/gather | solution.py:68
  883.0 10.6 copy.46
  898.8 16.3 gather_fusion.1
  915.2 114.9 %gather_fusion = bf16[32768,65]{1,0:T(8,128)(2,1)} fusion(bf16[65,65]{0,1:T(8,128)(2,1)S(1)} %dynamic-slice_bitcast_fusion.6, s32[32768]{0:T(1024)S(1)} %fusion.82), kind=kCustom, calls=%fused_computation.1.clone.clone.1 | custom fusion | bytes 8650752 | tf_op jit(solution)/shard_map/while/body/eval_jaxpr/gather | solution.py:68
  1030.1 10.6 copy.46
  1045.9 16.3 gather_fusion.1
  1062.2 114.9 %gather_fusion = bf16[32768,65]{1,0:T(8,128)(2,1)} fusion(bf16[65,65]{0,1:T(8,128)(2,1)S(1)} %dynamic-slice_bitcast_fusion.6, s32[32768]{0:T(1024)S(1)} %fusion.82), kind=kCustom, calls=%fused_computation.1.clone.clone.1 | custom fusion | bytes 8650752 | tf_op jit(solution)/shard_map/while/body/eval_jaxpr/gather | solution.py:68
  1177.1 10.6 copy.46
  1192.5 17.0 psum.43
  1217.6 1188.4 %while.27 = (s32[]{:T(128)}, f32[64,256]{1,0:T(8,128)S(1)}, f32[8,64,256]{2,1,0:T(8,128)S(1)}, bf16[128,256]{1,0:T(8,128)(2,1)S(1)}, bf16[8,65,65]{1,2,0:T(8,128)(2,1)S(1)}, /*index=5*/s32[]{:T(128)}, s32[]{:T(128)}) while((s32[]{:T(128)}, f32[64,256]{1,0:T(8,128)S(1)}, f32[8,64,256]{2,1,0:T(8,128)S(1)}, ...), condition=%wide.region_6.7_spmd.clone, body=%wide.region_5.6_spmd.clone.sunk | while | flops 548050176 | bytes 44095328 | solution.py:103
  1217.7 114.9 %gather_fusion.3 = bf16[32768,65]{1,0:T(8,128)(2,1)} fusion(bf16[65,65]{0,1:T(8,128)(2,1)S(1)} %dynamic-slice_bitcast_fusion.8, s32[32768]{0:T(1024)S(1)} %fusion.87), kind=kCustom, calls=%fused_computation.3.clone.clone.1 | custom fusion | bytes 8650752 | tf_op jit(solution)/shard_map/while/body/eval_jaxpr/gather | solution.py:68
  1343.5 16.3 gather_fusion.2
  1366.2 114.9 %gather_fusion.3 = bf16[32768,65]{1,0:T(8,128)(2,1)} fusion(bf16[65,65]{0,1:T(8,128)(2,1)S(1)} %dynamic-slice_bitcast_fusion.8, s32[32768]{0:T(1024)S(1)} %fusion.87), kind=kCustom, calls=%fused_computation.3.clone.clone.1 | custom fusion | bytes 8650752 | tf_op jit(solution)/shard_map/while/body/eval_jaxpr/gather | solution.py:68
  1481.1 10.5 copy.49
  1492.0 16.3 gather_fusion.2
  1514.8 114.9 %gather_fusion.3 = bf16[32768,65]{1,0:T(8,128)(2,1)} fusion(bf16[65,65]{0,1:T(8,128)(2,1)S(1)} %dynamic-slice_bitcast_fusion.8, s32[32768]{0:T(1024)S(1)} %fusion.87), kind=kCustom, calls=%fused_computation.3.clone.clone.1 | custom fusion | bytes 8650752 | tf_op jit(solution)/shard_map/while/body/eval_jaxpr/gather | solution.py:68
  1640.6 16.3 gather_fusion.2
  1663.3 114.9 %gather_fusion.3 = bf16[32768,65]{1,0:T(8,128)(2,1)} fusion(bf16[65,65]{0,1:T(8,128)(2,1)S(1)} %dynamic-slice_bitcast_fusion.8, s32[32768]{0:T(1024)S(1)} %fusion.87), kind=kCustom, calls=%fused_computation.3.clone.clone.1 | custom fusion | bytes 8650752 | tf_op jit(solution)/shard_map/while/body/eval_jaxpr/gather | solution.py:68
  1778.2 10.5 copy.49
  1789.1 16.3 gather_fusion.2
  1811.9 114.9 %gather_fusion.3 = bf16[32768,65]{1,0:T(8,128)(2,1)} fusion(bf16[65,65]{0,1:T(8,128)(2,1)S(1)} %dynamic-slice_bitcast_fusion.8, s32[32768]{0:T(1024)S(1)} %fusion.87), kind=kCustom, calls=%fused_computation.3.clone.clone.1 | custom fusion | bytes 8650752 | tf_op jit(solution)/shard_map/while/body/eval_jaxpr/gather | solution.py:68
  1926.8 10.5 copy.49
  1937.7 16.3 gather_fusion.2
  1960.4 114.9 %gather_fusion.3 = bf16[32768,65]{1,0:T(8,128)(2,1)} fusion(bf16[65,65]{0,1:T(8,128)(2,1)S(1)} %dynamic-slice_bitcast_fusion.8, s32[32768]{0:T(1024)S(1)} %fusion.87), kind=kCustom, calls=%fused_computation.3.clone.clone.1 | custom fusion | bytes 8650752 | tf_op jit(solution)/shard_map/while/body/eval_jaxpr/gather | solution.py:68
  2086.2 16.3 gather_fusion.2
  2109.0 114.9 %gather_fusion.3 = bf16[32768,65]{1,0:T(8,128)(2,1)} fusion(bf16[65,65]{0,1:T(8,128)(2,1)S(1)} %dynamic-slice_bitcast_fusion.8, s32[32768]{0:T(1024)S(1)} %fusion.87), kind=kCustom, calls=%fused_computation.3.clone.clone.1 | custom fusion | bytes 8650752 | tf_op jit(solution)/shard_map/while/body/eval_jaxpr/gather | solution.py:68
  2234.8 16.3 gather_fusion.2
  2257.5 114.9 %gather_fusion.3 = bf16[32768,65]{1,0:T(8,128)(2,1)} fusion(bf16[65,65]{0,1:T(8,128)(2,1)S(1)} %dynamic-slice_bitcast_fusion.8, s32[32768]{0:T(1024)S(1)} %fusion.87), kind=kCustom, calls=%fused_computation.3.clone.clone.1 | custom fusion | bytes 8650752 | tf_op jit(solution)/shard_map/while/body/eval_jaxpr/gather | solution.py:68
  2383.4 16.3 gather_fusion.2
  2406.7 42.4 %all-reduce.6.cloned.1.call-done = f32[64,256]{1,0:T(8,128)} async-done(((f32[64,256]{1,0:T(8,128)}), f32[64,256]{1,0:T(8,128)}) %all-reduce.6.cloned.1.call-update) | async-done | bytes 65552 | tf_op jit(solution)/shard_map/psum | solution.py:106
  2450.5 16.6 all-reduce.3
  (276 shorter events, 178.7 us)
Async XLA Ops:
  7.2 2441.9 %all-reduce.6.cloned.1.call-start = ((), (), s32[]{:S(2)}) async-start(), calls=%async_computation | async-start | bytes 131072 | tf_op jit(solution)/shard_map/psum | solution.py:106
  8.3 4.8 collective-permute-start
  10.7 5.4 collective-permute-start.1
  16.1 1197.6 %copy-start.1 = (bf16[8,64,256]{2,1,0:T(8,128)(2,1)S(1)}, bf16[8,64,256]{2,1,0:T(8,128)(2,1)}, u32[]{:S(2)}) copy-start(bf16[8,64,256]{2,1,0:T(8,128)(2,1)} %param.16) | copy-start | bytes 786436
  1209.5 4.3 collective-permute-start.2
  1211.5 6.0 collective-permute-start.3
  1217.5 1231.5 %copy-start.2 = (f32[64,256]{1,0:T(8,128)S(1)}, f32[64,256]{1,0:T(8,128)}, u32[]{:S(2)}) copy-start(f32[64,256]{1,0:T(8,128)} %param.14) | copy-start | bytes 196612
  1217.5 1231.5 %copy-start.4 = (f32[64,256]{1,0:T(8,128)S(1)}, f32[64,256]{1,0:T(8,128)}, u32[]{:S(2)}) copy-start(f32[64,256]{1,0:T(8,128)} %param.13) | copy-start | bytes 196612
  1217.5 1253.5 %copy-start.5 = (f32[64,256]{1,0:T(8,128)S(1)}, f32[64,256]{1,0:T(8,128)}, u32[]{:S(2)}) copy-start(f32[64,256]{1,0:T(8,128)} %param.12) | copy-start | bytes 196612
  1217.5 1257.9 %copy-start.6 = (f32[64,3,3]{0,2,1:T(4,128)S(1)}, f32[64,3,3]{0,2,1:T(4,128)}, u32[]{:S(2)}) copy-start(f32[64,3,3]{0,2,1:T(4,128)} %param.17) | copy-start | bytes 6916
  1217.6 1257.9 %copy-start.7 = (f32[64,3,3]{0,2,1:T(4,128)S(1)}, f32[64,3,3]{0,2,1:T(4,128)}, u32[]{:S(2)}) copy-start(f32[64,3,3]{0,2,1:T(4,128)} %param.19) | copy-start | bytes 6916
  2406.0 0.6 copy-start
  2406.0 73.4 %copy-start.8 = (f32[64]{0:T(128)S(1)}, f32[64]{0:T(128)}, u32[]{:S(2)}) copy-start(f32[64]{0:T(128)} %param.18) | copy-start | bytes 772
  2472.6 9.6 copy-start.3
  2472.6 2.9 collective-permute-start.4
  2473.9 3.1 collective-permute-start.5
Sparse Core Ops, SparseCore 0:
  2406.8 42.2 all-reduce.5
where the time goes:
time: 2490 us
  local copies, waits for them, and re-layouts  2300 us (92%)
  matrix products  69.7 us (3%)
  waiting for transfers between devices  50.5 us (2%)
  blocking collectives  33.6 us (1%)
    gather x32, local copies, waits for them, and re-layouts, correlate(): taps[:, jnp.clip(spacing, 0, span - 1)]  2010 us
    gather x24, local copies, waits for them, and re-layouts, correlate(): stacked = blocks[offsets]  282 us
    dot_general x16, matrix products, correlate(): jnp.einsum('arnu,auv->rnv', stacked, toeplitz, preferred_element_type=jnp...  66.4 us
  transfers between devices with their start and end apart: 7, of which 4 were waited for; matrix products, arithmetic and copies ran while one was open for 0% of the time, Pallas kernels for 0%

commit v1 on v0

--- a/solution.py
+++ b/solution.py
@@ -1,9 +1,14 @@
+import functools
+
 import jax
 import jax.numpy as jnp
 from jax import lax
+from jax.experimental import pallas as pl
+from jax.experimental.pallas import tpu as pltpu
 from jax.sharding import PartitionSpec as P
 
 damping = 0.5
+LANES = 128
 
 
 def with_halo(array, sides, width):
@@ -50,37 +55,114 @@
     return tile[2 : 2 + rows, 2 : 2 + columns] - mixed
 
 
-def correlate(source, taps):
-    span = taps.shape[0]
-    half = (span - 1) // 2
-    source_rows, width = source.shape
-    out_rows = source_rows - span + 1
-    count = width // 128
-    framed = jnp.pad(source, ((0, 0), (half, 128 - half)))
-    lower = framed[:, :width].reshape(source_rows, count, 128)
-    upper = framed[:, 128 : width + 128].reshape(source_rows, count, 128)
-    blocks = jnp.concatenate([lower, upper], axis=2)
-    offsets = jnp.arange(span)[:, None] + jnp.arange(out_rows)[None, :]
-    stacked = blocks[offsets]
-    spacing = jnp.arange(256)[:, None] - jnp.arange(128)[None, :]
-    valid = (spacing >= 0) & (spacing < span)
-    toeplitz = jnp.where(
-        valid[None], taps[:, jnp.clip(spacing, 0, span - 1)], jnp.zeros((), taps.dtype)
-    )
-    result = jnp.einsum("arnu,auv->rnv", stacked, toeplitz, preferred_element_type=jnp.float32)
-    return result.reshape(out_rows, width)
-
-
-def blur_all(sources, kernels, out_rows, width):
-
-    def add_one(total, pair):
-        source, taps = pair
-        return (total + correlate(source, taps), None)
-
-    result, unused = lax.scan(
-        add_one, jnp.zeros((out_rows, width), jnp.float32), (sources, kernels)
-    )
-    return result
+def tap_rows(kernels):
+    span = kernels.shape[2]
+    idx = (LANES - jnp.arange(LANES)) % LANES
+    taps = kernels.astype(jnp.float32)[:, :, jnp.clip(idx, 0, span - 1)]
+    return jnp.where((idx < span)[None, None], taps, 0.0)
+
+
+def _toeplitz(g, valid):
+    t = pltpu.roll(jnp.broadcast_to(g, valid.shape), 0, 1, stride=1, stride_axis=0)
+    return jnp.where(valid, t, 0.0).astype(jnp.bfloat16)
+
+
+def _band(span):
+    p = lax.broadcasted_iota(jnp.int32, (2 * LANES, LANES), 0)
+    v = lax.broadcasted_iota(jnp.int32, (2 * LANES, LANES), 1)
+    d = p - v
+    return (d >= 0) & (d < span)
+
+
+def _lhs(part, r, rows, blocks):
+    pieces = [part[r : r + rows, n * LANES : n * LANES + 2 * LANES] for n in range(blocks)]
+    return jnp.concatenate(pieces, axis=0).astype(jnp.bfloat16)
+
+
+def _sweep(g_ref, src_ref, valid, span, rows, blocks):
+    full = (span - 1) // 8
+
+    def group(q, acc):
+        base = pl.multiple_of(q * 8, 8)
+        part = src_ref[pl.ds(base, rows + 8), :]
+        taps = g_ref[0, pl.ds(base, 8), :]
+        for r in range(8):
+            t = _toeplitz(taps[r : r + 1], valid)
+            acc = acc + jnp.dot(_lhs(part, r, rows, blocks), t, preferred_element_type=jnp.float32)
+        return acc
+
+    acc = lax.fori_loop(0, full, group, jnp.zeros((rows * blocks, LANES), jnp.float32))
+    tail = span - 8 * full
+    part = src_ref[pl.ds(8 * full, rows + tail - 1), :]
+    taps = g_ref[0, pl.ds(8 * full, tail), :]
+    for r in range(tail):
+        t = _toeplitz(taps[r : r + 1], valid)
+        acc = acc + jnp.dot(_lhs(part, r, rows, blocks), t, preferred_element_type=jnp.float32)
+    return acc
+
+
+def _blur_body(g_ref, x_ref, o_ref, *, span, rows, blocks):
+    k = pl.program_id(0)
+
+    @pl.when(k == 0)
+    def _():
+        o_ref[...] = jnp.zeros_like(o_ref)
+
+    valid = _band(span)
+    acc = _sweep(g_ref, x_ref.at[0], valid, span, rows, blocks)
+    o_ref[...] += acc
+
+
+def blur(g, x, rows):
+    nk, span, _ = g.shape
+    src_rows, padded_width = x.shape[1], x.shape[2]
+    blocks = (padded_width - LANES) // LANES
+    out = pl.pallas_call(
+        functools.partial(_blur_body, span=span, rows=rows, blocks=blocks),
+        grid=(nk,),
+        in_specs=[
+            pl.BlockSpec((1, span, LANES), lambda k: (k, 0, 0)),
+            pl.BlockSpec((1, src_rows, padded_width), lambda k: (k, 0, 0)),
+        ],
+        out_specs=pl.BlockSpec((rows * blocks, LANES), lambda k: (0, 0)),
+        out_shape=jax.ShapeDtypeStruct((rows * blocks, LANES), jnp.float32),
+        compiler_params=pltpu.CompilerParams(dimension_semantics=("arbitrary",)),
+    )(g, x)
+    return jnp.concatenate([out[n * rows : (n + 1) * rows] for n in range(blocks)], axis=1)
+
+
+def _back_body(g_ref, e_ref, w_ref, o_ref, *, span, rows, blocks):
+    k = pl.program_id(0)
+
+    @pl.when(k == 0)
+    def _():
+        o_ref[...] = jnp.zeros_like(o_ref)
+
+    valid = _band(span)
+
+    acc = _sweep(g_ref, e_ref, valid, span, rows, blocks)
+    for n in range(blocks):
+        cols = slice(n * LANES, (n + 1) * LANES)
+        w = w_ref[0, :, cols].astype(jnp.float32)
+        o_ref[:, cols] += w * acc[n * rows : (n + 1) * rows]
+
+
+def back_weighted(g, e, w):
+    nk, span, _ = g.shape
+    rows, width = w.shape[1], w.shape[2]
+    blocks = width // LANES
+    return pl.pallas_call(
+        functools.partial(_back_body, span=span, rows=rows, blocks=blocks),
+        grid=(nk,),
+        in_specs=[
+            pl.BlockSpec((1, span, LANES), lambda k: (k, 0, 0)),
+            pl.BlockSpec(e.shape, lambda k: (0, 0)),
+            pl.BlockSpec((1, rows, width), lambda k: (k, 0, 0)),
+        ],
+        out_specs=pl.BlockSpec((rows, width), lambda k: (0, 0)),
+        out_shape=jax.ShapeDtypeStruct((rows, width), jnp.float32),
+        compiler_params=pltpu.CompilerParams(dimension_semantics=("arbitrary",)),
+    )(g, e, w)
 
 
 def per_device(
@@ -91,18 +173,12 @@
     maps_wide = weight_maps.astype(jnp.float32)
     shaped = (maps_wide * direction[None]).astype(jnp.bfloat16)
     padded = with_halo(shaped, (("band", 1),), half)
-    partial_value = blur_all(padded, kernels, rows, width)
+    framed = jnp.pad(padded.astype(jnp.float32), ((0, 0), (0, 0), (half, LANES - half)))
+    partial_value = blur(tap_rows(kernels), framed, rows)
     image = lax.psum(partial_value, "comp").astype(jnp.bfloat16)
     edged = with_halo(image, (("band", 0),), half)
-    flipped = kernels[:, ::-1, ::-1]
-
-    def add_back(total, pair):
-        taps, weights = pair
-        return (total + weights * correlate(edged, taps), None)
-
-    local_sum, unused = lax.scan(
-        add_back, jnp.zeros((rows, width), jnp.float32), (flipped, maps_wide)
-    )
+    edged = jnp.pad(edged.astype(jnp.float32), ((0, 0), (half, LANES - half)))
+    local_sum = back_weighted(tap_rows(kernels[:, ::-1, ::-1]), edged, weight_maps)
     normal = lax.psum(local_sum, "comp")
     curved = normal + damping * direction
     old, product, cross, square = lax.psum(

time: 2490 us -> 185 us (0.07)
  local copies, waits for them, and re-layouts: 2300 us -> 4.66 us
  matrix products: 69.7 us -> 3.39 us
  Pallas kernels: 0 us -> 56 us
    gather x56 -> x4, local copies, waits for them, and re-layouts: 2290 us -> 2.01 us  [tap_rows(): taps = kernels.astype(jnp.float32)[:, :, jnp.clip(idx, 0, span - 1)]]
    dot_general x16 -> x0, matrix products: 66.4 us -> none  [correlate(): jnp.einsum('arnu,auv->rnv', stacked, toeplitz, preferred_element_type=jnp...]
    pallas_call x0 -> x2, Pallas kernels: none -> 56 us  [the longest x1 28 us: blur(): pl.pallas_call(functools.partial(_blur_body, span=span, rows=rows, blocks...]
  transfers between devices with their start and end apart: 7 -> 7, of which waited for: 4 -> 3; matrix products, arithmetic and copies ran while one was open for 0% -> 2% of each run, Pallas kernels for 0% -> 0%
where the time goes in v1:
time: 185 us
  Pallas kernels  56 us (30%)
  waiting for transfers between devices  49.2 us (27%)
  blocking collectives  34.5 us (19%)
  between operations  18.3 us (10%)
  starting transfers between devices  10.6 us (6%)
  other arithmetic  8.16 us (4%)
  local copies, waits for them, and re-layouts  4.66 us (3%)
  matrix products  3.39 us (2%)
    psum x1, waiting for transfers between devices, per_device(): normal = lax.psum(local_sum, 'comp')  42.6 us
    pallas_call x1, Pallas kernels, blur(): pl.pallas_call(functools.partial(_blur_body, span=span, rows=rows, blocks...  28 us
    pallas_call x1, Pallas kernels, back_weighted(): pl.pallas_call(functools.partial(_back_body, span=span, rows=rows, blocks...  27.9 us
    psum x1, blocking collectives, per_device(): image = lax.psum(partial_value, 'comp').astype(jnp.bfloat16)  17.9 us
    psum x1, blocking collectives, per_device(): lax.psum((jnp.sum(residual * residual), jnp.sum(direction * curved), jnp....  16.6 us
    ppermute x3, starting transfers between devices, with_halo(): before = lax.ppermute(last, axis, up)  6.73 us
    ppermute x3, waiting for transfers between devices, with_halo(): after = lax.ppermute(first, axis, down)  5.86 us
    ppermute x3, starting transfers between devices, with_halo(): after = lax.ppermute(first, axis, down)  3.87 us
  transfers between devices with their start and end apart: 7, of which 3 were waited for; matrix products, arithmetic and copies ran while one was open for 2% of the time, Pallas kernels for 0%

profile of v1, /device:TPU:0, one launch (start us, length us, event | category | flops | bytes accessed | tf_op | source)
XLA Modules:
  0.0 184.7 jit_solution(13157418666935463090)
XLA Ops:
  7.2 0.0 all-reduce.6.cloned.1.call-start
  7.2 1.0 multiply_convert_fusion
  8.2 2.4 %collective-permute-start = (bf16[8,32,256]{2,1,0:T(8,128)(2,1)S(1)}, bf16[8,32,256]{2,1,0:T(8,128)(2,1)S(1)}, u32[]{:S(2)}, u32[]{:S(2)}) collective-permute-start(bf16[8,32,256]{2,1,0:T(8,128)(2,1)S(1)} %get-tuple-element.14), channel_id=1, source_target_pairs={{0,1},{1,2},{2,3},{3,4},{4,5},{5,6},{6,7},{8,9},{9,10},{10,11},{11... | collective-permute-start | bytes 393224 | tf_op jit(solution)/shard_map/ppermute | solution.py:21
  10.7 1.3 collective-permute-start.1
  12.0 1.1 copy.13
  13.1 0.1 rev.3
  13.3 0.8 gather_fusion
  14.1 0.2 copy.14
  14.3 0.8 gather_fusion.1
  15.1 0.2 copy.16
  15.3 0.9 select_bitcast_fusion
  16.2 0.0 collective-permute-done
  16.2 0.0 collective-permute-done.1
  16.2 1.5 fusion.14.x_ref
  17.7 0.0 copy-start.5
  17.7 28.0 %shard_map.111 = f32[128,128]{1,0:T(8,128)} custom-call(f32[8,65,128]{2,1,0:T(8,128)} %get-tuple-element.23.g_ref, f32[8,128,384]{2,1,0:T(8,128)} %fusion.14.x_ref), custom_call_target="tpu_custom_call" | custom-call | tf_op jit(solution)/shard_map/pallas_call | solution.py:120
  45.8 0.8 fusion.51
  46.5 17.9 %psum.43 = bf16[64,256]{1,0:T(8,128)(2,1)S(1)} all-reduce(f32[64,256]{1,0:T(8,128)S(1)} %pad_maximum_fusion), channel_id=1, replica_groups=mesh['comp'=4,'band'=8] {'comp'}, use_global_device_ids=true, to_apply=%region_2.3 | all-reduce | flops 16384 | bytes 98304 | tf_op jit(solution)/shard_map/psum | solution.py:178
  64.5 1.3 collective-permute-start.2
  65.8 1.3 collective-permute-start.3
  67.1 0.0 collective-permute-done.2
  67.1 5.8 %collective-permute-done.3 = bf16[32,256]{1,0:T(8,128)(2,1)S(1)} collective-permute-done((bf16[32,256]{1,0:T(8,128)(2,1)S(1)}, bf16[32,256]{1,0:T(8,128)(2,1)S(1)}, u32[]{:S(2)}, u32[]{:S(2)}) %collective-permute-start.3) | collective-permute-done | bytes 16416 | tf_op jit(solution)/shard_map/ppermute | solution.py:22
  72.9 0.8 fusion.23.e_ref
  73.7 27.9 %shard_map.112 = f32[64,256]{1,0:T(8,128)} custom-call(f32[8,65,128]{2,1,0:T(8,128)} %get-tuple-element.24.g_ref, f32[128,384]{1,0:T(8,128)} %fusion.23.e_ref, bf16[8,64,256]{2,1,0:T(8,128)(2,1)} %w_ref.1), custom_call_target="tpu_custom_call" | custom-call | tf_op jit(solution)/shard_map/pallas_call | solution.py:154
  101.6 0.0 all-reduce.6.cloned.1.call-update
  101.7 42.6 %all-reduce.6.cloned.1.call-done = f32[64,256]{1,0:T(8,128)} async-done(((f32[64,256]{1,0:T(8,128)}), f32[64,256]{1,0:T(8,128)}) %all-reduce.6.cloned.1.call-update) | async-done | bytes 65552 | tf_op jit(solution)/shard_map/psum | solution.py:182
  144.3 0.0 copy-done
  144.3 1.5 multiply_reduce_fusion
  145.8 16.6 %all-reduce.3 = (f32[]{:T(128)}, f32[]{:T(128)}, f32[]{:T(128)}, f32[]{:T(128)}) all-reduce(f32[]{:T(128)} %get-tuple-element.7, f32[]{:T(128)} %get-tuple-element.6, f32[]{:T(128)} %get-tuple-element.5, f32[]{:T(128)} %get-tuple-element.4), channel_id=1, replica_groups=mesh['comp'=4,'band'=8] {'band'}, use_global_device_ids=true, to_apply=%region_1.2 | all-reduce | flops 4 | bytes 32 | tf_op jit(solution)/shard_map/psum | solution.py:184
  166.3 0.0 copy-done.3
  166.3 1.5 multiply_add_fusion
  167.9 1.3 collective-permute-start.5
  169.2 3.0 %collective-permute-start.4 = (f32[2,256]{1,0:T(2,128)S(1)}, f32[2,256]{1,0:T(2,128)S(1)}, u32[]{:S(2)}, u32[]{:S(2)}) collective-permute-start(f32[2,256]{1,0:T(2,128)S(1)} %get-tuple-element.17), channel_id=1, source_target_pairs={{0,1},{1,2},{2,3},{3,4},{4,5},{5,6},{6,7},{8,9},{9,10},{10,11},{11... | collective-permute-start | bytes 6152 | tf_op jit(solution)/shard_map/ppermute | solution.py:21
  172.2 0.1 and_convert_fusion
  172.3 0.0 copy-done.5
  172.3 0.0 collective-permute-done.5
  172.3 0.7 collective-permute-done.4
  173.0 0.1 fusion.26
  173.1 0.1 fusion.36
  173.2 0.1 fusion.35
  173.3 0.1 fusion.33
  173.4 0.1 fusion.32
  173.5 0.1 fusion.30
  173.5 0.1 fusion.29
  173.6 1.9 %fusion.15 = f32[66,66,64]{1,2,0:T(8,128)S(1)} fusion(f32[64,9,1]{0,1,2:T(8,128)S(1)} %reshape.152, f32[9,66,66]{2,1,0:T(8,128)S(1)} %fusion.29), kind=kOutput, calls=%fused_computation.19 | convolution fusion | flops 30108672 | bytes 1274256 | tf_op jit(solution)/shard_map/ct,tij->cij/dot_general | solution.py:38
  175.5 1.5 fusion
  177.0 0.1 copy.22
  177.1 0.7 fusion.42
  (25 shorter events, 0.2 us)
Async XLA Ops:
  7.2 137.2 %all-reduce.6.cloned.1.call-start = ((), (), s32[]{:S(2)}) async-start(), calls=%async_computation | async-start | bytes 131072 | tf_op jit(solution)/shard_map/psum | solution.py:182
  8.2 7.9 %collective-permute-start = (bf16[8,32,256]{2,1,0:T(8,128)(2,1)S(1)}, bf16[8,32,256]{2,1,0:T(8,128)(2,1)S(1)}, u32[]{:S(2)}, u32[]{:S(2)}) collective-permute-start(bf16[8,32,256]{2,1,0:T(8,128)(2,1)S(1)} %get-tuple-element.14), channel_id=1, source_target_pairs={{0,1},{1,2},{2,3},{3,4},{4,5},{5,6},{6,7},{8,9},{9,10},{10,11},{11... | collective-permute-start | bytes 393224 | tf_op jit(solution)/shard_map/ppermute | solution.py:21
  10.7 5.5 %collective-permute-start.1 = (bf16[8,32,256]{2,1,0:T(8,128)(2,1)S(1)}, bf16[8,32,256]{2,1,0:T(8,128)(2,1)S(1)}, u32[]{:S(2)}, u32[]{:S(2)}) collective-permute-start(bf16[8,32,256]{2,1,0:T(8,128)(2,1)S(1)} %get-tuple-element.15), channel_id=1, source_target_pairs={{1,0},{2,1},{3,2},{4,3},{5,4},{6,5},{7,6},{9,8},{10,9},{11,10},{12... | collective-permute-start | bytes 393224 | tf_op jit(solution)/shard_map/ppermute | solution.py:22
  17.7 126.6 %copy-start = (f32[64,256]{1,0:T(8,128)S(1)}, f32[64,256]{1,0:T(8,128)}, u32[]{:S(2)}) copy-start(f32[64,256]{1,0:T(8,128)} %param.10) | copy-start | bytes 196612
  17.7 126.6 %copy-start.2 = (f32[64,256]{1,0:T(8,128)S(1)}, f32[64,256]{1,0:T(8,128)}, u32[]{:S(2)}) copy-start(f32[64,256]{1,0:T(8,128)} %param.9) | copy-start | bytes 196612
  17.7 148.6 %copy-start.3 = (f32[64,256]{1,0:T(8,128)S(1)}, f32[64,256]{1,0:T(8,128)}, u32[]{:S(2)}) copy-start(f32[64,256]{1,0:T(8,128)} %param.8) | copy-start | bytes 196612
  17.7 154.6 %copy-start.4 = (f32[64,3,3]{0,2,1:T(4,128)S(1)}, f32[64,3,3]{0,2,1:T(4,128)}, u32[]{:S(2)}) copy-start(f32[64,3,3]{0,2,1:T(4,128)} %param.13) | copy-start | bytes 6916
  17.7 154.6 %copy-start.5 = (f32[64,3,3]{0,2,1:T(4,128)S(1)}, f32[64,3,3]{0,2,1:T(4,128)}, u32[]{:S(2)}) copy-start(f32[64,3,3]{0,2,1:T(4,128)} %param.15) | copy-start | bytes 6916
  64.5 2.6 %collective-permute-start.2 = (bf16[32,256]{1,0:T(8,128)(2,1)S(1)}, bf16[32,256]{1,0:T(8,128)(2,1)S(1)}, u32[]{:S(2)}, u32[]{:S(2)}) collective-permute-start(bf16[32,256]{1,0:T(8,128)(2,1)S(1)} %get-tuple-element.21), channel_id=1, source_target_pairs={{0,1},{1,2},{2,3},{3,4},{4,5},{5,6},{6,7},{8,9},{9,10},{10,11},{11... | collective-permute-start | bytes 49160 | tf_op jit(solution)/shard_map/ppermute | solution.py:21
  65.8 7.2 %collective-permute-start.3 = (bf16[32,256]{1,0:T(8,128)(2,1)S(1)}, bf16[32,256]{1,0:T(8,128)(2,1)S(1)}, u32[]{:S(2)}, u32[]{:S(2)}) collective-permute-start(bf16[32,256]{1,0:T(8,128)(2,1)S(1)} %get-tuple-element.22), channel_id=1, source_target_pairs={{1,0},{2,1},{3,2},{4,3},{5,4},{6,5},{7,6},{9,8},{10,9},{11,10},{12... | collective-permute-start | bytes 49160 | tf_op jit(solution)/shard_map/ppermute | solution.py:22
  101.6 73.9 %copy-start.6 = (f32[64]{0:T(128)S(1)}, f32[64]{0:T(128)}, u32[]{:S(2)}) copy-start(f32[64]{0:T(128)} %param.14) | copy-start | bytes 772
  167.9 9.2 %copy-start.1 = (f32[64,256]{1,0:T(8,128)}, f32[64,256]{1,0:T(8,128)S(1)}, u32[]{:S(2)}) copy-start(f32[64,256]{1,0:T(8,128)S(1)} %get-tuple-element.18) | copy-start | bytes 196612
  167.9 4.5 %collective-permute-start.5 = (f32[2,256]{1,0:T(2,128)S(1)}, f32[2,256]{1,0:T(2,128)S(1)}, u32[]{:S(2)}, u32[]{:S(2)}) collective-permute-start(f32[2,256]{1,0:T(2,128)S(1)} %get-tuple-element.16), channel_id=1, source_target_pairs={{1,0},{2,1},{3,2},{4,3},{5,4},{6,5},{7,6},{9,8},{10,9},{11,10},{12... | collective-permute-start | bytes 6152 | tf_op jit(solution)/shard_map/ppermute | solution.py:22
  169.2 3.8 %collective-permute-start.4 = (f32[2,256]{1,0:T(2,128)S(1)}, f32[2,256]{1,0:T(2,128)S(1)}, u32[]{:S(2)}, u32[]{:S(2)}) collective-permute-start(f32[2,256]{1,0:T(2,128)S(1)} %get-tuple-element.17), channel_id=1, source_target_pairs={{0,1},{1,2},{2,3},{3,4},{4,5},{5,6},{6,7},{8,9},{9,10},{10,11},{11... | collective-permute-start | bytes 6152 | tf_op jit(solution)/shard_map/ppermute | solution.py:21
Sparse Core Ops, SparseCore 0:
  101.8 42.4 all-reduce.5

commit v2 on v1

--- a/solution.py
+++ b/solution.py
@@ -24,9 +24,17 @@
     return array
 
 
-def denoise(estimate_next, filters_in, biases, filters_out):
-    rows, width = estimate_next.shape
-    framed = with_halo(estimate_next, (("band", 0),), 2)
+def pair_sum(value, axis):
+    count = lax.axis_size(axis)
+    step = 1
+    while step < count:
+        value = value + lax.ppermute(value, axis, [(i, i ^ step) for i in range(count)])
+        step *= 2
+    return value
+
+
+def denoise(framed, filters_in, biases, filters_out):
+    rows, width = framed.shape[0] - 4, framed.shape[1]
     columns = width // lax.axis_size("comp")
     start = lax.axis_index("comp") * columns
     padded = jnp.pad(framed, ((0, 0), (2, 2)))
@@ -170,6 +178,8 @@
 ):
     rows, width = direction.shape
     half = (kernels.shape[1] - 1) // 2
+    framed_both = with_halo(jnp.stack([estimate, direction]), (("band", 1),), 2)
+    framed_estimate, framed_direction = framed_both[0], framed_both[1]
     maps_wide = weight_maps.astype(jnp.float32)
     shaped = (maps_wide * direction[None]).astype(jnp.bfloat16)
     padded = with_halo(shaped, (("band", 1),), half)
@@ -179,7 +189,7 @@
     edged = with_halo(image, (("band", 0),), half)
     edged = jnp.pad(edged.astype(jnp.float32), ((0, 0), (half, LANES - half)))
     local_sum = back_weighted(tap_rows(kernels[:, ::-1, ::-1]), edged, weight_maps)
-    normal = lax.psum(local_sum, "comp")
+    normal = pair_sum(local_sum, "comp")
     curved = normal + damping * direction
     old, product, cross, square = lax.psum(
         (
@@ -195,7 +205,9 @@
     new = old - 2.0 * alpha * cross + alpha * alpha * square
     estimate_next = estimate + alpha * direction
     direction_next = residual_next + new / old * direction
-    denoised = denoise(estimate_next, filters_in, biases, filters_out)
+    framed_next = framed_estimate + alpha * framed_direction
+    framed_next = lax.dynamic_update_slice_in_dim(framed_next, estimate_next, 2, 0)
+    denoised = denoise(framed_next, filters_in, biases, filters_out)
     return (estimate_next, residual_next, direction_next, denoised)
 
 

time: 185 us -> 138 us (0.75)
  waiting for transfers between devices: 49.2 us -> 14.1 us
  between operations: 18.3 us -> 4.89 us
  blocking collectives: 34.5 us -> 31.5 us
  starting transfers between devices: 10.6 us -> 13.5 us
    psum x1 -> x0, waiting for transfers between devices: 42.6 us -> none  [per_device(): normal = lax.psum(local_sum, 'comp')]
    ppermute x0 -> x2, waiting for transfers between devices: none -> 8.27 us  [pair_sum(): lax.ppermute(value, axis, [(i, i ^ step) for i in range(count)])]
    ppermute x3, starting transfers between devices: 6.73 us -> 8.89 us  [with_halo(): before = lax.ppermute(last, axis, up)]
    psum x1, blocking collectives: 16.6 us -> 14.4 us  [per_device(): lax.psum((jnp.sum(residual * residual), jnp.sum(direction * curved), jnp....]
  transfers between devices with their start and end apart: 7 -> 8, of which waited for: 3 -> 3; matrix products, arithmetic and copies ran while one was open for 2% -> 7% of each run, Pallas kernels for 0% -> 41%
where the time goes in v2:
time: 138 us; the launch traced here: 137 us
  Pallas kernels  55.9 us (41%)
  blocking collectives  31.5 us (23%)
  waiting for transfers between devices  14.1 us (10%)
  starting transfers between devices  13.5 us (10%)
  other arithmetic  8.44 us (6%)
  local copies, waits for them, and re-layouts  5.23 us (4%)
  between operations  4.89 us (4%)
  matrix products  3.38 us (2%)
    pallas_call x1, Pallas kernels, blur(): pl.pallas_call(functools.partial(_blur_body, span=span, rows=rows, blocks...  28 us
    pallas_call x1, Pallas kernels, back_weighted(): pl.pallas_call(functools.partial(_back_body, span=span, rows=rows, blocks...  27.9 us
    psum x1, blocking collectives, per_device(): image = lax.psum(partial_value, 'comp').astype(jnp.bfloat16)  17.1 us
    psum x1, blocking collectives, per_device(): lax.psum((jnp.sum(residual * residual), jnp.sum(direction * curved), jnp....  14.4 us
    ppermute x3, starting transfers between devices, with_halo(): before = lax.ppermute(last, axis, up)  8.89 us
    ppermute x2, waiting for transfers between devices, pair_sum(): lax.ppermute(value, axis, [(i, i ^ step) for i in range(count)])  8.27 us
    ppermute x3, waiting for transfers between devices, with_halo(): after = lax.ppermute(first, axis, down)  5.85 us
    ppermute x3, starting transfers between devices, with_halo(): after = lax.ppermute(first, axis, down)  3.88 us
  transfers between devices with their start and end apart: 8, of which 3 were waited for; matrix products, arithmetic and copies ran while one was open for 7% of the time, Pallas kernels for 41%

profile of v2, /device:TPU:0, one launch (start us, length us, event | category | flops | bytes accessed | tf_op | source)
XLA Modules:
  0.0 137.0 jit_solution(13299945566594971465)
XLA Ops:
  0.6 0.8 pad_maximum_fusion.3
  1.4 2.4 %collective-permute-start.6 = (f32[2,2,256]{2,1,0:T(2,128)S(1)}, f32[2,2,256]{2,1,0:T(2,128)S(1)}, u32[]{:S(2)}, u32[]{:S(2)}) collective-permute-start(f32[2,2,256]{2,1,0:T(2,128)S(1)} %get-tuple-element.17), channel_id=1, source_target_pairs={{0,1},{1,2},{2,3},{3,4},{4,5},{5,6},{6,7},{8,9},{9,10},{10,11},{11... | collective-permute-start | bytes 12296 | tf_op jit(solution)/shard_map/ppermute | solution.py:21
  3.8 1.3 collective-permute-start.7
  5.1 1.0 multiply_convert_fusion
  6.1 5.2 %collective-permute-start = (bf16[8,32,256]{2,1,0:T(8,128)(2,1)S(1)}, bf16[8,32,256]{2,1,0:T(8,128)(2,1)S(1)}, u32[]{:S(2)}, u32[]{:S(2)}) collective-permute-start(bf16[8,32,256]{2,1,0:T(8,128)(2,1)S(1)} %get-tuple-element.15), channel_id=1, source_target_pairs={{0,1},{1,2},{2,3},{3,4},{4,5},{5,6},{6,7},{8,9},{9,10},{10,11},{11... | collective-permute-start | bytes 393224 | tf_op jit(solution)/shard_map/ppermute | solution.py:21
  11.3 1.3 collective-permute-start.1
  12.7 1.1 copy.12
  13.8 0.1 rev.3
  14.0 0.8 gather_fusion
  14.8 0.2 copy.13
  15.0 0.8 gather_fusion.1
  15.8 0.2 copy.15
  16.0 0.9 select_bitcast_fusion
  16.9 1.5 %fusion.17.x_ref = f32[8,128,384]{2,1,0:T(8,128)} fusion(bf16[8,32,256]{2,1,0:T(8,128)(2,1)S(1)} %collective-permute-done.1, bf16[8,64,256]{2,1,0:T(8,128)(2,1)S(1)} %multiply_convert_fusion, bf16[8,32,256]{2,1,0:T(8,128)(2,1)S(1)} %collective-permute-done), kind=kLoop, calls=%fused_computation.19 | loop fusion | flops 4718592 | bytes 2097152 | tf_op jit(solution)/shard_map/jit(_pad)/pad | solution.py:186
  18.4 0.0 copy-start.2
  18.4 28.0 %shard_map.111 = f32[128,128]{1,0:T(8,128)} custom-call(f32[8,65,128]{2,1,0:T(8,128)} %get-tuple-element.24.g_ref, f32[8,128,384]{2,1,0:T(8,128)} %fusion.17.x_ref), custom_call_target="tpu_custom_call" | custom-call | tf_op jit(solution)/shard_map/pallas_call | solution.py:128
  46.4 0.8 fusion.55
  47.2 17.1 %psum.36 = bf16[64,256]{1,0:T(8,128)(2,1)S(1)} all-reduce(f32[64,256]{1,0:T(8,128)S(1)} %pad_maximum_fusion.1), channel_id=1, replica_groups=mesh['comp'=4,'band'=8] {'comp'}, use_global_device_ids=true, to_apply=%region_2.3 | all-reduce | flops 16384 | bytes 98304 | tf_op jit(solution)/shard_map/psum | solution.py:188
  64.3 1.3 collective-permute-start.2
  65.6 1.3 collective-permute-start.3
  66.9 5.8 %collective-permute-done.3 = bf16[32,256]{1,0:T(8,128)(2,1)S(1)} collective-permute-done((bf16[32,256]{1,0:T(8,128)(2,1)S(1)}, bf16[32,256]{1,0:T(8,128)(2,1)S(1)}, u32[]{:S(2)}, u32[]{:S(2)}) %collective-permute-start.3) | collective-permute-done | bytes 16416 | tf_op jit(solution)/shard_map/ppermute | solution.py:22
  72.8 0.8 fusion.26.e_ref
  73.6 27.9 %shard_map.112 = f32[64,256]{1,0:T(8,128)} custom-call(f32[8,65,128]{2,1,0:T(8,128)} %get-tuple-element.25.g_ref, f32[128,384]{1,0:T(8,128)} %fusion.26.e_ref, bf16[8,64,256]{2,1,0:T(8,128)(2,1)} %w_ref.1), custom_call_target="tpu_custom_call" | custom-call | tf_op jit(solution)/shard_map/pallas_call | solution.py:162
  101.5 0.0 collective-permute-start.4
  101.5 0.1 and_convert_fusion
  101.6 4.4 %collective-permute-done.4 = f32[64,256]{1,0:T(8,128)S(1)} collective-permute-done((f32[64,256]{1,0:T(8,128)}, f32[64,256]{1,0:T(8,128)S(1)}, u32[]{:S(2)}, u32[]{:S(2)}) %collective-permute-start.4) | collective-permute-done | bytes 65568 | tf_op jit(solution)/shard_map/ppermute | solution.py:31
  106.0 0.8 add.145
  106.8 0.7 collective-permute-start.5
  107.5 0.0 collective-permute-done.6
  107.6 3.9 %collective-permute-done.5 = f32[64,256]{1,0:T(8,128)S(1)} collective-permute-done((f32[64,256]{1,0:T(8,128)S(1)}, f32[64,256]{1,0:T(8,128)S(1)}, u32[]{:S(2)}, u32[]{:S(2)}) %collective-permute-start.5) | collective-permute-done | bytes 65568 | tf_op jit(solution)/shard_map/ppermute | solution.py:31
  111.5 0.6 multiply_reduce_fusion
  112.1 14.4 %all-reduce.3 = (f32[]{:T(128)}, f32[]{:T(128)}, f32[]{:T(128)}, f32[]{:T(128)}) all-reduce(f32[]{:T(128)} %get-tuple-element.6, f32[]{:T(128)} %get-tuple-element.7, f32[]{:T(128)} %get-tuple-element.5, f32[]{:T(128)} %get-tuple-element.4), channel_id=1, replica_groups=mesh['comp'=4,'band'=8] {'band'}, use_global_device_ids=true, to_apply=%region_1.2 | all-reduce | flops 4 | bytes 32 | tf_op jit(solution)/shard_map/psum | solution.py:194
  130.5 0.0 copy-start.6
  130.5 0.7 multiply_add_fusion
  131.2 0.3 dynamic_update_slice.3
  131.6 0.1 fusion.32
  131.6 0.1 fusion.34
  131.7 0.1 fusion.36
  131.8 0.1 fusion.38
  131.9 0.1 fusion.40
  132.0 0.1 fusion.42
  132.1 0.1 fusion.44
  132.2 0.1 fusion.46
  132.3 0.1 fusion.30
  132.4 1.9 %fusion.18 = f32[66,66,64]{1,2,0:T(8,128)S(1)} fusion(f32[64,9,1]{0,1,2:T(8,128)S(1)} %reshape.155, f32[9,66,66]{2,1,0:T(8,128)S(1)} %fusion.30), kind=kOutput, calls=%fused_computation.20 | convolution fusion | flops 30108672 | bytes 1274256 | tf_op jit(solution)/shard_map/ct,tij->cij/dot_general | solution.py:46
  134.3 1.5 %fusion.6 = f32[9,66,66]{2,0,1:T(8,128)S(1)} fusion(f32[64,9,1]{0,1,2:T(8,128)S(1)} %reshape.156, f32[66,66,64]{1,2,0:T(8,128)S(1)} %fusion.18, f32[66,66]{1,0:T(8,128)S(1)} %and_convert_fusion, f32[64]{0:T(128)S(1)} %copy-done.6), kind=kOutput, calls=%fused_computation.10 | convolution fusion | flops 30945024 | bytes 1291936 | tf_op jit(solution)/shard_map/ct,cij->tij/dot_general | solution.py:57
  135.8 0.5 slice_add_fusion
  136.3 0.7 fusion.47
  (29 shorter events, 0.2 us)
Async XLA Ops:
  1.4 106.1 %collective-permute-start.6 = (f32[2,2,256]{2,1,0:T(2,128)S(1)}, f32[2,2,256]{2,1,0:T(2,128)S(1)}, u32[]{:S(2)}, u32[]{:S(2)}) collective-permute-start(f32[2,2,256]{2,1,0:T(2,128)S(1)} %get-tuple-element.17), channel_id=1, source_target_pairs={{0,1},{1,2},{2,3},{3,4},{4,5},{5,6},{6,7},{8,9},{9,10},{10,11},{11... | collective-permute-start | bytes 12296 | tf_op jit(solution)/shard_map/ppermute | solution.py:21
  3.8 103.8 %collective-permute-start.7 = (f32[2,2,256]{2,1,0:T(2,128)S(1)}, f32[2,2,256]{2,1,0:T(2,128)S(1)}, u32[]{:S(2)}, u32[]{:S(2)}) collective-permute-start(f32[2,2,256]{2,1,0:T(2,128)S(1)} %get-tuple-element.18), channel_id=1, source_target_pairs={{1,0},{2,1},{3,2},{4,3},{5,4},{6,5},{7,6},{9,8},{10,9},{11,10},{12... | collective-permute-start | bytes 12296 | tf_op jit(solution)/shard_map/ppermute | solution.py:22
  6.1 10.8 %collective-permute-start = (bf16[8,32,256]{2,1,0:T(8,128)(2,1)S(1)}, bf16[8,32,256]{2,1,0:T(8,128)(2,1)S(1)}, u32[]{:S(2)}, u32[]{:S(2)}) collective-permute-start(bf16[8,32,256]{2,1,0:T(8,128)(2,1)S(1)} %get-tuple-element.15), channel_id=1, source_target_pairs={{0,1},{1,2},{2,3},{3,4},{4,5},{5,6},{6,7},{8,9},{9,10},{10,11},{11... | collective-permute-start | bytes 393224 | tf_op jit(solution)/shard_map/ppermute | solution.py:21
  11.3 5.5 %collective-permute-start.1 = (bf16[8,32,256]{2,1,0:T(8,128)(2,1)S(1)}, bf16[8,32,256]{2,1,0:T(8,128)(2,1)S(1)}, u32[]{:S(2)}, u32[]{:S(2)}) collective-permute-start(bf16[8,32,256]{2,1,0:T(8,128)(2,1)S(1)} %get-tuple-element.16), channel_id=1, source_target_pairs={{1,0},{2,1},{3,2},{4,3},{5,4},{6,5},{7,6},{9,8},{10,9},{11,10},{12... | collective-permute-start | bytes 393224 | tf_op jit(solution)/shard_map/ppermute | solution.py:22
  18.4 83.2 %copy-start.4 = (f32[64,3,3]{0,2,1:T(4,128)S(1)}, f32[64,3,3]{0,2,1:T(4,128)}, u32[]{:S(2)}) copy-start(f32[64,3,3]{0,2,1:T(4,128)} %param.13) | copy-start | bytes 6916
  18.4 83.2 %copy-start.5 = (f32[64,3,3]{0,2,1:T(4,128)S(1)}, f32[64,3,3]{0,2,1:T(4,128)}, u32[]{:S(2)}) copy-start(f32[64,3,3]{0,2,1:T(4,128)} %param.15) | copy-start | bytes 6916
  18.4 89.1 %copy-start = (f32[64,256]{1,0:T(8,128)S(1)}, f32[64,256]{1,0:T(8,128)}, u32[]{:S(2)}) copy-start(f32[64,256]{1,0:T(8,128)} %param.10) | copy-start | bytes 196612
  18.4 89.1 %copy-start.1 = (f32[64,256]{1,0:T(8,128)S(1)}, f32[64,256]{1,0:T(8,128)}, u32[]{:S(2)}) copy-start(f32[64,256]{1,0:T(8,128)} %param.8) | copy-start | bytes 196612
  18.4 93.1 %copy-start.2 = (f32[64,256]{1,0:T(8,128)S(1)}, f32[64,256]{1,0:T(8,128)}, u32[]{:S(2)}) copy-start(f32[64,256]{1,0:T(8,128)} %param.9) | copy-start | bytes 196612
  64.3 2.6 %collective-permute-start.2 = (bf16[32,256]{1,0:T(8,128)(2,1)S(1)}, bf16[32,256]{1,0:T(8,128)(2,1)S(1)}, u32[]{:S(2)}, u32[]{:S(2)}) collective-permute-start(bf16[32,256]{1,0:T(8,128)(2,1)S(1)} %get-tuple-element.22), channel_id=1, source_target_pairs={{0,1},{1,2},{2,3},{3,4},{4,5},{5,6},{6,7},{8,9},{9,10},{10,11},{11... | collective-permute-start | bytes 49160 | tf_op jit(solution)/shard_map/ppermute | solution.py:21
  65.6 7.2 %collective-permute-start.3 = (bf16[32,256]{1,0:T(8,128)(2,1)S(1)}, bf16[32,256]{1,0:T(8,128)(2,1)S(1)}, u32[]{:S(2)}, u32[]{:S(2)}) collective-permute-start(bf16[32,256]{1,0:T(8,128)(2,1)S(1)} %get-tuple-element.23), channel_id=1, source_target_pairs={{1,0},{2,1},{3,2},{4,3},{5,4},{6,5},{7,6},{9,8},{10,9},{11,10},{12... | collective-permute-start | bytes 49160 | tf_op jit(solution)/shard_map/ppermute | solution.py:22
  101.5 4.5 %collective-permute-start.4 = (f32[64,256]{1,0:T(8,128)}, f32[64,256]{1,0:T(8,128)S(1)}, u32[]{:S(2)}, u32[]{:S(2)}) collective-permute-start(f32[64,256]{1,0:T(8,128)} %shard_map.112), channel_id=1, source_target_pairs={{0,8},{8,0},{16,24},{24,16},{1,9},{9,1},{17,25},{25,17},{2,10},{10... | collective-permute-start | bytes 196616 | tf_op jit(solution)/shard_map/ppermute | solution.py:31
  106.8 4.7 %collective-permute-start.5 = (f32[64,256]{1,0:T(8,128)S(1)}, f32[64,256]{1,0:T(8,128)S(1)}, u32[]{:S(2)}, u32[]{:S(2)}) collective-permute-start(f32[64,256]{1,0:T(8,128)S(1)} %add.145), channel_id=1, source_target_pairs={{0,16},{8,24},{16,0},{24,8},{1,17},{9,25},{17,1},{25,9},{2,18},{10... | collective-permute-start | bytes 196616 | tf_op jit(solution)/shard_map/ppermute | solution.py:31
  130.5 3.7 %copy-start.6 = (f32[64]{0:T(128)S(1)}, f32[64]{0:T(128)}, u32[]{:S(2)}) copy-start(f32[64]{0:T(128)} %param.14) | copy-start | bytes 772
  131.2 4.6 %copy-start.3 = (f32[64,256]{1,0:T(8,128)}, f32[64,256]{1,0:T(8,128)S(1)}, u32[]{:S(2)}) copy-start(f32[64,256]{1,0:T(8,128)S(1)} %get-tuple-element.19) | copy-start | bytes 196612

commit v3 on v2

--- a/solution.py
+++ b/solution.py
@@ -9,6 +9,7 @@
 
 damping = 0.5
 LANES = 128
+GROUP = 16
 
 
 def with_halo(array, sides, width):
@@ -82,42 +83,48 @@
     return (d >= 0) & (d < span)
 
 
-def _lhs(part, r, rows, blocks):
-    pieces = [part[r : r + rows, n * LANES : n * LANES + 2 * LANES] for n in range(blocks)]
-    return jnp.concatenate(pieces, axis=0).astype(jnp.bfloat16)
-
-
-def _sweep(g_ref, src_ref, valid, span, rows, blocks):
-    full = (span - 1) // 8
+def _lhs(shifted_ref, r, base, rows, blocks):
+    part = shifted_ref[r, pl.ds(base, rows), :]
+    pieces = [part[:, n * LANES : n * LANES + 2 * LANES] for n in range(blocks)]
+    return jnp.concatenate(pieces, axis=0)
+
+
+def _shift_rows(src_ref, shifted_ref):
+    src_rows = src_ref.shape[0]
+    for r in range(GROUP):
+        shifted_ref[r, 0 : src_rows - r, :] = src_ref[r:src_rows, :].astype(jnp.bfloat16)
+
+
+def _sweep(g_ref, shifted_ref, valid, span, rows, blocks):
+    full = (span - 1) // GROUP
 
     def group(q, acc):
-        base = pl.multiple_of(q * 8, 8)
-        part = src_ref[pl.ds(base, rows + 8), :]
-        taps = g_ref[0, pl.ds(base, 8), :]
-        for r in range(8):
+        base = pl.multiple_of(q * GROUP, GROUP)
+        taps = g_ref[0, pl.ds(base, GROUP), :]
+        for r in range(GROUP):
             t = _toeplitz(taps[r : r + 1], valid)
-            acc = acc + jnp.dot(_lhs(part, r, rows, blocks), t, preferred_element_type=jnp.float32)
+            lhs = _lhs(shifted_ref, r, base, rows, blocks)
+            acc = acc + jnp.dot(lhs, t, preferred_element_type=jnp.float32)
         return acc
 
     acc = lax.fori_loop(0, full, group, jnp.zeros((rows * blocks, LANES), jnp.float32))
-    tail = span - 8 * full
-    part = src_ref[pl.ds(8 * full, rows + tail - 1), :]
-    taps = g_ref[0, pl.ds(8 * full, tail), :]
-    for r in range(tail):
+    base = GROUP * full
+    taps = g_ref[0, pl.ds(base, span - base), :]
+    for r in range(span - base):
         t = _toeplitz(taps[r : r + 1], valid)
-        acc = acc + jnp.dot(_lhs(part, r, rows, blocks), t, preferred_element_type=jnp.float32)
+        acc = acc + jnp.dot(_lhs(shifted_ref, r, base, rows, blocks), t, preferred_element_type=jnp.float32)
     return acc
 
 
-def _blur_body(g_ref, x_ref, o_ref, *, span, rows, blocks):
+def _blur_body(g_ref, x_ref, o_ref, shifted_ref, *, span, rows, blocks):
     k = pl.program_id(0)
 
     @pl.when(k == 0)
     def _():
         o_ref[...] = jnp.zeros_like(o_ref)
 
-    valid = _band(span)
-    acc = _sweep(g_ref, x_ref.at[0], valid, span, rows, blocks)
+    _shift_rows(x_ref.at[0], shifted_ref)
+    acc = _sweep(g_ref, shifted_ref, _band(span), span, rows, blocks)
     o_ref[...] += acc
 
 
@@ -134,21 +141,21 @@
         ],
         out_specs=pl.BlockSpec((rows * blocks, LANES), lambda k: (0, 0)),
         out_shape=jax.ShapeDtypeStruct((rows * blocks, LANES), jnp.float32),
+        scratch_shapes=[pltpu.VMEM((GROUP, src_rows, padded_width), jnp.bfloat16)],
         compiler_params=pltpu.CompilerParams(dimension_semantics=("arbitrary",)),
     )(g, x)
     return jnp.concatenate([out[n * rows : (n + 1) * rows] for n in range(blocks)], axis=1)
 
 
-def _back_body(g_ref, e_ref, w_ref, o_ref, *, span, rows, blocks):
+def _back_body(g_ref, e_ref, w_ref, o_ref, shifted_ref, *, span, rows, blocks):
     k = pl.program_id(0)
 
     @pl.when(k == 0)
     def _():
         o_ref[...] = jnp.zeros_like(o_ref)
-
-    valid = _band(span)
-
-    acc = _sweep(g_ref, e_ref, valid, span, rows, blocks)
+        _shift_rows(e_ref, shifted_ref)
+
+    acc = _sweep(g_ref, shifted_ref, _band(span), span, rows, blocks)
     for n in range(blocks):
         cols = slice(n * LANES, (n + 1) * LANES)
         w = w_ref[0, :, cols].astype(jnp.float32)
@@ -169,6 +176,7 @@
         ],
         out_specs=pl.BlockSpec((rows, width), lambda k: (0, 0)),
         out_shape=jax.ShapeDtypeStruct((rows, width), jnp.float32),
+        scratch_shapes=[pltpu.VMEM((GROUP,) + e.shape, jnp.bfloat16)],
         compiler_params=pltpu.CompilerParams(dimension_semantics=("arbitrary",)),
     )(g, e, w)
 
@@ -185,7 +193,7 @@
     padded = with_halo(shaped, (("band", 1),), half)
     framed = jnp.pad(padded.astype(jnp.float32), ((0, 0), (0, 0), (half, LANES - half)))
     partial_value = blur(tap_rows(kernels), framed, rows)
-    image = lax.psum(partial_value, "comp").astype(jnp.bfloat16)
+    image = pair_sum(partial_value, "comp").astype(jnp.bfloat16)
     edged = with_halo(image, (("band", 0),), half)
     edged = jnp.pad(edged.astype(jnp.float32), ((0, 0), (half, LANES - half)))
     local_sum = back_weighted(tap_rows(kernels[:, ::-1, ::-1]), edged, weight_maps)

time: 138 us -> 113 us (0.82)
  blocking collectives: 31.5 us -> 14.4 us
  Pallas kernels: 55.9 us -> 43.6 us
  starting transfers between devices: 13.5 us -> 21.5 us
  waiting for transfers between devices: 14.1 us -> 12.2 us
    psum x1 -> x0, blocking collectives: 17.1 us -> none  [per_device(): image = lax.psum(partial_value, 'comp').astype(jnp.bfloat16)]
    pallas_call x1, Pallas kernels: 27.9 us -> 20.4 us  [back_weighted(): pl.pallas_call(functools.partial(_back_body, span=span, rows=rows, blocks...]
    ppermute x2 -> x4, starting transfers between devices: 0.71 us -> 6.55 us  [pair_sum(): lax.ppermute(value, axis, [(i, i ^ step) for i in range(count)])]
    pallas_call x1, Pallas kernels: 28 us -> 23.2 us  [blur(): pl.pallas_call(functools.partial(_blur_body, span=span, rows=rows, blocks...]
    ppermute x3, waiting for transfers between devices: 5.85 us -> 2.99 us  [with_halo(): after = lax.ppermute(first, axis, down)]
    ppermute x3, starting transfers between devices: 8.89 us -> 11.1 us  [with_halo(): before = lax.ppermute(last, axis, up)]
    ppermute x2 -> x4, waiting for transfers between devices: 8.27 us -> 9.19 us  [pair_sum(): lax.ppermute(value, axis, [(i, i ^ step) for i in range(count)])]
  transfers between devices with their start and end apart: 8 -> 10, of which waited for: 3 -> 4; matrix products, arithmetic and copies ran while one was open for 7% -> 5% of each run, Pallas kernels for 41% -> 18%
where the time goes in v3:
time: 113 us
  Pallas kernels  43.6 us (39%)
  starting transfers between devices  21.5 us (19%)
  blocking collectives  14.4 us (13%)
  waiting for transfers between devices  12.2 us (11%)
  other arithmetic  7.72 us (7%)
  local copies, waits for them, and re-layouts  5.23 us (5%)
  between operations  4.88 us (4%)
  matrix products  3.38 us (3%)
    pallas_call x1, Pallas kernels, blur(): pl.pallas_call(functools.partial(_blur_body, span=span, rows=rows, blocks...  23.2 us
    pallas_call x1, Pallas kernels, back_weighted(): pl.pallas_call(functools.partial(_back_body, span=span, rows=rows, blocks...  20.4 us
    psum x1, blocking collectives, per_device(): lax.psum((jnp.sum(residual * residual), jnp.sum(direction * curved), jnp....  14.4 us
    ppermute x3, starting transfers between devices, with_halo(): before = lax.ppermute(last, axis, up)  11.1 us
    ppermute x4, waiting for transfers between devices, pair_sum(): lax.ppermute(value, axis, [(i, i ^ step) for i in range(count)])  9.19 us
    ppermute x4, starting transfers between devices, pair_sum(): lax.ppermute(value, axis, [(i, i ^ step) for i in range(count)])  6.55 us
    ppermute x3, starting transfers between devices, with_halo(): after = lax.ppermute(first, axis, down)  3.88 us
    ppermute x3, waiting for transfers between devices, with_halo(): after = lax.ppermute(first, axis, down)  2.99 us
  transfers between devices with their start and end apart: 10, of which 4 were waited for; matrix products, arithmetic and copies ran while one was open for 5% of the time, Pallas kernels for 18%

profile of v3, /device:TPU:0, one launch (start us, length us, event | category | flops | bytes accessed | tf_op | source)
XLA Modules:
  0.0 112.9 jit_solution(12296536584062610936)
XLA Ops:
  0.6 1.0 multiply_convert_fusion
  1.7 2.4 %collective-permute-start = (bf16[8,32,256]{2,1,0:T(8,128)(2,1)S(1)}, bf16[8,32,256]{2,1,0:T(8,128)(2,1)S(1)}, u32[]{:S(2)}, u32[]{:S(2)}) collective-permute-start(bf16[8,32,256]{2,1,0:T(8,128)(2,1)S(1)} %get-tuple-element.15), channel_id=1, source_target_pairs={{0,1},{1,2},{2,3},{3,4},{4,5},{5,6},{6,7},{8,9},{9,10},{10,11},{11... | collective-permute-start | bytes 393224 | tf_op jit(solution)/shard_map/ppermute | solution.py:22
  4.1 1.3 %collective-permute-start.1 = (bf16[8,32,256]{2,1,0:T(8,128)(2,1)S(1)}, bf16[8,32,256]{2,1,0:T(8,128)(2,1)S(1)}, u32[]{:S(2)}, u32[]{:S(2)}) collective-permute-start(bf16[8,32,256]{2,1,0:T(8,128)(2,1)S(1)} %get-tuple-element.16), channel_id=1, source_target_pairs={{1,0},{2,1},{3,2},{4,3},{5,4},{6,5},{7,6},{9,8},{10,9},{11,10},{12... | collective-permute-start | bytes 393224 | tf_op jit(solution)/shard_map/ppermute | solution.py:23
  5.4 1.1 copy.12
  6.5 0.1 rev.3
  6.7 0.8 gather_fusion
  7.5 0.2 copy.13
  7.7 0.8 gather_fusion.1
  8.5 0.2 copy.15
  8.7 0.9 select_bitcast_fusion
  9.6 0.0 collective-permute-done.1
  9.6 1.5 %fusion.17.x_ref = f32[8,128,384]{2,1,0:T(8,128)} fusion(bf16[8,32,256]{2,1,0:T(8,128)(2,1)S(1)} %collective-permute-done.1, bf16[8,64,256]{2,1,0:T(8,128)(2,1)S(1)} %multiply_convert_fusion, bf16[8,32,256]{2,1,0:T(8,128)(2,1)S(1)} %collective-permute-done), kind=kLoop, calls=%fused_computation.19 | loop fusion | flops 4718592 | bytes 2097152 | tf_op jit(solution)/shard_map/jit(_pad)/pad | solution.py:194
  11.1 23.2 %shard_map.111 = f32[128,128]{1,0:T(8,128)} custom-call(f32[8,65,128]{2,1,0:T(8,128)} %get-tuple-element.24.g_ref, f32[8,128,384]{2,1,0:T(8,128)} %fusion.17.x_ref), custom_call_target="tpu_custom_call" | custom-call | tf_op jit(solution)/shard_map/pallas_call | solution.py:135
  34.3 0.8 fusion.56
  35.1 2.4 %collective-permute-start.2 = (f32[64,256]{1,0:T(8,128)S(1)}, f32[64,256]{1,0:T(8,128)S(1)}, u32[]{:S(2)}, u32[]{:S(2)}) collective-permute-start(f32[64,256]{1,0:T(8,128)S(1)} %pad_maximum_fusion.1), channel_id=1, source_target_pairs={{0,8},{8,0},{16,24},{24,16},{1,9},{9,1},{17,25},{25,17},{2,10},{10... | collective-permute-start | bytes 196616 | tf_op jit(solution)/shard_map/ppermute | solution.py:32
  37.5 2.2 %collective-permute-done.2 = f32[64,256]{1,0:T(8,128)S(1)} collective-permute-done((f32[64,256]{1,0:T(8,128)S(1)}, f32[64,256]{1,0:T(8,128)S(1)}, u32[]{:S(2)}, u32[]{:S(2)}) %collective-permute-start.2) | collective-permute-done | bytes 65568 | tf_op jit(solution)/shard_map/ppermute | solution.py:32
  39.7 2.1 %collective-permute-start.3 = (f32[64,256]{1,0:T(8,128)S(1)}, f32[64,256]{1,0:T(8,128)S(1)}, u32[]{:S(2)}, u32[]{:S(2)}) collective-permute-start(f32[64,256]{1,0:T(8,128)S(1)} %fusion.54), channel_id=1, source_target_pairs={{0,16},{8,24},{16,0},{24,8},{1,17},{9,25},{17,1},{25,9},{2,18},{10... | collective-permute-start | bytes 196616 | tf_op jit(solution)/shard_map/ppermute | solution.py:32
  41.8 3.1 %collective-permute-start.8 = (f32[2,2,256]{2,1,0:T(2,128)S(1)}, f32[2,2,256]{2,1,0:T(2,128)S(1)}, u32[]{:S(2)}, u32[]{:S(2)}) collective-permute-start(f32[2,2,256]{2,1,0:T(2,128)S(1)} %get-tuple-element.17), channel_id=1, source_target_pairs={{0,1},{1,2},{2,3},{3,4},{4,5},{5,6},{6,7},{8,9},{9,10},{10,11},{11... | collective-permute-start | bytes 12296 | tf_op jit(solution)/shard_map/ppermute | solution.py:22
  44.9 1.3 %collective-permute-start.9 = (f32[2,2,256]{2,1,0:T(2,128)S(1)}, f32[2,2,256]{2,1,0:T(2,128)S(1)}, u32[]{:S(2)}, u32[]{:S(2)}) collective-permute-start(f32[2,2,256]{2,1,0:T(2,128)S(1)} %get-tuple-element.18), channel_id=1, source_target_pairs={{1,0},{2,1},{3,2},{4,3},{5,4},{6,5},{7,6},{9,8},{10,9},{11,10},{12... | collective-permute-start | bytes 12296 | tf_op jit(solution)/shard_map/ppermute | solution.py:23
  46.3 5.6 %collective-permute-start.4 = (bf16[32,256]{1,0:T(8,128)(2,1)S(1)}, bf16[32,256]{1,0:T(8,128)(2,1)S(1)}, u32[]{:S(2)}, u32[]{:S(2)}) collective-permute-start(bf16[32,256]{1,0:T(8,128)(2,1)S(1)} %get-tuple-element.22), channel_id=1, source_target_pairs={{0,1},{1,2},{2,3},{3,4},{4,5},{5,6},{6,7},{8,9},{9,10},{10,11},{11... | collective-permute-start | bytes 49160 | tf_op jit(solution)/shard_map/ppermute | solution.py:22
  51.9 1.3 %collective-permute-start.5 = (bf16[32,256]{1,0:T(8,128)(2,1)S(1)}, bf16[32,256]{1,0:T(8,128)(2,1)S(1)}, u32[]{:S(2)}, u32[]{:S(2)}) collective-permute-start(bf16[32,256]{1,0:T(8,128)(2,1)S(1)} %get-tuple-element.23), channel_id=1, source_target_pairs={{1,0},{2,1},{3,2},{4,3},{5,4},{6,5},{7,6},{9,8},{10,9},{11,10},{12... | collective-permute-start | bytes 49160 | tf_op jit(solution)/shard_map/ppermute | solution.py:23
  53.2 3.0 %collective-permute-done.5 = bf16[32,256]{1,0:T(8,128)(2,1)S(1)} collective-permute-done((bf16[32,256]{1,0:T(8,128)(2,1)S(1)}, bf16[32,256]{1,0:T(8,128)(2,1)S(1)}, u32[]{:S(2)}, u32[]{:S(2)}) %collective-permute-start.5) | collective-permute-done | bytes 16416 | tf_op jit(solution)/shard_map/ppermute | solution.py:23
  56.2 0.8 fusion.26.e_ref
  57.0 20.4 %shard_map.112 = f32[64,256]{1,0:T(8,128)} custom-call(f32[8,65,128]{2,1,0:T(8,128)} %get-tuple-element.25.g_ref, f32[128,384]{1,0:T(8,128)} %fusion.26.e_ref, bf16[8,64,256]{2,1,0:T(8,128)(2,1)} %w_ref.1), custom_call_target="tpu_custom_call" | custom-call | tf_op jit(solution)/shard_map/pallas_call | solution.py:169
  77.4 1.5 %collective-permute-start.6 = (f32[64,256]{1,0:T(8,128)}, f32[64,256]{1,0:T(8,128)S(1)}, u32[]{:S(2)}, u32[]{:S(2)}) collective-permute-start(f32[64,256]{1,0:T(8,128)} %shard_map.112), channel_id=1, source_target_pairs={{0,8},{8,0},{16,24},{24,16},{1,9},{9,1},{17,25},{25,17},{2,10},{10... | collective-permute-start | bytes 196616 | tf_op jit(solution)/shard_map/ppermute | solution.py:32
  78.9 0.1 and_convert_fusion
  79.0 2.9 %collective-permute-done.6 = f32[64,256]{1,0:T(8,128)S(1)} collective-permute-done((f32[64,256]{1,0:T(8,128)}, f32[64,256]{1,0:T(8,128)S(1)}, u32[]{:S(2)}, u32[]{:S(2)}) %collective-permute-start.6) | collective-permute-done | bytes 65568 | tf_op jit(solution)/shard_map/ppermute | solution.py:32
  81.9 0.8 add.151
  82.7 0.6 collective-permute-start.7
  83.3 4.1 %collective-permute-done.7 = f32[64,256]{1,0:T(8,128)S(1)} collective-permute-done((f32[64,256]{1,0:T(8,128)S(1)}, f32[64,256]{1,0:T(8,128)S(1)}, u32[]{:S(2)}, u32[]{:S(2)}) %collective-permute-start.7) | collective-permute-done | bytes 65568 | tf_op jit(solution)/shard_map/ppermute | solution.py:32
  87.4 0.6 multiply_reduce_fusion
  88.1 14.4 %all-reduce.3 = (f32[]{:T(128)}, f32[]{:T(128)}, f32[]{:T(128)}, f32[]{:T(128)}) all-reduce(f32[]{:T(128)} %get-tuple-element.6, f32[]{:T(128)} %get-tuple-element.7, f32[]{:T(128)} %get-tuple-element.5, f32[]{:T(128)} %get-tuple-element.4), channel_id=1, replica_groups=mesh['comp'=4,'band'=8] {'band'}, use_global_device_ids=true, to_apply=%region_1.2 | all-reduce | flops 4 | bytes 32 | tf_op jit(solution)/shard_map/psum | solution.py:202
  106.4 0.0 copy-start.6
  106.4 0.7 multiply_add_fusion
  107.1 0.3 dynamic_update_slice.3
  107.5 0.1 fusion.32
  107.6 0.1 fusion.34
  107.6 0.1 fusion.36
  107.7 0.1 fusion.38
  107.8 0.1 fusion.40
  107.9 0.1 fusion.42
  108.0 0.1 fusion.44
  108.1 0.1 fusion.46
  108.2 0.1 fusion.30
  108.3 1.9 %fusion.18 = f32[66,66,64]{1,2,0:T(8,128)S(1)} fusion(f32[64,9,1]{0,1,2:T(8,128)S(1)} %reshape.155, f32[9,66,66]{2,1,0:T(8,128)S(1)} %fusion.30), kind=kOutput, calls=%fused_computation.20 | convolution fusion | flops 30108672 | bytes 1274256 | tf_op jit(solution)/shard_map/ct,tij->cij/dot_general | solution.py:47
  110.2 1.5 %fusion.6 = f32[9,66,66]{2,0,1:T(8,128)S(1)} fusion(f32[64,9,1]{0,1,2:T(8,128)S(1)} %reshape.156, f32[66,66,64]{1,2,0:T(8,128)S(1)} %fusion.18, f32[66,66]{1,0:T(8,128)S(1)} %and_convert_fusion, f32[64]{0:T(128)S(1)} %copy-done.6), kind=kOutput, calls=%fused_computation.10 | convolution fusion | flops 30945024 | bytes 1291936 | tf_op jit(solution)/shard_map/ct,cij->tij/dot_general | solution.py:58
  111.7 0.5 slice_add_fusion
  112.2 0.7 fusion.47
  (34 shorter events, 0.2 us)
Async XLA Ops:
  1.7 7.9 %collective-permute-start = (bf16[8,32,256]{2,1,0:T(8,128)(2,1)S(1)}, bf16[8,32,256]{2,1,0:T(8,128)(2,1)S(1)}, u32[]{:S(2)}, u32[]{:S(2)}) collective-permute-start(bf16[8,32,256]{2,1,0:T(8,128)(2,1)S(1)} %get-tuple-element.15), channel_id=1, source_target_pairs={{0,1},{1,2},{2,3},{3,4},{4,5},{5,6},{6,7},{8,9},{9,10},{10,11},{11... | collective-permute-start | bytes 393224 | tf_op jit(solution)/shard_map/ppermute | solution.py:22
  4.1 5.5 %collective-permute-start.1 = (bf16[8,32,256]{2,1,0:T(8,128)(2,1)S(1)}, bf16[8,32,256]{2,1,0:T(8,128)(2,1)S(1)}, u32[]{:S(2)}, u32[]{:S(2)}) collective-permute-start(bf16[8,32,256]{2,1,0:T(8,128)(2,1)S(1)} %get-tuple-element.16), channel_id=1, source_target_pairs={{1,0},{2,1},{3,2},{4,3},{5,4},{6,5},{7,6},{9,8},{10,9},{11,10},{12... | collective-permute-start | bytes 393224 | tf_op jit(solution)/shard_map/ppermute | solution.py:23
  9.6 32.2 %copy-start = (f32[64,256]{1,0:T(8,128)S(1)}, f32[64,256]{1,0:T(8,128)}, u32[]{:S(2)}) copy-start(f32[64,256]{1,0:T(8,128)} %param.10) | copy-start | bytes 196612
  9.6 32.2 %copy-start.1 = (f32[64,256]{1,0:T(8,128)S(1)}, f32[64,256]{1,0:T(8,128)}, u32[]{:S(2)}) copy-start(f32[64,256]{1,0:T(8,128)} %param.8) | copy-start | bytes 196612
  11.1 67.8 %copy-start.4 = (f32[64,3,3]{0,2,1:T(4,128)S(1)}, f32[64,3,3]{0,2,1:T(4,128)}, u32[]{:S(2)}) copy-start(f32[64,3,3]{0,2,1:T(4,128)} %param.13) | copy-start | bytes 6916
  11.1 67.9 %copy-start.5 = (f32[64,3,3]{0,2,1:T(4,128)S(1)}, f32[64,3,3]{0,2,1:T(4,128)}, u32[]{:S(2)}) copy-start(f32[64,3,3]{0,2,1:T(4,128)} %param.15) | copy-start | bytes 6916
  11.1 76.3 %copy-start.2 = (f32[64,256]{1,0:T(8,128)S(1)}, f32[64,256]{1,0:T(8,128)}, u32[]{:S(2)}) copy-start(f32[64,256]{1,0:T(8,128)} %param.9) | copy-start | bytes 196612
  35.1 4.6 %collective-permute-start.2 = (f32[64,256]{1,0:T(8,128)S(1)}, f32[64,256]{1,0:T(8,128)S(1)}, u32[]{:S(2)}, u32[]{:S(2)}) collective-permute-start(f32[64,256]{1,0:T(8,128)S(1)} %pad_maximum_fusion.1), channel_id=1, source_target_pairs={{0,8},{8,0},{16,24},{24,16},{1,9},{9,1},{17,25},{25,17},{2,10},{10... | collective-permute-start | bytes 196616 | tf_op jit(solution)/shard_map/ppermute | solution.py:32
  39.7 6.5 %collective-permute-start.3 = (f32[64,256]{1,0:T(8,128)S(1)}, f32[64,256]{1,0:T(8,128)S(1)}, u32[]{:S(2)}, u32[]{:S(2)}) collective-permute-start(f32[64,256]{1,0:T(8,128)S(1)} %fusion.54), channel_id=1, source_target_pairs={{0,16},{8,24},{16,0},{24,8},{1,17},{9,25},{17,1},{25,9},{2,18},{10... | collective-permute-start | bytes 196616 | tf_op jit(solution)/shard_map/ppermute | solution.py:32
  41.8 41.5 %collective-permute-start.8 = (f32[2,2,256]{2,1,0:T(2,128)S(1)}, f32[2,2,256]{2,1,0:T(2,128)S(1)}, u32[]{:S(2)}, u32[]{:S(2)}) collective-permute-start(f32[2,2,256]{2,1,0:T(2,128)S(1)} %get-tuple-element.17), channel_id=1, source_target_pairs={{0,1},{1,2},{2,3},{3,4},{4,5},{5,6},{6,7},{8,9},{9,10},{10,11},{11... | collective-permute-start | bytes 12296 | tf_op jit(solution)/shard_map/ppermute | solution.py:22
  44.9 38.4 %collective-permute-start.9 = (f32[2,2,256]{2,1,0:T(2,128)S(1)}, f32[2,2,256]{2,1,0:T(2,128)S(1)}, u32[]{:S(2)}, u32[]{:S(2)}) collective-permute-start(f32[2,2,256]{2,1,0:T(2,128)S(1)} %get-tuple-element.18), channel_id=1, source_target_pairs={{1,0},{2,1},{3,2},{4,3},{5,4},{6,5},{7,6},{9,8},{10,9},{11,10},{12... | collective-permute-start | bytes 12296 | tf_op jit(solution)/shard_map/ppermute | solution.py:23
  46.3 6.9 %collective-permute-start.4 = (bf16[32,256]{1,0:T(8,128)(2,1)S(1)}, bf16[32,256]{1,0:T(8,128)(2,1)S(1)}, u32[]{:S(2)}, u32[]{:S(2)}) collective-permute-start(bf16[32,256]{1,0:T(8,128)(2,1)S(1)} %get-tuple-element.22), channel_id=1, source_target_pairs={{0,1},{1,2},{2,3},{3,4},{4,5},{5,6},{6,7},{8,9},{9,10},{10,11},{11... | collective-permute-start | bytes 49160 | tf_op jit(solution)/shard_map/ppermute | solution.py:22
  51.9 4.3 %collective-permute-start.5 = (bf16[32,256]{1,0:T(8,128)(2,1)S(1)}, bf16[32,256]{1,0:T(8,128)(2,1)S(1)}, u32[]{:S(2)}, u32[]{:S(2)}) collective-permute-start(bf16[32,256]{1,0:T(8,128)(2,1)S(1)} %get-tuple-element.23), channel_id=1, source_target_pairs={{1,0},{2,1},{3,2},{4,3},{5,4},{6,5},{7,6},{9,8},{10,9},{11,10},{12... | collective-permute-start | bytes 49160 | tf_op jit(solution)/shard_map/ppermute | solution.py:23
  77.4 4.5 %collective-permute-start.6 = (f32[64,256]{1,0:T(8,128)}, f32[64,256]{1,0:T(8,128)S(1)}, u32[]{:S(2)}, u32[]{:S(2)}) collective-permute-start(f32[64,256]{1,0:T(8,128)} %shard_map.112), channel_id=1, source_target_pairs={{0,8},{8,0},{16,24},{24,16},{1,9},{9,1},{17,25},{25,17},{2,10},{10... | collective-permute-start | bytes 196616 | tf_op jit(solution)/shard_map/ppermute | solution.py:32
  82.7 4.7 %collective-permute-start.7 = (f32[64,256]{1,0:T(8,128)S(1)}, f32[64,256]{1,0:T(8,128)S(1)}, u32[]{:S(2)}, u32[]{:S(2)}) collective-permute-start(f32[64,256]{1,0:T(8,128)S(1)} %add.151), channel_id=1, source_target_pairs={{0,16},{8,24},{16,0},{24,8},{1,17},{9,25},{17,1},{25,9},{2,18},{10... | collective-permute-start | bytes 196616 | tf_op jit(solution)/shard_map/ppermute | solution.py:32
  106.4 3.7 %copy-start.6 = (f32[64]{0:T(128)S(1)}, f32[64]{0:T(128)}, u32[]{:S(2)}) copy-start(f32[64]{0:T(128)} %param.14) | copy-start | bytes 772
  107.1 4.6 %copy-start.3 = (f32[64,256]{1,0:T(8,128)}, f32[64,256]{1,0:T(8,128)S(1)}, u32[]{:S(2)}) copy-start(f32[64,256]{1,0:T(8,128)S(1)} %get-tuple-element.19) | copy-start | bytes 196612

commit v4 on v3

--- a/solution.py
+++ b/solution.py
@@ -23,6 +23,41 @@
         after = lax.ppermute(first, axis, down)
         array = jnp.concatenate([before, array, after], axis=dim)
     return array
+
+
+def split3(value):
+    parts = []
+    for _ in range(3):
+        part = lax.reduce_precision(value, exponent_bits=8, mantissa_bits=7)
+        parts.append(part.astype(jnp.bfloat16))
+        value = value - part
+    return jnp.stack(parts)
+
+
+def join3(parts):
+    parts = parts.astype(jnp.float32)
+    return (parts[0] + parts[1]) + parts[2]
+
+
+def band_halo(shaped, edges, half, reach):
+    count, rows = lax.axis_size("band"), shaped.shape[1]
+    up = [(i, i + 1) for i in range(count - 1)]
+    down = [(j, i) for i, j in up]
+    width = shaped.shape[2]
+
+    def slab(shaped_rows, edge_rows):
+        coded = split3(edge_rows).reshape(-1, width)
+        coded = jnp.pad(coded, ((0, half - coded.shape[0]), (0, 0)))
+        return jnp.concatenate([shaped_rows, coded[None]], axis=0)
+
+    last = slab(shaped[:, rows - half :], edges[:, edges.shape[1] - reach :])
+    first = slab(shaped[:, :half], edges[:, :reach])
+    before = lax.ppermute(last, "band", up)
+    after = lax.ppermute(first, "band", down)
+    nk, count_parts = shaped.shape[0], 3 * edges.shape[0] * reach
+    decode = lambda got: join3(got[nk, :count_parts].reshape(3, edges.shape[0], reach, width))
+    padded = jnp.concatenate([before[:nk], shaped, after[:nk]], axis=1)
+    return padded, decode(before), decode(after)
 
 
 def pair_sum(value, axis):
@@ -186,11 +221,12 @@
 ):
     rows, width = direction.shape
     half = (kernels.shape[1] - 1) // 2
-    framed_both = with_halo(jnp.stack([estimate, direction]), (("band", 1),), 2)
-    framed_estimate, framed_direction = framed_both[0], framed_both[1]
     maps_wide = weight_maps.astype(jnp.float32)
     shaped = (maps_wide * direction[None]).astype(jnp.bfloat16)
-    padded = with_halo(shaped, (("band", 1),), half)
+    edges = jnp.stack([estimate, direction])
+    padded, edge_before, edge_after = band_halo(shaped, edges, half, 2)
+    framed_both = jnp.concatenate([edge_before, edges, edge_after], axis=1)
+    framed_estimate, framed_direction = framed_both[0], framed_both[1]
     framed = jnp.pad(padded.astype(jnp.float32), ((0, 0), (0, 0), (half, LANES - half)))
     partial_value = blur(tap_rows(kernels), framed, rows)
     image = pair_sum(partial_value, "comp").astype(jnp.bfloat16)
@@ -199,15 +235,16 @@
     local_sum = back_weighted(tap_rows(kernels[:, ::-1, ::-1]), edged, weight_maps)
     normal = pair_sum(local_sum, "comp")
     curved = normal + damping * direction
-    old, product, cross, square = lax.psum(
-        (
+    sums = jnp.stack(
+        [
             jnp.sum(residual * residual),
             jnp.sum(direction * curved),
             jnp.sum(residual * curved),
             jnp.sum(curved * curved),
-        ),
-        "band",
-    )
+        ]
+    )
+    sums = jnp.where(lax.axis_index("comp") == 0, sums, 0.0)
+    old, product, cross, square = lax.psum(sums, ("comp", "band"))
     alpha = old / product
     residual_next = residual - alpha * curved
     new = old - 2.0 * alpha * cross + alpha * alpha * square

time: 113 us -> 141 us (1.25)
  blocking collectives: 14.4 us -> 41.4 us
  starting transfers between devices: 21.5 us -> 15.8 us
  other arithmetic: 7.72 us -> 11.2 us
  waiting for transfers between devices: 12.2 us -> 14.3 us
    psum x1, blocking collectives: 14.4 us -> 41.4 us  [per_device(): old, product, cross, square = lax.psum(sums, ('comp', 'band'))]
    ppermute x3 -> x1, starting transfers between devices: 11.1 us -> 1.44 us  [with_halo(): before = lax.ppermute(last, axis, up)]
    ppermute x0 -> x2, starting transfers between devices: none -> 4.33 us  [the longest x1 3.04 us: band_halo(): before = lax.ppermute(last, 'band', up)]
    select_n x0 -> x1, other arithmetic: none -> 2.66 us  [per_device(): sums = jnp.where(lax.axis_index('comp') == 0, sums, 0.0)]
    ppermute x3 -> x1, starting transfers between devices: 3.88 us -> 1.29 us  [with_halo(): after = lax.ppermute(first, axis, down)]
    ppermute x4, starting transfers between devices: 6.55 us -> 8.69 us  [pair_sum(): lax.ppermute(value, axis, [(i, i ^ step) for i in range(count)])]
    ppermute x3 -> x1, waiting for transfers between devices: 2.99 us -> 3.79 us  [with_halo(): after = lax.ppermute(first, axis, down)]
  transfers between devices with their start and end apart: 10 -> 8, of which waited for: 4 -> 5; matrix products, arithmetic and copies ran while one was open for 5% -> 3% of each run, Pallas kernels for 18% -> 0%
where the time goes in v4:
time: 141 us
  Pallas kernels  43.6 us (31%)
  blocking collectives  41.4 us (29%)
  starting transfers between devices  15.8 us (11%)
  waiting for transfers between devices  14.3 us (10%)
  other arithmetic  11.2 us (8%)
  local copies, waits for them, and re-layouts  5.91 us (4%)
  between operations  4.94 us (4%)
  matrix products  3.38 us (2%)
    psum x1, blocking collectives, per_device(): old, product, cross, square = lax.psum(sums, ('comp', 'band'))  41.4 us
    pallas_call x1, Pallas kernels, blur(): pl.pallas_call(functools.partial(_blur_body, span=span, rows=rows, blocks...  23.1 us
    pallas_call x1, Pallas kernels, back_weighted(): pl.pallas_call(functools.partial(_back_body, span=span, rows=rows, blocks...  20.4 us
    ppermute x4, waiting for transfers between devices, pair_sum(): lax.ppermute(value, axis, [(i, i ^ step) for i in range(count)])  10.5 us
    ppermute x4, starting transfers between devices, pair_sum(): lax.ppermute(value, axis, [(i, i ^ step) for i in range(count)])  8.69 us
    ppermute x1, waiting for transfers between devices, with_halo(): after = lax.ppermute(first, axis, down)  3.79 us
    ppermute x1, starting transfers between devices, band_halo(): before = lax.ppermute(last, 'band', up)  3.04 us
  transfers between devices with their start and end apart: 8, of which 5 were waited for; matrix products, arithmetic and copies ran while one was open for 3% of the time, Pallas kernels for 0%

profile of v4, /device:TPU:0, one launch (start us, length us, event | category | flops | bytes accessed | tf_op | source)
XLA Modules:
  0.0 140.6 jit_solution(8877999007434066431)
XLA Ops:
  0.6 0.8 fusion.52
  1.5 1.0 multiply_convert_fusion
  2.5 1.3 collective-permute-start.1
  3.9 3.0 %collective-permute-start = (bf16[9,32,256]{2,1,0:T(8,128)(2,1)S(1)}, bf16[9,32,256]{2,1,0:T(8,128)(2,1)S(1)}, u32[]{:S(2)}, u32[]{:S(2)}) collective-permute-start(bf16[9,32,256]{2,1,0:T(8,128)(2,1)S(1)} %pad_maximum_fusion), channel_id=1, source_target_pairs={{0,1},{1,2},{2,3},{3,4},{4,5},{5,6},{6,7},{8,9},{9,10},{10,11},{11... | collective-permute-start | bytes 442376 | tf_op jit(solution)/shard_map/ppermute | solution.py:55
  7.0 1.1 copy.12
  8.1 0.1 rev.3
  8.3 0.8 gather_fusion
  9.0 0.2 copy.13
  9.3 0.8 gather_fusion.1
  10.1 0.2 copy.15
  10.3 0.9 select_bitcast_fusion
  11.3 1.5 %fusion.17.x_ref = f32[8,128,384]{2,1,0:T(8,128)} fusion(bf16[8,32,256]{2,1,0:T(8,128)(2,1)S(1)} %slice.169, bf16[8,64,256]{2,1,0:T(8,128)(2,1)S(1)} %multiply_convert_fusion, bf16[8,32,256]{2,1,0:T(8,128)(2,1)S(1)} %slice.167), kind=kLoop, calls=%fused_computation.19 | loop fusion | flops 4718592 | bytes 2097152 | tf_op jit(solution)/shard_map/jit(_pad)/pad | solution.py:230
  12.8 23.1 %shard_map.111 = f32[128,128]{1,0:T(8,128)} custom-call(f32[8,65,128]{2,1,0:T(8,128)} %get-tuple-element.32.g_ref, f32[8,128,384]{2,1,0:T(8,128)} %fusion.17.x_ref), custom_call_target="tpu_custom_call" | custom-call | tf_op jit(solution)/shard_map/pallas_call | solution.py:170
  35.9 0.8 fusion.66
  36.7 3.0 %collective-permute-start.2 = (f32[64,256]{1,0:T(8,128)S(1)}, f32[64,256]{1,0:T(8,128)S(1)}, u32[]{:S(2)}, u32[]{:S(2)}) collective-permute-start(f32[64,256]{1,0:T(8,128)S(1)} %pad_maximum_fusion.3), channel_id=1, source_target_pairs={{0,8},{8,0},{16,24},{24,16},{1,9},{9,1},{17,25},{25,17},{2,10},{10... | collective-permute-start | bytes 196616 | tf_op jit(solution)/shard_map/ppermute | solution.py:67
  39.8 0.1 and_convert_fusion
  39.9 2.1 %collective-permute-done.2 = f32[64,256]{1,0:T(8,128)S(1)} collective-permute-done((f32[64,256]{1,0:T(8,128)S(1)}, f32[64,256]{1,0:T(8,128)S(1)}, u32[]{:S(2)}, u32[]{:S(2)}) %collective-permute-start.2) | collective-permute-done | bytes 65568 | tf_op jit(solution)/shard_map/ppermute | solution.py:67
  42.0 2.6 %collective-permute-start.3 = (f32[64,256]{1,0:T(8,128)S(1)}, f32[64,256]{1,0:T(8,128)S(1)}, u32[]{:S(2)}, u32[]{:S(2)}) collective-permute-start(f32[64,256]{1,0:T(8,128)S(1)} %fusion.64), channel_id=1, source_target_pairs={{0,16},{8,24},{16,0},{24,8},{1,17},{9,25},{17,1},{25,9},{2,18},{10... | collective-permute-start | bytes 196616 | tf_op jit(solution)/shard_map/ppermute | solution.py:67
  44.6 2.4 %collective-permute-done.3 = f32[64,256]{1,0:T(8,128)S(1)} collective-permute-done((f32[64,256]{1,0:T(8,128)S(1)}, f32[64,256]{1,0:T(8,128)S(1)}, u32[]{:S(2)}, u32[]{:S(2)}) %collective-permute-start.3) | collective-permute-done | bytes 65568 | tf_op jit(solution)/shard_map/ppermute | solution.py:67
  47.0 1.4 %collective-permute-start.4 = (bf16[32,256]{1,0:T(8,128)(2,1)S(1)}, bf16[32,256]{1,0:T(8,128)(2,1)S(1)}, u32[]{:S(2)}, u32[]{:S(2)}) collective-permute-start(bf16[32,256]{1,0:T(8,128)(2,1)S(1)} %get-tuple-element.22), channel_id=1, source_target_pairs={{0,1},{1,2},{2,3},{3,4},{4,5},{5,6},{6,7},{8,9},{9,10},{10,11},{11... | collective-permute-start | bytes 49160 | tf_op jit(solution)/shard_map/ppermute | solution.py:22
  48.5 1.3 collective-permute-start.5
  49.8 3.8 %collective-permute-done.5 = bf16[32,256]{1,0:T(8,128)(2,1)S(1)} collective-permute-done((bf16[32,256]{1,0:T(8,128)(2,1)S(1)}, bf16[32,256]{1,0:T(8,128)(2,1)S(1)}, u32[]{:S(2)}, u32[]{:S(2)}) %collective-permute-start.5) | collective-permute-done | bytes 16416 | tf_op jit(solution)/shard_map/ppermute | solution.py:23
  53.6 0.8 fusion.26.e_ref
  54.3 20.4 %shard_map.112 = f32[64,256]{1,0:T(8,128)} custom-call(f32[8,65,128]{2,1,0:T(8,128)} %get-tuple-element.33.g_ref, f32[128,384]{1,0:T(8,128)} %fusion.26.e_ref, bf16[8,64,256]{2,1,0:T(8,128)(2,1)} %w_ref.1), custom_call_target="tpu_custom_call" | custom-call | tf_op jit(solution)/shard_map/pallas_call | solution.py:204
  74.8 1.5 %collective-permute-start.6 = (f32[64,256]{1,0:T(8,128)}, f32[64,256]{1,0:T(8,128)S(1)}, u32[]{:S(2)}, u32[]{:S(2)}) collective-permute-start(f32[64,256]{1,0:T(8,128)} %shard_map.112), channel_id=1, source_target_pairs={{0,8},{8,0},{16,24},{24,16},{1,9},{9,1},{17,25},{25,17},{2,10},{10... | collective-permute-start | bytes 196616 | tf_op jit(solution)/shard_map/ppermute | solution.py:67
  76.3 3.0 %collective-permute-done.6 = f32[64,256]{1,0:T(8,128)S(1)} collective-permute-done((f32[64,256]{1,0:T(8,128)}, f32[64,256]{1,0:T(8,128)S(1)}, u32[]{:S(2)}, u32[]{:S(2)}) %collective-permute-start.6) | collective-permute-done | bytes 65568 | tf_op jit(solution)/shard_map/ppermute | solution.py:67
  79.3 0.8 add.171
  80.1 1.6 %collective-permute-start.7 = (f32[64,256]{1,0:T(8,128)S(1)}, f32[64,256]{1,0:T(8,128)S(1)}, u32[]{:S(2)}, u32[]{:S(2)}) collective-permute-start(f32[64,256]{1,0:T(8,128)S(1)} %add.171), channel_id=1, source_target_pairs={{0,16},{8,24},{16,0},{24,8},{1,17},{9,25},{17,1},{25,9},{2,18},{10... | collective-permute-start | bytes 196616 | tf_op jit(solution)/shard_map/ppermute | solution.py:67
  81.7 3.1 %collective-permute-done.7 = f32[64,256]{1,0:T(8,128)S(1)} collective-permute-done((f32[64,256]{1,0:T(8,128)S(1)}, f32[64,256]{1,0:T(8,128)S(1)}, u32[]{:S(2)}, u32[]{:S(2)}) %collective-permute-start.7) | collective-permute-done | bytes 65568 | tf_op jit(solution)/shard_map/ppermute | solution.py:67
  84.8 0.6 multiply_reduce_fusion.3
  85.4 2.7 %broadcast_select_fusion = f32[4]{0:T(128)S(1)} fusion(pred[]{:T(512)S(6)} %eq.6, f32[1]{0:T(128)} %bitcast.16, f32[1]{0:T(128)} %bitcast.15, f32[1]{0:T(128)} %bitcast.14, f32[1]{0:T(128)} %bitcast), kind=kLoop, calls=%fused_computation.128 | loop fusion | flops 16 | bytes 33 | tf_op jit(solution)/shard_map/jit(_where)/select_n | solution.py:246
  88.1 41.4 %psum.7 = f32[4]{0:T(128)S(1)} all-reduce(f32[4]{0:T(128)S(1)} %broadcast_select_fusion), channel_id=1, replica_groups=mesh['comp'=4,'band'=8] {'comp','band'}, use_global_device_ids=true, to_apply=%region_4.5 | all-reduce | flops 4 | bytes 32 | tf_op jit(solution)/shard_map/psum | solution.py:247
  129.6 0.6 fusion.68
  134.2 0.7 multiply_add_fusion
  134.8 0.3 dynamic_update_slice.3
  135.2 0.1 fusion.32
  135.3 0.1 fusion.34
  135.4 0.1 fusion.36
  135.4 0.1 fusion.38
  135.5 0.1 fusion.40
  135.6 0.1 fusion.42
  135.7 0.1 fusion.44
  135.8 0.1 fusion.46
  135.9 0.1 fusion.30
  136.0 1.9 %fusion.18 = f32[66,66,64]{1,2,0:T(8,128)S(1)} fusion(f32[64,9,1]{0,1,2:T(8,128)S(1)} %reshape.181, f32[9,66,66]{2,1,0:T(8,128)S(1)} %fusion.30), kind=kOutput, calls=%fused_computation.20 | convolution fusion | flops 30108672 | bytes 1274256 | tf_op jit(solution)/shard_map/ct,tij->cij/dot_general | solution.py:82
  137.9 1.5 %fusion.6 = f32[9,66,66]{2,0,1:T(8,128)S(1)} fusion(f32[64,9,1]{0,1,2:T(8,128)S(1)} %reshape.182, f32[66,66,64]{1,2,0:T(8,128)S(1)} %fusion.18, f32[66,66]{1,0:T(8,128)S(1)} %and_convert_fusion, f32[64]{0:T(128)S(1)} %copy-done.6), kind=kOutput, calls=%fused_computation.10 | convolution fusion | flops 30945024 | bytes 1291936 | tf_op jit(solution)/shard_map/ct,cij->tij/dot_general | solution.py:93
  139.4 0.5 slice_add_fusion
  139.9 0.7 fusion.47
  (49 shorter events, 0.4 us)
Async XLA Ops:
  2.5 8.7 %collective-permute-start.1 = (bf16[9,32,256]{2,1,0:T(8,128)(2,1)S(1)}, bf16[9,32,256]{2,1,0:T(8,128)(2,1)S(1)}, u32[]{:S(2)}, u32[]{:S(2)}) collective-permute-start(bf16[9,32,256]{2,1,0:T(8,128)(2,1)S(1)} %pad_maximum_fusion.1), channel_id=1, source_target_pairs={{1,0},{2,1},{3,2},{4,3},{5,4},{6,5},{7,6},{9,8},{10,9},{11,10},{12... | collective-permute-start | bytes 442376 | tf_op jit(solution)/shard_map/ppermute | solution.py:56
  3.9 7.3 %collective-permute-start = (bf16[9,32,256]{2,1,0:T(8,128)(2,1)S(1)}, bf16[9,32,256]{2,1,0:T(8,128)(2,1)S(1)}, u32[]{:S(2)}, u32[]{:S(2)}) collective-permute-start(bf16[9,32,256]{2,1,0:T(8,128)(2,1)S(1)} %pad_maximum_fusion), channel_id=1, source_target_pairs={{0,1},{1,2},{2,3},{3,4},{4,5},{5,6},{6,7},{8,9},{9,10},{10,11},{11... | collective-permute-start | bytes 442376 | tf_op jit(solution)/shard_map/ppermute | solution.py:55
  11.2 28.6 %copy-start.4 = (f32[64,3,3]{0,2,1:T(4,128)S(1)}, f32[64,3,3]{0,2,1:T(4,128)}, u32[]{:S(2)}) copy-start(f32[64,3,3]{0,2,1:T(4,128)} %param.13) | copy-start | bytes 6916
  11.3 28.6 %copy-start.5 = (f32[64,3,3]{0,2,1:T(4,128)S(1)}, f32[64,3,3]{0,2,1:T(4,128)}, u32[]{:S(2)}) copy-start(f32[64,3,3]{0,2,1:T(4,128)} %param.15) | copy-start | bytes 6916
  12.8 72.0 %copy-start = (f32[64,256]{1,0:T(8,128)S(1)}, f32[64,256]{1,0:T(8,128)}, u32[]{:S(2)}) copy-start(f32[64,256]{1,0:T(8,128)} %param.10) | copy-start | bytes 196612
  12.8 72.0 %copy-start.2 = (f32[64,256]{1,0:T(8,128)S(1)}, f32[64,256]{1,0:T(8,128)}, u32[]{:S(2)}) copy-start(f32[64,256]{1,0:T(8,128)} %param.9) | copy-start | bytes 196612
  12.8 75.3 %copy-start.1 = (f32[64,256]{1,0:T(8,128)S(1)}, f32[64,256]{1,0:T(8,128)}, u32[]{:S(2)}) copy-start(f32[64,256]{1,0:T(8,128)} %param.8) | copy-start | bytes 196612
  36.7 5.3 %collective-permute-start.2 = (f32[64,256]{1,0:T(8,128)S(1)}, f32[64,256]{1,0:T(8,128)S(1)}, u32[]{:S(2)}, u32[]{:S(2)}) collective-permute-start(f32[64,256]{1,0:T(8,128)S(1)} %pad_maximum_fusion.3), channel_id=1, source_target_pairs={{0,8},{8,0},{16,24},{24,16},{1,9},{9,1},{17,25},{25,17},{2,10},{10... | collective-permute-start | bytes 196616 | tf_op jit(solution)/shard_map/ppermute | solution.py:67
  42.0 4.9 %collective-permute-start.3 = (f32[64,256]{1,0:T(8,128)S(1)}, f32[64,256]{1,0:T(8,128)S(1)}, u32[]{:S(2)}, u32[]{:S(2)}) collective-permute-start(f32[64,256]{1,0:T(8,128)S(1)} %fusion.64), channel_id=1, source_target_pairs={{0,16},{8,24},{16,0},{24,8},{1,17},{9,25},{17,1},{25,9},{2,18},{10... | collective-permute-start | bytes 196616 | tf_op jit(solution)/shard_map/ppermute | solution.py:67
  47.0 2.8 %collective-permute-start.4 = (bf16[32,256]{1,0:T(8,128)(2,1)S(1)}, bf16[32,256]{1,0:T(8,128)(2,1)S(1)}, u32[]{:S(2)}, u32[]{:S(2)}) collective-permute-start(bf16[32,256]{1,0:T(8,128)(2,1)S(1)} %get-tuple-element.22), channel_id=1, source_target_pairs={{0,1},{1,2},{2,3},{3,4},{4,5},{5,6},{6,7},{8,9},{9,10},{10,11},{11... | collective-permute-start | bytes 49160 | tf_op jit(solution)/shard_map/ppermute | solution.py:22
  48.5 5.1 %collective-permute-start.5 = (bf16[32,256]{1,0:T(8,128)(2,1)S(1)}, bf16[32,256]{1,0:T(8,128)(2,1)S(1)}, u32[]{:S(2)}, u32[]{:S(2)}) collective-permute-start(bf16[32,256]{1,0:T(8,128)(2,1)S(1)} %get-tuple-element.23), channel_id=1, source_target_pairs={{1,0},{2,1},{3,2},{4,3},{5,4},{6,5},{7,6},{9,8},{10,9},{11,10},{12... | collective-permute-start | bytes 49160 | tf_op jit(solution)/shard_map/ppermute | solution.py:23
  74.8 4.5 %collective-permute-start.6 = (f32[64,256]{1,0:T(8,128)}, f32[64,256]{1,0:T(8,128)S(1)}, u32[]{:S(2)}, u32[]{:S(2)}) collective-permute-start(f32[64,256]{1,0:T(8,128)} %shard_map.112), channel_id=1, source_target_pairs={{0,8},{8,0},{16,24},{24,16},{1,9},{9,1},{17,25},{25,17},{2,10},{10... | collective-permute-start | bytes 196616 | tf_op jit(solution)/shard_map/ppermute | solution.py:67
  80.1 4.7 %collective-permute-start.7 = (f32[64,256]{1,0:T(8,128)S(1)}, f32[64,256]{1,0:T(8,128)S(1)}, u32[]{:S(2)}, u32[]{:S(2)}) collective-permute-start(f32[64,256]{1,0:T(8,128)S(1)} %add.171), channel_id=1, source_target_pairs={{0,16},{8,24},{16,0},{24,8},{1,17},{9,25},{17,1},{25,9},{2,18},{10... | collective-permute-start | bytes 196616 | tf_op jit(solution)/shard_map/ppermute | solution.py:67
  134.1 3.7 %copy-start.6 = (f32[64]{0:T(128)S(1)}, f32[64]{0:T(128)}, u32[]{:S(2)}) copy-start(f32[64]{0:T(128)} %param.14) | copy-start | bytes 772
  134.8 4.6 %copy-start.3 = (f32[64,256]{1,0:T(8,128)}, f32[64,256]{1,0:T(8,128)S(1)}, u32[]{:S(2)}) copy-start(f32[64,256]{1,0:T(8,128)S(1)} %get-tuple-element.19) | copy-start | bytes 196612

commit v5 on v4

--- a/solution.py
+++ b/solution.py
@@ -243,8 +243,7 @@
             jnp.sum(curved * curved),
         ]
     )
-    sums = jnp.where(lax.axis_index("comp") == 0, sums, 0.0)
-    old, product, cross, square = lax.psum(sums, ("comp", "band"))
+    old, product, cross, square = lax.psum(sums, "band")
     alpha = old / product
     residual_next = residual - alpha * curved
     new = old - 2.0 * alpha * cross + alpha * alpha * square

time: 141 us -> 113 us (0.80)
  blocking collectives: 41.4 us -> 13.8 us
    psum x1, blocking collectives: 41.4 us -> 13.8 us  [per_device(): old, product, cross, square = lax.psum(sums, 'band')]
    select_n x1 -> x0, other arithmetic: 2.66 us -> none  [per_device(): sums = jnp.where(lax.axis_index('comp') == 0, sums, 0.0)]
    another operation x0 -> x1, other arithmetic: none -> 2.66 us  [per_device(): jnp.stack([jnp.sum(residual * residual), jnp.sum(direction * curved), jnp...]
  transfers between devices with their start and end apart: 8 -> 8, of which waited for: 5 -> 5; matrix products, arithmetic and copies ran while one was open for 3% -> 4% of each run, Pallas kernels for 0% -> 0%
where the time goes in v5:
time: 113 us
  Pallas kernels  43.6 us (39%)
  starting transfers between devices  15.8 us (14%)
  waiting for transfers between devices  14.3 us (13%)
  blocking collectives  13.8 us (12%)
  other arithmetic  11.2 us (10%)
  local copies, waits for them, and re-layouts  5.91 us (5%)
  between operations  4.94 us (4%)
  matrix products  3.38 us (3%)
    pallas_call x1, Pallas kernels, blur(): pl.pallas_call(functools.partial(_blur_body, span=span, rows=rows, blocks...  23.1 us
    pallas_call x1, Pallas kernels, back_weighted(): pl.pallas_call(functools.partial(_back_body, span=span, rows=rows, blocks...  20.4 us
    psum x1, blocking collectives, per_device(): old, product, cross, square = lax.psum(sums, 'band')  13.8 us
    ppermute x4, waiting for transfers between devices, pair_sum(): lax.ppermute(value, axis, [(i, i ^ step) for i in range(count)])  10.5 us
    ppermute x4, starting transfers between devices, pair_sum(): lax.ppermute(value, axis, [(i, i ^ step) for i in range(count)])  8.69 us
    ppermute x1, waiting for transfers between devices, with_halo(): after = lax.ppermute(first, axis, down)  3.79 us
    ppermute x1, starting transfers between devices, band_halo(): before = lax.ppermute(last, 'band', up)  3.04 us
    another operation x1, other arithmetic, per_device(): jnp.stack([jnp.sum(residual * residual), jnp.sum(direction * curved), jnp...  2.66 us
  transfers between devices with their start and end apart: 8, of which 5 were waited for; matrix products, arithmetic and copies ran while one was open for 4% of the time, Pallas kernels for 0%

profile of v5, /device:TPU:0, one launch (start us, length us, event | category | flops | bytes accessed | tf_op | source)
XLA Modules:
  0.0 112.9 jit_solution(1982109081603715678)
XLA Ops:
  0.6 0.8 fusion.52
  1.5 1.0 multiply_convert_fusion
  2.5 1.3 %collective-permute-start.1 = (bf16[9,32,256]{2,1,0:T(8,128)(2,1)S(1)}, bf16[9,32,256]{2,1,0:T(8,128)(2,1)S(1)}, u32[]{:S(2)}, u32[]{:S(2)}) collective-permute-start(bf16[9,32,256]{2,1,0:T(8,128)(2,1)S(1)} %pad_maximum_fusion.1), channel_id=1, source_target_pairs={{1,0},{2,1},{3,2},{4,3},{5,4},{6,5},{7,6},{9,8},{10,9},{11,10},{12... | collective-permute-start | bytes 442376 | tf_op jit(solution)/shard_map/ppermute | solution.py:56
  3.9 3.0 %collective-permute-start = (bf16[9,32,256]{2,1,0:T(8,128)(2,1)S(1)}, bf16[9,32,256]{2,1,0:T(8,128)(2,1)S(1)}, u32[]{:S(2)}, u32[]{:S(2)}) collective-permute-start(bf16[9,32,256]{2,1,0:T(8,128)(2,1)S(1)} %pad_maximum_fusion), channel_id=1, source_target_pairs={{0,1},{1,2},{2,3},{3,4},{4,5},{5,6},{6,7},{8,9},{9,10},{10,11},{11... | collective-permute-start | bytes 442376 | tf_op jit(solution)/shard_map/ppermute | solution.py:55
  7.0 1.1 copy.12
  8.1 0.1 rev.3
  8.3 0.8 gather_fusion
  9.0 0.2 copy.13
  9.3 0.8 gather_fusion.1
  10.1 0.2 copy.15
  10.3 0.9 select_bitcast_fusion
  11.3 1.5 %fusion.17.x_ref = f32[8,128,384]{2,1,0:T(8,128)} fusion(bf16[8,32,256]{2,1,0:T(8,128)(2,1)S(1)} %slice.169, bf16[8,64,256]{2,1,0:T(8,128)(2,1)S(1)} %multiply_convert_fusion, bf16[8,32,256]{2,1,0:T(8,128)(2,1)S(1)} %slice.167), kind=kLoop, calls=%fused_computation.19 | loop fusion | flops 4718592 | bytes 2097152 | tf_op jit(solution)/shard_map/jit(_pad)/pad | solution.py:230
  12.8 23.1 %shard_map.111 = f32[128,128]{1,0:T(8,128)} custom-call(f32[8,65,128]{2,1,0:T(8,128)} %get-tuple-element.32.g_ref, f32[8,128,384]{2,1,0:T(8,128)} %fusion.17.x_ref), custom_call_target="tpu_custom_call" | custom-call | tf_op jit(solution)/shard_map/pallas_call | solution.py:170
  35.9 0.8 fusion.66
  36.7 3.0 %collective-permute-start.2 = (f32[64,256]{1,0:T(8,128)S(1)}, f32[64,256]{1,0:T(8,128)S(1)}, u32[]{:S(2)}, u32[]{:S(2)}) collective-permute-start(f32[64,256]{1,0:T(8,128)S(1)} %pad_maximum_fusion.3), channel_id=1, source_target_pairs={{0,8},{8,0},{16,24},{24,16},{1,9},{9,1},{17,25},{25,17},{2,10},{10... | collective-permute-start | bytes 196616 | tf_op jit(solution)/shard_map/ppermute | solution.py:67
  39.8 0.1 and_convert_fusion
  39.9 2.1 %collective-permute-done.2 = f32[64,256]{1,0:T(8,128)S(1)} collective-permute-done((f32[64,256]{1,0:T(8,128)S(1)}, f32[64,256]{1,0:T(8,128)S(1)}, u32[]{:S(2)}, u32[]{:S(2)}) %collective-permute-start.2) | collective-permute-done | bytes 65568 | tf_op jit(solution)/shard_map/ppermute | solution.py:67
  42.0 2.6 %collective-permute-start.3 = (f32[64,256]{1,0:T(8,128)S(1)}, f32[64,256]{1,0:T(8,128)S(1)}, u32[]{:S(2)}, u32[]{:S(2)}) collective-permute-start(f32[64,256]{1,0:T(8,128)S(1)} %fusion.64), channel_id=1, source_target_pairs={{0,16},{8,24},{16,0},{24,8},{1,17},{9,25},{17,1},{25,9},{2,18},{10... | collective-permute-start | bytes 196616 | tf_op jit(solution)/shard_map/ppermute | solution.py:67
  44.6 2.4 %collective-permute-done.3 = f32[64,256]{1,0:T(8,128)S(1)} collective-permute-done((f32[64,256]{1,0:T(8,128)S(1)}, f32[64,256]{1,0:T(8,128)S(1)}, u32[]{:S(2)}, u32[]{:S(2)}) %collective-permute-start.3) | collective-permute-done | bytes 65568 | tf_op jit(solution)/shard_map/ppermute | solution.py:67
  47.0 1.4 %collective-permute-start.4 = (bf16[32,256]{1,0:T(8,128)(2,1)S(1)}, bf16[32,256]{1,0:T(8,128)(2,1)S(1)}, u32[]{:S(2)}, u32[]{:S(2)}) collective-permute-start(bf16[32,256]{1,0:T(8,128)(2,1)S(1)} %get-tuple-element.22), channel_id=1, source_target_pairs={{0,1},{1,2},{2,3},{3,4},{4,5},{5,6},{6,7},{8,9},{9,10},{10,11},{11... | collective-permute-start | bytes 49160 | tf_op jit(solution)/shard_map/ppermute | solution.py:22
  48.5 1.3 %collective-permute-start.5 = (bf16[32,256]{1,0:T(8,128)(2,1)S(1)}, bf16[32,256]{1,0:T(8,128)(2,1)S(1)}, u32[]{:S(2)}, u32[]{:S(2)}) collective-permute-start(bf16[32,256]{1,0:T(8,128)(2,1)S(1)} %get-tuple-element.23), channel_id=1, source_target_pairs={{1,0},{2,1},{3,2},{4,3},{5,4},{6,5},{7,6},{9,8},{10,9},{11,10},{12... | collective-permute-start | bytes 49160 | tf_op jit(solution)/shard_map/ppermute | solution.py:23
  49.8 3.8 %collective-permute-done.5 = bf16[32,256]{1,0:T(8,128)(2,1)S(1)} collective-permute-done((bf16[32,256]{1,0:T(8,128)(2,1)S(1)}, bf16[32,256]{1,0:T(8,128)(2,1)S(1)}, u32[]{:S(2)}, u32[]{:S(2)}) %collective-permute-start.5) | collective-permute-done | bytes 16416 | tf_op jit(solution)/shard_map/ppermute | solution.py:23
  53.6 0.8 fusion.26.e_ref
  54.3 20.4 %shard_map.112 = f32[64,256]{1,0:T(8,128)} custom-call(f32[8,65,128]{2,1,0:T(8,128)} %get-tuple-element.33.g_ref, f32[128,384]{1,0:T(8,128)} %fusion.26.e_ref, bf16[8,64,256]{2,1,0:T(8,128)(2,1)} %w_ref.1), custom_call_target="tpu_custom_call" | custom-call | tf_op jit(solution)/shard_map/pallas_call | solution.py:204
  74.8 1.5 %collective-permute-start.6 = (f32[64,256]{1,0:T(8,128)}, f32[64,256]{1,0:T(8,128)S(1)}, u32[]{:S(2)}, u32[]{:S(2)}) collective-permute-start(f32[64,256]{1,0:T(8,128)} %shard_map.112), channel_id=1, source_target_pairs={{0,8},{8,0},{16,24},{24,16},{1,9},{9,1},{17,25},{25,17},{2,10},{10... | collective-permute-start | bytes 196616 | tf_op jit(solution)/shard_map/ppermute | solution.py:67
  76.3 3.0 %collective-permute-done.6 = f32[64,256]{1,0:T(8,128)S(1)} collective-permute-done((f32[64,256]{1,0:T(8,128)}, f32[64,256]{1,0:T(8,128)S(1)}, u32[]{:S(2)}, u32[]{:S(2)}) %collective-permute-start.6) | collective-permute-done | bytes 65568 | tf_op jit(solution)/shard_map/ppermute | solution.py:67
  79.3 0.8 add.171
  80.1 1.6 %collective-permute-start.7 = (f32[64,256]{1,0:T(8,128)S(1)}, f32[64,256]{1,0:T(8,128)S(1)}, u32[]{:S(2)}, u32[]{:S(2)}) collective-permute-start(f32[64,256]{1,0:T(8,128)S(1)} %add.171), channel_id=1, source_target_pairs={{0,16},{8,24},{16,0},{24,8},{1,17},{9,25},{17,1},{25,9},{2,18},{10... | collective-permute-start | bytes 196616 | tf_op jit(solution)/shard_map/ppermute | solution.py:67
  81.7 3.1 %collective-permute-done.7 = f32[64,256]{1,0:T(8,128)S(1)} collective-permute-done((f32[64,256]{1,0:T(8,128)S(1)}, f32[64,256]{1,0:T(8,128)S(1)}, u32[]{:S(2)}, u32[]{:S(2)}) %collective-permute-start.7) | collective-permute-done | bytes 65568 | tf_op jit(solution)/shard_map/ppermute | solution.py:67
  84.8 0.6 multiply_reduce_fusion.3
  85.4 2.7 %pad_maximum_fusion.8 = f32[4]{0:T(128)S(1)} fusion(f32[1]{0:T(128)} %bitcast.16, f32[1]{0:T(128)} %bitcast.15, f32[1]{0:T(128)} %bitcast.14, f32[1]{0:T(128)} %bitcast), kind=kLoop, calls=%fused_computation.133 | loop fusion | flops 12 | bytes 32 | tf_op jit(solution)/shard_map/stack | solution.py:238
  88.1 13.8 %psum.7 = f32[4]{0:T(128)S(1)} all-reduce(f32[4]{0:T(128)S(1)} %pad_maximum_fusion.8), channel_id=1, replica_groups=mesh['comp'=4,'band'=8] {'band'}, use_global_device_ids=true, to_apply=%region_4.5 | all-reduce | flops 4 | bytes 32 | tf_op jit(solution)/shard_map/psum | solution.py:246
  101.9 0.6 fusion.68
  106.5 0.7 multiply_add_fusion
  107.2 0.3 dynamic_update_slice.3
  107.5 0.1 fusion.32
  107.6 0.1 fusion.34
  107.7 0.1 fusion.36
  107.8 0.1 fusion.38
  107.9 0.1 fusion.40
  108.0 0.1 fusion.42
  108.0 0.1 fusion.44
  108.1 0.1 fusion.46
  108.2 0.1 fusion.30
  108.3 1.9 %fusion.18 = f32[66,66,64]{1,2,0:T(8,128)S(1)} fusion(f32[64,9,1]{0,1,2:T(8,128)S(1)} %reshape.181, f32[9,66,66]{2,1,0:T(8,128)S(1)} %fusion.30), kind=kOutput, calls=%fused_computation.20 | convolution fusion | flops 30108672 | bytes 1274256 | tf_op jit(solution)/shard_map/ct,tij->cij/dot_general | solution.py:82
  110.2 1.5 %fusion.6 = f32[9,66,66]{2,0,1:T(8,128)S(1)} fusion(f32[64,9,1]{0,1,2:T(8,128)S(1)} %reshape.182, f32[66,66,64]{1,2,0:T(8,128)S(1)} %fusion.18, f32[66,66]{1,0:T(8,128)S(1)} %and_convert_fusion, f32[64]{0:T(128)S(1)} %copy-done.6), kind=kOutput, calls=%fused_computation.10 | convolution fusion | flops 30945024 | bytes 1291936 | tf_op jit(solution)/shard_map/ct,cij->tij/dot_general | solution.py:93
  111.7 0.5 slice_add_fusion
  112.2 0.7 fusion.47
  (49 shorter events, 0.4 us)
Async XLA Ops:
  2.5 8.7 %collective-permute-start.1 = (bf16[9,32,256]{2,1,0:T(8,128)(2,1)S(1)}, bf16[9,32,256]{2,1,0:T(8,128)(2,1)S(1)}, u32[]{:S(2)}, u32[]{:S(2)}) collective-permute-start(bf16[9,32,256]{2,1,0:T(8,128)(2,1)S(1)} %pad_maximum_fusion.1), channel_id=1, source_target_pairs={{1,0},{2,1},{3,2},{4,3},{5,4},{6,5},{7,6},{9,8},{10,9},{11,10},{12... | collective-permute-start | bytes 442376 | tf_op jit(solution)/shard_map/ppermute | solution.py:56
  3.9 7.3 %collective-permute-start = (bf16[9,32,256]{2,1,0:T(8,128)(2,1)S(1)}, bf16[9,32,256]{2,1,0:T(8,128)(2,1)S(1)}, u32[]{:S(2)}, u32[]{:S(2)}) collective-permute-start(bf16[9,32,256]{2,1,0:T(8,128)(2,1)S(1)} %pad_maximum_fusion), channel_id=1, source_target_pairs={{0,1},{1,2},{2,3},{3,4},{4,5},{5,6},{6,7},{8,9},{9,10},{10,11},{11... | collective-permute-start | bytes 442376 | tf_op jit(solution)/shard_map/ppermute | solution.py:55
  11.2 28.6 %copy-start.4 = (f32[64,3,3]{0,2,1:T(4,128)S(1)}, f32[64,3,3]{0,2,1:T(4,128)}, u32[]{:S(2)}) copy-start(f32[64,3,3]{0,2,1:T(4,128)} %param.13) | copy-start | bytes 6916
  11.3 28.6 %copy-start.5 = (f32[64,3,3]{0,2,1:T(4,128)S(1)}, f32[64,3,3]{0,2,1:T(4,128)}, u32[]{:S(2)}) copy-start(f32[64,3,3]{0,2,1:T(4,128)} %param.15) | copy-start | bytes 6916
  12.8 72.0 %copy-start = (f32[64,256]{1,0:T(8,128)S(1)}, f32[64,256]{1,0:T(8,128)}, u32[]{:S(2)}) copy-start(f32[64,256]{1,0:T(8,128)} %param.10) | copy-start | bytes 196612
  12.8 72.0 %copy-start.2 = (f32[64,256]{1,0:T(8,128)S(1)}, f32[64,256]{1,0:T(8,128)}, u32[]{:S(2)}) copy-start(f32[64,256]{1,0:T(8,128)} %param.9) | copy-start | bytes 196612
  12.8 75.3 %copy-start.1 = (f32[64,256]{1,0:T(8,128)S(1)}, f32[64,256]{1,0:T(8,128)}, u32[]{:S(2)}) copy-start(f32[64,256]{1,0:T(8,128)} %param.8) | copy-start | bytes 196612
  36.7 5.3 %collective-permute-start.2 = (f32[64,256]{1,0:T(8,128)S(1)}, f32[64,256]{1,0:T(8,128)S(1)}, u32[]{:S(2)}, u32[]{:S(2)}) collective-permute-start(f32[64,256]{1,0:T(8,128)S(1)} %pad_maximum_fusion.3), channel_id=1, source_target_pairs={{0,8},{8,0},{16,24},{24,16},{1,9},{9,1},{17,25},{25,17},{2,10},{10... | collective-permute-start | bytes 196616 | tf_op jit(solution)/shard_map/ppermute | solution.py:67
  42.0 4.9 %collective-permute-start.3 = (f32[64,256]{1,0:T(8,128)S(1)}, f32[64,256]{1,0:T(8,128)S(1)}, u32[]{:S(2)}, u32[]{:S(2)}) collective-permute-start(f32[64,256]{1,0:T(8,128)S(1)} %fusion.64), channel_id=1, source_target_pairs={{0,16},{8,24},{16,0},{24,8},{1,17},{9,25},{17,1},{25,9},{2,18},{10... | collective-permute-start | bytes 196616 | tf_op jit(solution)/shard_map/ppermute | solution.py:67
  47.0 2.8 %collective-permute-start.4 = (bf16[32,256]{1,0:T(8,128)(2,1)S(1)}, bf16[32,256]{1,0:T(8,128)(2,1)S(1)}, u32[]{:S(2)}, u32[]{:S(2)}) collective-permute-start(bf16[32,256]{1,0:T(8,128)(2,1)S(1)} %get-tuple-element.22), channel_id=1, source_target_pairs={{0,1},{1,2},{2,3},{3,4},{4,5},{5,6},{6,7},{8,9},{9,10},{10,11},{11... | collective-permute-start | bytes 49160 | tf_op jit(solution)/shard_map/ppermute | solution.py:22
  48.5 5.1 %collective-permute-start.5 = (bf16[32,256]{1,0:T(8,128)(2,1)S(1)}, bf16[32,256]{1,0:T(8,128)(2,1)S(1)}, u32[]{:S(2)}, u32[]{:S(2)}) collective-permute-start(bf16[32,256]{1,0:T(8,128)(2,1)S(1)} %get-tuple-element.23), channel_id=1, source_target_pairs={{1,0},{2,1},{3,2},{4,3},{5,4},{6,5},{7,6},{9,8},{10,9},{11,10},{12... | collective-permute-start | bytes 49160 | tf_op jit(solution)/shard_map/ppermute | solution.py:23
  74.8 4.5 %collective-permute-start.6 = (f32[64,256]{1,0:T(8,128)}, f32[64,256]{1,0:T(8,128)S(1)}, u32[]{:S(2)}, u32[]{:S(2)}) collective-permute-start(f32[64,256]{1,0:T(8,128)} %shard_map.112), channel_id=1, source_target_pairs={{0,8},{8,0},{16,24},{24,16},{1,9},{9,1},{17,25},{25,17},{2,10},{10... | collective-permute-start | bytes 196616 | tf_op jit(solution)/shard_map/ppermute | solution.py:67
  80.1 4.7 %collective-permute-start.7 = (f32[64,256]{1,0:T(8,128)S(1)}, f32[64,256]{1,0:T(8,128)S(1)}, u32[]{:S(2)}, u32[]{:S(2)}) collective-permute-start(f32[64,256]{1,0:T(8,128)S(1)} %add.171), channel_id=1, source_target_pairs={{0,16},{8,24},{16,0},{24,8},{1,17},{9,25},{17,1},{25,9},{2,18},{10... | collective-permute-start | bytes 196616 | tf_op jit(solution)/shard_map/ppermute | solution.py:67
  106.5 3.7 %copy-start.6 = (f32[64]{0:T(128)S(1)}, f32[64]{0:T(128)}, u32[]{:S(2)}) copy-start(f32[64]{0:T(128)} %param.14) | copy-start | bytes 772
  107.2 4.6 %copy-start.3 = (f32[64,256]{1,0:T(8,128)}, f32[64,256]{1,0:T(8,128)S(1)}, u32[]{:S(2)}) copy-start(f32[64,256]{1,0:T(8,128)S(1)} %get-tuple-element.19) | copy-start | bytes 196612

commit v6 on v5

--- a/solution.py
+++ b/solution.py
@@ -182,19 +182,38 @@
     return jnp.concatenate([out[n * rows : (n + 1) * rows] for n in range(blocks)], axis=1)
 
 
-def _back_body(g_ref, e_ref, w_ref, o_ref, shifted_ref, *, span, rows, blocks):
-    k = pl.program_id(0)
-
-    @pl.when(k == 0)
-    def _():
-        o_ref[...] = jnp.zeros_like(o_ref)
-        _shift_rows(e_ref, shifted_ref)
-
-    acc = _sweep(g_ref, shifted_ref, _band(span), span, rows, blocks)
-    for n in range(blocks):
-        cols = slice(n * LANES, (n + 1) * LANES)
-        w = w_ref[0, :, cols].astype(jnp.float32)
-        o_ref[:, cols] += w * acc[n * rows : (n + 1) * rows]
+def _back_body(g_ref, e_ref, w_ref, o_ref, shifted_ref, acc_ref, *, span, rows, blocks):
+    nk = g_ref.shape[0]
+    _shift_rows(e_ref, shifted_ref)
+    acc_ref[...] = jnp.zeros_like(acc_ref)
+    valid = _band(span)
+
+    def step(taps, r, base):
+        t = jnp.concatenate([_toeplitz(taps[k, r : r + 1], valid) for k in range(nk)], axis=1)
+        lhs = _lhs(shifted_ref, r, base, rows, blocks)
+        acc_ref[...] += jnp.dot(lhs, t, preferred_element_type=jnp.float32)
+
+    full = (span - 1) // GROUP
+
+    def group(q, carry):
+        base = pl.multiple_of(q * GROUP, GROUP)
+        taps = g_ref[:, pl.ds(base, GROUP), :]
+        for r in range(GROUP):
+            step(taps, r, base)
+        return carry
+
+    lax.fori_loop(0, full, group, 0)
+    base = GROUP * full
+    taps = g_ref[:, pl.ds(base, span - base), :]
+    for r in range(span - base):
+        step(taps, r, base)
+    total = jnp.zeros(o_ref.shape, jnp.float32)
+    for k in range(nk):
+        back = jnp.concatenate(
+            [acc_ref[n * rows : (n + 1) * rows, k * LANES : (k + 1) * LANES] for n in range(blocks)], axis=1
+        )
+        total = total + w_ref[k].astype(jnp.float32) * back
+    o_ref[...] = total
 
 
 def back_weighted(g, e, w):
@@ -203,16 +222,11 @@
     blocks = width // LANES
     return pl.pallas_call(
         functools.partial(_back_body, span=span, rows=rows, blocks=blocks),
-        grid=(nk,),
-        in_specs=[
-            pl.BlockSpec((1, span, LANES), lambda k: (k, 0, 0)),
-            pl.BlockSpec(e.shape, lambda k: (0, 0)),
-            pl.BlockSpec((1, rows, width), lambda k: (k, 0, 0)),
+        out_shape=jax.ShapeDtypeStruct((rows, width), jnp.float32),
+        scratch_shapes=[
+            pltpu.VMEM((GROUP,) + e.shape, jnp.bfloat16),
+            pltpu.VMEM((rows * blocks, nk * LANES), jnp.float32),
         ],
-        out_specs=pl.BlockSpec((rows, width), lambda k: (0, 0)),
-        out_shape=jax.ShapeDtypeStruct((rows, width), jnp.float32),
-        scratch_shapes=[pltpu.VMEM((GROUP,) + e.shape, jnp.bfloat16)],
-        compiler_params=pltpu.CompilerParams(dimension_semantics=("arbitrary",)),
     )(g, e, w)
 
 

time: 113 us -> 101 us (0.89)
  Pallas kernels: 43.6 us -> 30.9 us
    pallas_call x1, Pallas kernels: 20.4 us -> 7.8 us  [back_weighted(): pl.pallas_call(functools.partial(_back_body, span=span, rows=rows, blocks...]
where the time goes in v6:
time: 101 us; the launch traced here: 100 us
  Pallas kernels  30.9 us (31%)
  starting transfers between devices  15.8 us (16%)
  waiting for transfers between devices  14.3 us (14%)
  blocking collectives  13.8 us (14%)
  other arithmetic  11.2 us (11%)
  local copies, waits for them, and re-layouts  5.91 us (6%)
  between operations  4.94 us (5%)
  matrix products  3.38 us (3%)
    pallas_call x1, Pallas kernels, blur(): pl.pallas_call(functools.partial(_blur_body, span=span, rows=rows, blocks...  23.1 us
    psum x1, blocking collectives, per_device(): old, product, cross, square = lax.psum(sums, 'band')  13.8 us
    ppermute x4, waiting for transfers between devices, pair_sum(): lax.ppermute(value, axis, [(i, i ^ step) for i in range(count)])  10.5 us
    ppermute x4, starting transfers between devices, pair_sum(): lax.ppermute(value, axis, [(i, i ^ step) for i in range(count)])  8.69 us
    pallas_call x1, Pallas kernels, back_weighted(): pl.pallas_call(functools.partial(_back_body, span=span, rows=rows, blocks...  7.8 us
    ppermute x1, waiting for transfers between devices, with_halo(): after = lax.ppermute(first, axis, down)  3.79 us
    ppermute x1, starting transfers between devices, band_halo(): before = lax.ppermute(last, 'band', up)  3.04 us
    another operation x1, other arithmetic, per_device(): jnp.stack([jnp.sum(residual * residual), jnp.sum(direction * curved), jnp...  2.66 us
  transfers between devices with their start and end apart: 8, of which 5 were waited for; matrix products, arithmetic and copies ran while one was open for 4% of the time, Pallas kernels for 0%

profile of v6, /device:TPU:0, one launch (start us, length us, event | category | flops | bytes accessed | tf_op | source)
XLA Modules:
  0.0 100.3 jit_solution(16436686494079585082)
XLA Ops:
  0.6 0.8 fusion.52
  1.5 1.0 multiply_convert_fusion
  2.5 1.3 %collective-permute-start.1 = (bf16[9,32,256]{2,1,0:T(8,128)(2,1)S(1)}, bf16[9,32,256]{2,1,0:T(8,128)(2,1)S(1)}, u32[]{:S(2)}, u32[]{:S(2)}) collective-permute-start(bf16[9,32,256]{2,1,0:T(8,128)(2,1)S(1)} %pad_maximum_fusion.1), channel_id=1, source_target_pairs={{1,0},{2,1},{3,2},{4,3},{5,4},{6,5},{7,6},{9,8},{10,9},{11,10},{12... | collective-permute-start | bytes 442376 | tf_op jit(solution)/shard_map/ppermute | solution.py:56
  3.9 3.0 %collective-permute-start = (bf16[9,32,256]{2,1,0:T(8,128)(2,1)S(1)}, bf16[9,32,256]{2,1,0:T(8,128)(2,1)S(1)}, u32[]{:S(2)}, u32[]{:S(2)}) collective-permute-start(bf16[9,32,256]{2,1,0:T(8,128)(2,1)S(1)} %pad_maximum_fusion), channel_id=1, source_target_pairs={{0,1},{1,2},{2,3},{3,4},{4,5},{5,6},{6,7},{8,9},{9,10},{10,11},{11... | collective-permute-start | bytes 442376 | tf_op jit(solution)/shard_map/ppermute | solution.py:55
  7.0 1.1 %copy.12 = bf16[8,65,65]{1,0,2:T(8,128)(2,1)S(1)} copy(bf16[8,65,65]{2,0,1:T(8,128)(2,1)} %param.11) | data formatting | bytes 135200 | tf_op args[3]
  8.1 0.1 rev.3
  8.3 0.8 gather_fusion
  9.0 0.2 copy.13
  9.3 0.8 gather_fusion.1
  10.1 0.2 copy.15
  10.3 0.9 select_bitcast_fusion
  11.3 1.5 %fusion.17.x_ref = f32[8,128,384]{2,1,0:T(8,128)} fusion(bf16[8,32,256]{2,1,0:T(8,128)(2,1)S(1)} %slice.169, bf16[8,64,256]{2,1,0:T(8,128)(2,1)S(1)} %multiply_convert_fusion, bf16[8,32,256]{2,1,0:T(8,128)(2,1)S(1)} %slice.167), kind=kLoop, calls=%fused_computation.19 | loop fusion | flops 4718592 | bytes 2097152 | tf_op jit(solution)/shard_map/jit(_pad)/pad | solution.py:244
  12.8 23.1 %shard_map.111 = f32[128,128]{1,0:T(8,128)} custom-call(f32[8,65,128]{2,1,0:T(8,128)} %get-tuple-element.32.g_ref, f32[8,128,384]{2,1,0:T(8,128)} %fusion.17.x_ref), custom_call_target="tpu_custom_call" | custom-call | tf_op jit(solution)/shard_map/pallas_call | solution.py:170
  35.9 0.8 fusion.66
  36.7 3.0 %collective-permute-start.2 = (f32[64,256]{1,0:T(8,128)S(1)}, f32[64,256]{1,0:T(8,128)S(1)}, u32[]{:S(2)}, u32[]{:S(2)}) collective-permute-start(f32[64,256]{1,0:T(8,128)S(1)} %pad_maximum_fusion.3), channel_id=1, source_target_pairs={{0,8},{8,0},{16,24},{24,16},{1,9},{9,1},{17,25},{25,17},{2,10},{10... | collective-permute-start | bytes 196616 | tf_op jit(solution)/shard_map/ppermute | solution.py:67
  39.8 0.1 and_convert_fusion
  39.9 2.1 %collective-permute-done.2 = f32[64,256]{1,0:T(8,128)S(1)} collective-permute-done((f32[64,256]{1,0:T(8,128)S(1)}, f32[64,256]{1,0:T(8,128)S(1)}, u32[]{:S(2)}, u32[]{:S(2)}) %collective-permute-start.2) | collective-permute-done | bytes 65568 | tf_op jit(solution)/shard_map/ppermute | solution.py:67
  42.0 2.6 %collective-permute-start.3 = (f32[64,256]{1,0:T(8,128)S(1)}, f32[64,256]{1,0:T(8,128)S(1)}, u32[]{:S(2)}, u32[]{:S(2)}) collective-permute-start(f32[64,256]{1,0:T(8,128)S(1)} %fusion.64), channel_id=1, source_target_pairs={{0,16},{8,24},{16,0},{24,8},{1,17},{9,25},{17,1},{25,9},{2,18},{10... | collective-permute-start | bytes 196616 | tf_op jit(solution)/shard_map/ppermute | solution.py:67
  44.6 2.4 %collective-permute-done.3 = f32[64,256]{1,0:T(8,128)S(1)} collective-permute-done((f32[64,256]{1,0:T(8,128)S(1)}, f32[64,256]{1,0:T(8,128)S(1)}, u32[]{:S(2)}, u32[]{:S(2)}) %collective-permute-start.3) | collective-permute-done | bytes 65568 | tf_op jit(solution)/shard_map/ppermute | solution.py:67
  47.0 1.4 %collective-permute-start.4 = (bf16[32,256]{1,0:T(8,128)(2,1)S(1)}, bf16[32,256]{1,0:T(8,128)(2,1)S(1)}, u32[]{:S(2)}, u32[]{:S(2)}) collective-permute-start(bf16[32,256]{1,0:T(8,128)(2,1)S(1)} %get-tuple-element.22), channel_id=1, source_target_pairs={{0,1},{1,2},{2,3},{3,4},{4,5},{5,6},{6,7},{8,9},{9,10},{10,11},{11... | collective-permute-start | bytes 49160 | tf_op jit(solution)/shard_map/ppermute | solution.py:22
  48.5 1.3 %collective-permute-start.5 = (bf16[32,256]{1,0:T(8,128)(2,1)S(1)}, bf16[32,256]{1,0:T(8,128)(2,1)S(1)}, u32[]{:S(2)}, u32[]{:S(2)}) collective-permute-start(bf16[32,256]{1,0:T(8,128)(2,1)S(1)} %get-tuple-element.23), channel_id=1, source_target_pairs={{1,0},{2,1},{3,2},{4,3},{5,4},{6,5},{7,6},{9,8},{10,9},{11,10},{12... | collective-permute-start | bytes 49160 | tf_op jit(solution)/shard_map/ppermute | solution.py:23
  49.8 3.8 %collective-permute-done.5 = bf16[32,256]{1,0:T(8,128)(2,1)S(1)} collective-permute-done((bf16[32,256]{1,0:T(8,128)(2,1)S(1)}, bf16[32,256]{1,0:T(8,128)(2,1)S(1)}, u32[]{:S(2)}, u32[]{:S(2)}) %collective-permute-start.5) | collective-permute-done | bytes 16416 | tf_op jit(solution)/shard_map/ppermute | solution.py:23
  53.6 0.8 fusion.26.e_ref
  54.3 7.8 %shard_map.112 = f32[64,256]{1,0:T(8,128)} custom-call(f32[8,65,128]{2,1,0:T(8,128)} %get-tuple-element.33.g_ref, f32[128,384]{1,0:T(8,128)} %fusion.26.e_ref, bf16[8,64,256]{2,1,0:T(8,128)(2,1)} %w_ref.1), custom_call_target="tpu_custom_call" | custom-call | tf_op jit(solution)/shard_map/pallas_call | solution.py:223
  62.1 1.5 %collective-permute-start.6 = (f32[64,256]{1,0:T(8,128)}, f32[64,256]{1,0:T(8,128)S(1)}, u32[]{:S(2)}, u32[]{:S(2)}) collective-permute-start(f32[64,256]{1,0:T(8,128)} %shard_map.112), channel_id=1, source_target_pairs={{0,8},{8,0},{16,24},{24,16},{1,9},{9,1},{17,25},{25,17},{2,10},{10... | collective-permute-start | bytes 196616 | tf_op jit(solution)/shard_map/ppermute | solution.py:67
  63.6 3.0 %collective-permute-done.6 = f32[64,256]{1,0:T(8,128)S(1)} collective-permute-done((f32[64,256]{1,0:T(8,128)}, f32[64,256]{1,0:T(8,128)S(1)}, u32[]{:S(2)}, u32[]{:S(2)}) %collective-permute-start.6) | collective-permute-done | bytes 65568 | tf_op jit(solution)/shard_map/ppermute | solution.py:67
  66.6 0.8 add.171
  67.5 1.6 %collective-permute-start.7 = (f32[64,256]{1,0:T(8,128)S(1)}, f32[64,256]{1,0:T(8,128)S(1)}, u32[]{:S(2)}, u32[]{:S(2)}) collective-permute-start(f32[64,256]{1,0:T(8,128)S(1)} %add.171), channel_id=1, source_target_pairs={{0,16},{8,24},{16,0},{24,8},{1,17},{9,25},{17,1},{25,9},{2,18},{10... | collective-permute-start | bytes 196616 | tf_op jit(solution)/shard_map/ppermute | solution.py:67
  69.1 3.1 %collective-permute-done.7 = f32[64,256]{1,0:T(8,128)S(1)} collective-permute-done((f32[64,256]{1,0:T(8,128)S(1)}, f32[64,256]{1,0:T(8,128)S(1)}, u32[]{:S(2)}, u32[]{:S(2)}) %collective-permute-start.7) | collective-permute-done | bytes 65568 | tf_op jit(solution)/shard_map/ppermute | solution.py:67
  72.1 0.6 multiply_reduce_fusion.3
  72.8 2.7 %pad_maximum_fusion.8 = f32[4]{0:T(128)S(1)} fusion(f32[1]{0:T(128)} %bitcast.16, f32[1]{0:T(128)} %bitcast.15, f32[1]{0:T(128)} %bitcast.14, f32[1]{0:T(128)} %bitcast), kind=kLoop, calls=%fused_computation.133 | loop fusion | flops 12 | bytes 32 | tf_op jit(solution)/shard_map/stack | solution.py:252
  75.5 13.8 %psum.7 = f32[4]{0:T(128)S(1)} all-reduce(f32[4]{0:T(128)S(1)} %pad_maximum_fusion.8), channel_id=1, replica_groups=mesh['comp'=4,'band'=8] {'band'}, use_global_device_ids=true, to_apply=%region_4.5 | all-reduce | flops 4 | bytes 32 | tf_op jit(solution)/shard_map/psum | solution.py:260
  89.2 0.6 fusion.68
  93.8 0.7 multiply_add_fusion
  94.5 0.3 dynamic_update_slice.3
  94.9 0.1 fusion.32
  95.0 0.1 fusion.34
  95.0 0.1 fusion.36
  95.1 0.1 fusion.38
  95.2 0.1 fusion.40
  95.3 0.1 fusion.42
  95.4 0.1 fusion.44
  95.5 0.1 fusion.46
  95.6 0.1 fusion.30
  95.7 1.9 %fusion.18 = f32[66,66,64]{1,2,0:T(8,128)S(1)} fusion(f32[64,9,1]{0,1,2:T(8,128)S(1)} %reshape.181, f32[9,66,66]{2,1,0:T(8,128)S(1)} %fusion.30), kind=kOutput, calls=%fused_computation.20 | convolution fusion | flops 30108672 | bytes 1274256 | tf_op jit(solution)/shard_map/ct,tij->cij/dot_general | solution.py:82
  97.6 1.5 %fusion.6 = f32[9,66,66]{2,0,1:T(8,128)S(1)} fusion(f32[64,9,1]{0,1,2:T(8,128)S(1)} %reshape.182, f32[66,66,64]{1,2,0:T(8,128)S(1)} %fusion.18, f32[66,66]{1,0:T(8,128)S(1)} %and_convert_fusion, f32[64]{0:T(128)S(1)} %copy-done.6), kind=kOutput, calls=%fused_computation.10 | convolution fusion | flops 30945024 | bytes 1291936 | tf_op jit(solution)/shard_map/ct,cij->tij/dot_general | solution.py:93
  99.1 0.5 slice_add_fusion
  99.6 0.7 fusion.47
  (49 shorter events, 0.4 us)
Async XLA Ops:
  2.5 8.7 %collective-permute-start.1 = (bf16[9,32,256]{2,1,0:T(8,128)(2,1)S(1)}, bf16[9,32,256]{2,1,0:T(8,128)(2,1)S(1)}, u32[]{:S(2)}, u32[]{:S(2)}) collective-permute-start(bf16[9,32,256]{2,1,0:T(8,128)(2,1)S(1)} %pad_maximum_fusion.1), channel_id=1, source_target_pairs={{1,0},{2,1},{3,2},{4,3},{5,4},{6,5},{7,6},{9,8},{10,9},{11,10},{12... | collective-permute-start | bytes 442376 | tf_op jit(solution)/shard_map/ppermute | solution.py:56
  3.9 7.3 %collective-permute-start = (bf16[9,32,256]{2,1,0:T(8,128)(2,1)S(1)}, bf16[9,32,256]{2,1,0:T(8,128)(2,1)S(1)}, u32[]{:S(2)}, u32[]{:S(2)}) collective-permute-start(bf16[9,32,256]{2,1,0:T(8,128)(2,1)S(1)} %pad_maximum_fusion), channel_id=1, source_target_pairs={{0,1},{1,2},{2,3},{3,4},{4,5},{5,6},{6,7},{8,9},{9,10},{10,11},{11... | collective-permute-start | bytes 442376 | tf_op jit(solution)/shard_map/ppermute | solution.py:55
  11.2 28.6 %copy-start.4 = (f32[64,3,3]{0,2,1:T(4,128)S(1)}, f32[64,3,3]{0,2,1:T(4,128)}, u32[]{:S(2)}) copy-start(f32[64,3,3]{0,2,1:T(4,128)} %param.13) | copy-start | bytes 6916
  11.3 28.6 %copy-start.5 = (f32[64,3,3]{0,2,1:T(4,128)S(1)}, f32[64,3,3]{0,2,1:T(4,128)}, u32[]{:S(2)}) copy-start(f32[64,3,3]{0,2,1:T(4,128)} %param.15) | copy-start | bytes 6916
  12.8 59.4 %copy-start = (f32[64,256]{1,0:T(8,128)S(1)}, f32[64,256]{1,0:T(8,128)}, u32[]{:S(2)}) copy-start(f32[64,256]{1,0:T(8,128)} %param.10) | copy-start | bytes 196612
  12.8 59.4 %copy-start.2 = (f32[64,256]{1,0:T(8,128)S(1)}, f32[64,256]{1,0:T(8,128)}, u32[]{:S(2)}) copy-start(f32[64,256]{1,0:T(8,128)} %param.9) | copy-start | bytes 196612
  12.8 62.7 %copy-start.1 = (f32[64,256]{1,0:T(8,128)S(1)}, f32[64,256]{1,0:T(8,128)}, u32[]{:S(2)}) copy-start(f32[64,256]{1,0:T(8,128)} %param.8) | copy-start | bytes 196612
  36.7 5.3 %collective-permute-start.2 = (f32[64,256]{1,0:T(8,128)S(1)}, f32[64,256]{1,0:T(8,128)S(1)}, u32[]{:S(2)}, u32[]{:S(2)}) collective-permute-start(f32[64,256]{1,0:T(8,128)S(1)} %pad_maximum_fusion.3), channel_id=1, source_target_pairs={{0,8},{8,0},{16,24},{24,16},{1,9},{9,1},{17,25},{25,17},{2,10},{10... | collective-permute-start | bytes 196616 | tf_op jit(solution)/shard_map/ppermute | solution.py:67
  42.0 4.9 %collective-permute-start.3 = (f32[64,256]{1,0:T(8,128)S(1)}, f32[64,256]{1,0:T(8,128)S(1)}, u32[]{:S(2)}, u32[]{:S(2)}) collective-permute-start(f32[64,256]{1,0:T(8,128)S(1)} %fusion.64), channel_id=1, source_target_pairs={{0,16},{8,24},{16,0},{24,8},{1,17},{9,25},{17,1},{25,9},{2,18},{10... | collective-permute-start | bytes 196616 | tf_op jit(solution)/shard_map/ppermute | solution.py:67
  47.0 2.8 %collective-permute-start.4 = (bf16[32,256]{1,0:T(8,128)(2,1)S(1)}, bf16[32,256]{1,0:T(8,128)(2,1)S(1)}, u32[]{:S(2)}, u32[]{:S(2)}) collective-permute-start(bf16[32,256]{1,0:T(8,128)(2,1)S(1)} %get-tuple-element.22), channel_id=1, source_target_pairs={{0,1},{1,2},{2,3},{3,4},{4,5},{5,6},{6,7},{8,9},{9,10},{10,11},{11... | collective-permute-start | bytes 49160 | tf_op jit(solution)/shard_map/ppermute | solution.py:22
  48.5 5.1 %collective-permute-start.5 = (bf16[32,256]{1,0:T(8,128)(2,1)S(1)}, bf16[32,256]{1,0:T(8,128)(2,1)S(1)}, u32[]{:S(2)}, u32[]{:S(2)}) collective-permute-start(bf16[32,256]{1,0:T(8,128)(2,1)S(1)} %get-tuple-element.23), channel_id=1, source_target_pairs={{1,0},{2,1},{3,2},{4,3},{5,4},{6,5},{7,6},{9,8},{10,9},{11,10},{12... | collective-permute-start | bytes 49160 | tf_op jit(solution)/shard_map/ppermute | solution.py:23
  62.1 4.5 %collective-permute-start.6 = (f32[64,256]{1,0:T(8,128)}, f32[64,256]{1,0:T(8,128)S(1)}, u32[]{:S(2)}, u32[]{:S(2)}) collective-permute-start(f32[64,256]{1,0:T(8,128)} %shard_map.112), channel_id=1, source_target_pairs={{0,8},{8,0},{16,24},{24,16},{1,9},{9,1},{17,25},{25,17},{2,10},{10... | collective-permute-start | bytes 196616 | tf_op jit(solution)/shard_map/ppermute | solution.py:67
  67.5 4.7 %collective-permute-start.7 = (f32[64,256]{1,0:T(8,128)S(1)}, f32[64,256]{1,0:T(8,128)S(1)}, u32[]{:S(2)}, u32[]{:S(2)}) collective-permute-start(f32[64,256]{1,0:T(8,128)S(1)} %add.171), channel_id=1, source_target_pairs={{0,16},{8,24},{16,0},{24,8},{1,17},{9,25},{17,1},{25,9},{2,18},{10... | collective-permute-start | bytes 196616 | tf_op jit(solution)/shard_map/ppermute | solution.py:67
  93.8 3.7 %copy-start.6 = (f32[64]{0:T(128)S(1)}, f32[64]{0:T(128)}, u32[]{:S(2)}) copy-start(f32[64]{0:T(128)} %param.14) | copy-start | bytes 772
  94.5 4.6 %copy-start.3 = (f32[64,256]{1,0:T(8,128)}, f32[64,256]{1,0:T(8,128)S(1)}, u32[]{:S(2)}) copy-start(f32[64,256]{1,0:T(8,128)S(1)} %get-tuple-element.19) | copy-start | bytes 196612

commit v7 on v6

--- a/solution.py
+++ b/solution.py
@@ -151,6 +151,35 @@
     return acc
 
 
+def _blur_sweep(g_ref, shifted_ref, valid, span, rows, blocks):
+    tall = rows + GROUP
+    full = (span - 1) // GROUP
+
+    def pair(taps, r, base, acc):
+        t = jnp.concatenate([_toeplitz(taps[r : r + 1], valid), _toeplitz(taps[r + 1 : r + 2], valid)], axis=1)
+        z = jnp.dot(_lhs(shifted_ref, r, base, tall, blocks), t, preferred_element_type=jnp.float32)
+        pieces = [
+            z[n * tall : n * tall + rows, :LANES] + z[n * tall + 1 : n * tall + 1 + rows, LANES:]
+            for n in range(blocks)
+        ]
+        return acc + jnp.concatenate(pieces, axis=0)
+
+    def group(q, acc):
+        base = pl.multiple_of(q * GROUP, GROUP)
+        taps = g_ref[0, pl.ds(base, GROUP), :]
+        for r in range(0, GROUP, 2):
+            acc = pair(taps, r, base, acc)
+        return acc
+
+    acc = lax.fori_loop(0, full, group, jnp.zeros((rows * blocks, LANES), jnp.float32))
+    base = GROUP * full
+    taps = g_ref[0, pl.ds(base, span - base), :]
+    for r in range(span - base):
+        t = _toeplitz(taps[r : r + 1], valid)
+        acc = acc + jnp.dot(_lhs(shifted_ref, r, base, rows, blocks), t, preferred_element_type=jnp.float32)
+    return acc
+
+
 def _blur_body(g_ref, x_ref, o_ref, shifted_ref, *, span, rows, blocks):
     k = pl.program_id(0)
 
@@ -159,7 +188,7 @@
         o_ref[...] = jnp.zeros_like(o_ref)
 
     _shift_rows(x_ref.at[0], shifted_ref)
-    acc = _sweep(g_ref, shifted_ref, _band(span), span, rows, blocks)
+    acc = _blur_sweep(g_ref, shifted_ref, _band(span), span, rows, blocks)
     o_ref[...] += acc
 
 

time: 101 us -> 98.3 us (0.973)
  Pallas kernels: 30.9 us -> 28.4 us
    pallas_call x1, Pallas kernels: 23.1 us -> 20.6 us  [blur(): pl.pallas_call(functools.partial(_blur_body, span=span, rows=rows, blocks...]
where the time goes in v7:
time: 98.3 us; the launch traced here: 97.7 us
  Pallas kernels  28.4 us (29%)
  starting transfers between devices  15.7 us (16%)
  waiting for transfers between devices  14.4 us (15%)
  blocking collectives  13.8 us (14%)
  other arithmetic  11.2 us (11%)
  local copies, waits for them, and re-layouts  5.91 us (6%)
  between operations  4.94 us (5%)
  matrix products  3.38 us (3%)
    pallas_call x1, Pallas kernels, blur(): pl.pallas_call(functools.partial(_blur_body, span=span, rows=rows, blocks...  20.6 us
    psum x1, blocking collectives, per_device(): old, product, cross, square = lax.psum(sums, 'band')  13.8 us
    ppermute x4, waiting for transfers between devices, pair_sum(): lax.ppermute(value, axis, [(i, i ^ step) for i in range(count)])  10.6 us
    ppermute x4, starting transfers between devices, pair_sum(): lax.ppermute(value, axis, [(i, i ^ step) for i in range(count)])  8.67 us
    pallas_call x1, Pallas kernels, back_weighted(): pl.pallas_call(functools.partial(_back_body, span=span, rows=rows, blocks...  7.8 us
    ppermute x1, waiting for transfers between devices, with_halo(): after = lax.ppermute(first, axis, down)  3.79 us
    ppermute x1, starting transfers between devices, band_halo(): before = lax.ppermute(last, 'band', up)  3.04 us
    another operation x1, other arithmetic, per_device(): jnp.stack([jnp.sum(residual * residual), jnp.sum(direction * curved), jnp...  2.66 us
  transfers between devices with their start and end apart: 8, of which 5 were waited for; matrix products, arithmetic and copies ran while one was open for 4% of the time, Pallas kernels for 0%

profile of v7, /device:TPU:0, one launch (start us, length us, event | category | flops | bytes accessed | tf_op | source)
XLA Modules:
  0.0 97.7 jit_solution(17296139119990865342)
XLA Ops:
  0.6 0.8 fusion.52
  1.5 1.0 %multiply_convert_fusion = bf16[8,64,256]{2,1,0:T(8,128)(2,1)S(1)} fusion(bf16[8,64,256]{2,1,0:T(8,128)(2,1)} %w_ref.1, f32[64,256]{1,0:T(8,128)} %param.10), kind=kLoop, calls=%fused_computation.22 | loop fusion | flops 393216 | bytes 589824 | tf_op jit(solution)/shard_map/convert_element_type | solution.py:268
  2.5 1.3 %collective-permute-start.1 = (bf16[9,32,256]{2,1,0:T(8,128)(2,1)S(1)}, bf16[9,32,256]{2,1,0:T(8,128)(2,1)S(1)}, u32[]{:S(2)}, u32[]{:S(2)}) collective-permute-start(bf16[9,32,256]{2,1,0:T(8,128)(2,1)S(1)} %pad_maximum_fusion.1), channel_id=1, source_target_pairs={{1,0},{2,1},{3,2},{4,3},{5,4},{6,5},{7,6},{9,8},{10,9},{11,10},{12... | collective-permute-start | bytes 442376 | tf_op jit(solution)/shard_map/ppermute | solution.py:56
  3.9 3.0 %collective-permute-start = (bf16[9,32,256]{2,1,0:T(8,128)(2,1)S(1)}, bf16[9,32,256]{2,1,0:T(8,128)(2,1)S(1)}, u32[]{:S(2)}, u32[]{:S(2)}) collective-permute-start(bf16[9,32,256]{2,1,0:T(8,128)(2,1)S(1)} %pad_maximum_fusion), channel_id=1, source_target_pairs={{0,1},{1,2},{2,3},{3,4},{4,5},{5,6},{6,7},{8,9},{9,10},{10,11},{11... | collective-permute-start | bytes 442376 | tf_op jit(solution)/shard_map/ppermute | solution.py:55
  7.0 1.1 %copy.12 = bf16[8,65,65]{1,0,2:T(8,128)(2,1)S(1)} copy(bf16[8,65,65]{2,0,1:T(8,128)(2,1)} %param.11) | data formatting | bytes 135200 | tf_op args[3]
  8.1 0.1 rev.3
  8.3 0.8 gather_fusion
  9.0 0.2 copy.13
  9.3 0.8 gather_fusion.1
  10.1 0.2 copy.15
  10.3 0.9 select_bitcast_fusion
  11.3 1.5 %fusion.17.x_ref = f32[8,128,384]{2,1,0:T(8,128)} fusion(bf16[8,32,256]{2,1,0:T(8,128)(2,1)S(1)} %slice.169, bf16[8,64,256]{2,1,0:T(8,128)(2,1)S(1)} %multiply_convert_fusion, bf16[8,32,256]{2,1,0:T(8,128)(2,1)S(1)} %slice.167), kind=kLoop, calls=%fused_computation.19 | loop fusion | flops 4718592 | bytes 2097152 | tf_op jit(solution)/shard_map/jit(_pad)/pad | solution.py:273
  12.8 20.6 %shard_map.111 = f32[128,128]{1,0:T(8,128)} custom-call(f32[8,65,128]{2,1,0:T(8,128)} %get-tuple-element.32.g_ref, f32[8,128,384]{2,1,0:T(8,128)} %fusion.17.x_ref), custom_call_target="tpu_custom_call" | custom-call | tf_op jit(solution)/shard_map/pallas_call | solution.py:199
  33.4 0.8 fusion.66
  34.2 3.0 %collective-permute-start.2 = (f32[64,256]{1,0:T(8,128)S(1)}, f32[64,256]{1,0:T(8,128)S(1)}, u32[]{:S(2)}, u32[]{:S(2)}) collective-permute-start(f32[64,256]{1,0:T(8,128)S(1)} %pad_maximum_fusion.3), channel_id=1, source_target_pairs={{0,8},{8,0},{16,24},{24,16},{1,9},{9,1},{17,25},{25,17},{2,10},{10... | collective-permute-start | bytes 196616 | tf_op jit(solution)/shard_map/ppermute | solution.py:67
  37.2 0.1 and_convert_fusion
  37.3 2.2 %collective-permute-done.2 = f32[64,256]{1,0:T(8,128)S(1)} collective-permute-done((f32[64,256]{1,0:T(8,128)S(1)}, f32[64,256]{1,0:T(8,128)S(1)}, u32[]{:S(2)}, u32[]{:S(2)}) %collective-permute-start.2) | collective-permute-done | bytes 65568 | tf_op jit(solution)/shard_map/ppermute | solution.py:67
  39.5 2.6 %collective-permute-start.3 = (f32[64,256]{1,0:T(8,128)S(1)}, f32[64,256]{1,0:T(8,128)S(1)}, u32[]{:S(2)}, u32[]{:S(2)}) collective-permute-start(f32[64,256]{1,0:T(8,128)S(1)} %fusion.64), channel_id=1, source_target_pairs={{0,16},{8,24},{16,0},{24,8},{1,17},{9,25},{17,1},{25,9},{2,18},{10... | collective-permute-start | bytes 196616 | tf_op jit(solution)/shard_map/ppermute | solution.py:67
  42.1 2.4 %collective-permute-done.3 = f32[64,256]{1,0:T(8,128)S(1)} collective-permute-done((f32[64,256]{1,0:T(8,128)S(1)}, f32[64,256]{1,0:T(8,128)S(1)}, u32[]{:S(2)}, u32[]{:S(2)}) %collective-permute-start.3) | collective-permute-done | bytes 65568 | tf_op jit(solution)/shard_map/ppermute | solution.py:67
  44.5 1.4 %collective-permute-start.4 = (bf16[32,256]{1,0:T(8,128)(2,1)S(1)}, bf16[32,256]{1,0:T(8,128)(2,1)S(1)}, u32[]{:S(2)}, u32[]{:S(2)}) collective-permute-start(bf16[32,256]{1,0:T(8,128)(2,1)S(1)} %get-tuple-element.22), channel_id=1, source_target_pairs={{0,1},{1,2},{2,3},{3,4},{4,5},{5,6},{6,7},{8,9},{9,10},{10,11},{11... | collective-permute-start | bytes 49160 | tf_op jit(solution)/shard_map/ppermute | solution.py:22
  45.9 1.3 %collective-permute-start.5 = (bf16[32,256]{1,0:T(8,128)(2,1)S(1)}, bf16[32,256]{1,0:T(8,128)(2,1)S(1)}, u32[]{:S(2)}, u32[]{:S(2)}) collective-permute-start(bf16[32,256]{1,0:T(8,128)(2,1)S(1)} %get-tuple-element.23), channel_id=1, source_target_pairs={{1,0},{2,1},{3,2},{4,3},{5,4},{6,5},{7,6},{9,8},{10,9},{11,10},{12... | collective-permute-start | bytes 49160 | tf_op jit(solution)/shard_map/ppermute | solution.py:23
  47.2 3.8 %collective-permute-done.5 = bf16[32,256]{1,0:T(8,128)(2,1)S(1)} collective-permute-done((bf16[32,256]{1,0:T(8,128)(2,1)S(1)}, bf16[32,256]{1,0:T(8,128)(2,1)S(1)}, u32[]{:S(2)}, u32[]{:S(2)}) %collective-permute-start.5) | collective-permute-done | bytes 16416 | tf_op jit(solution)/shard_map/ppermute | solution.py:23
  51.0 0.8 fusion.26.e_ref
  51.8 7.8 %shard_map.112 = f32[64,256]{1,0:T(8,128)} custom-call(f32[8,65,128]{2,1,0:T(8,128)} %get-tuple-element.33.g_ref, f32[128,384]{1,0:T(8,128)} %fusion.26.e_ref, bf16[8,64,256]{2,1,0:T(8,128)(2,1)} %w_ref.1), custom_call_target="tpu_custom_call" | custom-call | tf_op jit(solution)/shard_map/pallas_call | solution.py:252
  59.6 1.5 %collective-permute-start.6 = (f32[64,256]{1,0:T(8,128)}, f32[64,256]{1,0:T(8,128)S(1)}, u32[]{:S(2)}, u32[]{:S(2)}) collective-permute-start(f32[64,256]{1,0:T(8,128)} %shard_map.112), channel_id=1, source_target_pairs={{0,8},{8,0},{16,24},{24,16},{1,9},{9,1},{17,25},{25,17},{2,10},{10... | collective-permute-start | bytes 196616 | tf_op jit(solution)/shard_map/ppermute | solution.py:67
  61.1 3.0 %collective-permute-done.6 = f32[64,256]{1,0:T(8,128)S(1)} collective-permute-done((f32[64,256]{1,0:T(8,128)}, f32[64,256]{1,0:T(8,128)S(1)}, u32[]{:S(2)}, u32[]{:S(2)}) %collective-permute-start.6) | collective-permute-done | bytes 65568 | tf_op jit(solution)/shard_map/ppermute | solution.py:67
  64.1 0.8 add.171
  64.9 1.6 %collective-permute-start.7 = (f32[64,256]{1,0:T(8,128)S(1)}, f32[64,256]{1,0:T(8,128)S(1)}, u32[]{:S(2)}, u32[]{:S(2)}) collective-permute-start(f32[64,256]{1,0:T(8,128)S(1)} %add.171), channel_id=1, source_target_pairs={{0,16},{8,24},{16,0},{24,8},{1,17},{9,25},{17,1},{25,9},{2,18},{10... | collective-permute-start | bytes 196616 | tf_op jit(solution)/shard_map/ppermute | solution.py:67
  66.5 3.1 %collective-permute-done.7 = f32[64,256]{1,0:T(8,128)S(1)} collective-permute-done((f32[64,256]{1,0:T(8,128)S(1)}, f32[64,256]{1,0:T(8,128)S(1)}, u32[]{:S(2)}, u32[]{:S(2)}) %collective-permute-start.7) | collective-permute-done | bytes 65568 | tf_op jit(solution)/shard_map/ppermute | solution.py:67
  69.6 0.6 multiply_reduce_fusion.3
  70.2 2.7 %pad_maximum_fusion.8 = f32[4]{0:T(128)S(1)} fusion(f32[1]{0:T(128)} %bitcast.16, f32[1]{0:T(128)} %bitcast.15, f32[1]{0:T(128)} %bitcast.14, f32[1]{0:T(128)} %bitcast), kind=kLoop, calls=%fused_computation.133 | loop fusion | flops 12 | bytes 32 | tf_op jit(solution)/shard_map/stack | solution.py:281
  72.9 13.8 %psum.7 = f32[4]{0:T(128)S(1)} all-reduce(f32[4]{0:T(128)S(1)} %pad_maximum_fusion.8), channel_id=1, replica_groups=mesh['comp'=4,'band'=8] {'band'}, use_global_device_ids=true, to_apply=%region_4.5 | all-reduce | flops 4 | bytes 32 | tf_op jit(solution)/shard_map/psum | solution.py:289
  86.7 0.6 fusion.68
  91.3 0.7 multiply_add_fusion
  92.0 0.3 dynamic_update_slice.3
  92.3 0.1 fusion.32
  92.4 0.1 fusion.34
  92.5 0.1 fusion.36
  92.6 0.1 fusion.38
  92.7 0.1 fusion.40
  92.8 0.1 fusion.42
  92.9 0.1 fusion.44
  93.0 0.1 fusion.46
  93.0 0.1 fusion.30
  93.1 1.9 %fusion.18 = f32[66,66,64]{1,2,0:T(8,128)S(1)} fusion(f32[64,9,1]{0,1,2:T(8,128)S(1)} %reshape.181, f32[9,66,66]{2,1,0:T(8,128)S(1)} %fusion.30), kind=kOutput, calls=%fused_computation.20 | convolution fusion | flops 30108672 | bytes 1274256 | tf_op jit(solution)/shard_map/ct,tij->cij/dot_general | solution.py:82
  95.0 1.5 %fusion.6 = f32[9,66,66]{2,0,1:T(8,128)S(1)} fusion(f32[64,9,1]{0,1,2:T(8,128)S(1)} %reshape.182, f32[66,66,64]{1,2,0:T(8,128)S(1)} %fusion.18, f32[66,66]{1,0:T(8,128)S(1)} %and_convert_fusion, f32[64]{0:T(128)S(1)} %copy-done.6), kind=kOutput, calls=%fused_computation.10 | convolution fusion | flops 30945024 | bytes 1291936 | tf_op jit(solution)/shard_map/ct,cij->tij/dot_general | solution.py:93
  96.5 0.5 slice_add_fusion
  97.0 0.7 fusion.47
  (49 shorter events, 0.4 us)
Async XLA Ops:
  2.5 8.7 %collective-permute-start.1 = (bf16[9,32,256]{2,1,0:T(8,128)(2,1)S(1)}, bf16[9,32,256]{2,1,0:T(8,128)(2,1)S(1)}, u32[]{:S(2)}, u32[]{:S(2)}) collective-permute-start(bf16[9,32,256]{2,1,0:T(8,128)(2,1)S(1)} %pad_maximum_fusion.1), channel_id=1, source_target_pairs={{1,0},{2,1},{3,2},{4,3},{5,4},{6,5},{7,6},{9,8},{10,9},{11,10},{12... | collective-permute-start | bytes 442376 | tf_op jit(solution)/shard_map/ppermute | solution.py:56
  3.9 7.3 %collective-permute-start = (bf16[9,32,256]{2,1,0:T(8,128)(2,1)S(1)}, bf16[9,32,256]{2,1,0:T(8,128)(2,1)S(1)}, u32[]{:S(2)}, u32[]{:S(2)}) collective-permute-start(bf16[9,32,256]{2,1,0:T(8,128)(2,1)S(1)} %pad_maximum_fusion), channel_id=1, source_target_pairs={{0,1},{1,2},{2,3},{3,4},{4,5},{5,6},{6,7},{8,9},{9,10},{10,11},{11... | collective-permute-start | bytes 442376 | tf_op jit(solution)/shard_map/ppermute | solution.py:55
  11.2 26.1 %copy-start.4 = (f32[64,3,3]{0,2,1:T(4,128)S(1)}, f32[64,3,3]{0,2,1:T(4,128)}, u32[]{:S(2)}) copy-start(f32[64,3,3]{0,2,1:T(4,128)} %param.13) | copy-start | bytes 6916
  11.3 26.1 %copy-start.5 = (f32[64,3,3]{0,2,1:T(4,128)S(1)}, f32[64,3,3]{0,2,1:T(4,128)}, u32[]{:S(2)}) copy-start(f32[64,3,3]{0,2,1:T(4,128)} %param.15) | copy-start | bytes 6916
  12.8 56.8 %copy-start = (f32[64,256]{1,0:T(8,128)S(1)}, f32[64,256]{1,0:T(8,128)}, u32[]{:S(2)}) copy-start(f32[64,256]{1,0:T(8,128)} %param.10) | copy-start | bytes 196612
  12.8 56.8 %copy-start.2 = (f32[64,256]{1,0:T(8,128)S(1)}, f32[64,256]{1,0:T(8,128)}, u32[]{:S(2)}) copy-start(f32[64,256]{1,0:T(8,128)} %param.9) | copy-start | bytes 196612
  12.8 60.1 %copy-start.1 = (f32[64,256]{1,0:T(8,128)S(1)}, f32[64,256]{1,0:T(8,128)}, u32[]{:S(2)}) copy-start(f32[64,256]{1,0:T(8,128)} %param.8) | copy-start | bytes 196612
  34.2 5.3 %collective-permute-start.2 = (f32[64,256]{1,0:T(8,128)S(1)}, f32[64,256]{1,0:T(8,128)S(1)}, u32[]{:S(2)}, u32[]{:S(2)}) collective-permute-start(f32[64,256]{1,0:T(8,128)S(1)} %pad_maximum_fusion.3), channel_id=1, source_target_pairs={{0,8},{8,0},{16,24},{24,16},{1,9},{9,1},{17,25},{25,17},{2,10},{10... | collective-permute-start | bytes 196616 | tf_op jit(solution)/shard_map/ppermute | solution.py:67
  39.5 4.9 %collective-permute-start.3 = (f32[64,256]{1,0:T(8,128)S(1)}, f32[64,256]{1,0:T(8,128)S(1)}, u32[]{:S(2)}, u32[]{:S(2)}) collective-permute-start(f32[64,256]{1,0:T(8,128)S(1)} %fusion.64), channel_id=1, source_target_pairs={{0,16},{8,24},{16,0},{24,8},{1,17},{9,25},{17,1},{25,9},{2,18},{10... | collective-permute-start | bytes 196616 | tf_op jit(solution)/shard_map/ppermute | solution.py:67
  44.5 2.8 %collective-permute-start.4 = (bf16[32,256]{1,0:T(8,128)(2,1)S(1)}, bf16[32,256]{1,0:T(8,128)(2,1)S(1)}, u32[]{:S(2)}, u32[]{:S(2)}) collective-permute-start(bf16[32,256]{1,0:T(8,128)(2,1)S(1)} %get-tuple-element.22), channel_id=1, source_target_pairs={{0,1},{1,2},{2,3},{3,4},{4,5},{5,6},{6,7},{8,9},{9,10},{10,11},{11... | collective-permute-start | bytes 49160 | tf_op jit(solution)/shard_map/ppermute | solution.py:22
  45.9 5.1 %collective-permute-start.5 = (bf16[32,256]{1,0:T(8,128)(2,1)S(1)}, bf16[32,256]{1,0:T(8,128)(2,1)S(1)}, u32[]{:S(2)}, u32[]{:S(2)}) collective-permute-start(bf16[32,256]{1,0:T(8,128)(2,1)S(1)} %get-tuple-element.23), channel_id=1, source_target_pairs={{1,0},{2,1},{3,2},{4,3},{5,4},{6,5},{7,6},{9,8},{10,9},{11,10},{12... | collective-permute-start | bytes 49160 | tf_op jit(solution)/shard_map/ppermute | solution.py:23
  59.6 4.5 %collective-permute-start.6 = (f32[64,256]{1,0:T(8,128)}, f32[64,256]{1,0:T(8,128)S(1)}, u32[]{:S(2)}, u32[]{:S(2)}) collective-permute-start(f32[64,256]{1,0:T(8,128)} %shard_map.112), channel_id=1, source_target_pairs={{0,8},{8,0},{16,24},{24,16},{1,9},{9,1},{17,25},{25,17},{2,10},{10... | collective-permute-start | bytes 196616 | tf_op jit(solution)/shard_map/ppermute | solution.py:67
  64.9 4.7 %collective-permute-start.7 = (f32[64,256]{1,0:T(8,128)S(1)}, f32[64,256]{1,0:T(8,128)S(1)}, u32[]{:S(2)}, u32[]{:S(2)}) collective-permute-start(f32[64,256]{1,0:T(8,128)S(1)} %add.171), channel_id=1, source_target_pairs={{0,16},{8,24},{16,0},{24,8},{1,17},{9,25},{17,1},{25,9},{2,18},{10... | collective-permute-start | bytes 196616 | tf_op jit(solution)/shard_map/ppermute | solution.py:67
  91.3 3.7 %copy-start.6 = (f32[64]{0:T(128)S(1)}, f32[64]{0:T(128)}, u32[]{:S(2)}) copy-start(f32[64]{0:T(128)} %param.14) | copy-start | bytes 772
  92.0 4.6 %copy-start.3 = (f32[64,256]{1,0:T(8,128)}, f32[64,256]{1,0:T(8,128)S(1)}, u32[]{:S(2)}) copy-start(f32[64,256]{1,0:T(8,128)S(1)} %get-tuple-element.19) | copy-start | bytes 196612

commit v8 on v7

--- a/solution.py
+++ b/solution.py
@@ -278,15 +278,15 @@
     local_sum = back_weighted(tap_rows(kernels[:, ::-1, ::-1]), edged, weight_maps)
     normal = pair_sum(local_sum, "comp")
     curved = normal + damping * direction
-    sums = jnp.stack(
-        [
+    old, product, cross, square = lax.psum(
+        (
             jnp.sum(residual * residual),
             jnp.sum(direction * curved),
             jnp.sum(residual * curved),
             jnp.sum(curved * curved),
-        ]
-    )
-    old, product, cross, square = lax.psum(sums, "band")
+        ),
+        "band",
+    )
     alpha = old / product
     residual_next = residual - alpha * curved
     new = old - 2.0 * alpha * cross + alpha * alpha * square

time: 98.3 us -> 95.7 us (0.974)
  other arithmetic: 11.2 us -> 8.59 us
    another operation x1 -> x0, other arithmetic: 2.66 us -> none  [per_device(): jnp.stack([jnp.sum(residual * residual), jnp.sum(direction * curved), jnp...]
  transfers between devices with their start and end apart: 8 -> 8, of which waited for: 5 -> 5; matrix products, arithmetic and copies ran while one was open for 4% -> 5% of each run, Pallas kernels for 0% -> 0%
where the time goes in v8:
time: 95.7 us; the launch traced here: 95.2 us
  Pallas kernels  28.4 us (30%)
  starting transfers between devices  15.8 us (17%)
  waiting for transfers between devices  14.4 us (15%)
  blocking collectives  14.4 us (15%)
  other arithmetic  8.59 us (9%)
  local copies, waits for them, and re-layouts  5.31 us (6%)
  between operations  4.96 us (5%)
  matrix products  3.38 us (4%)
    pallas_call x1, Pallas kernels, blur(): pl.pallas_call(functools.partial(_blur_body, span=span, rows=rows, blocks...  20.6 us
    psum x1, blocking collectives, per_device(): lax.psum((jnp.sum(residual * residual), jnp.sum(direction * curved), jnp....  14.4 us
    ppermute x4, waiting for transfers between devices, pair_sum(): lax.ppermute(value, axis, [(i, i ^ step) for i in range(count)])  10.6 us
    ppermute x4, starting transfers between devices, pair_sum(): lax.ppermute(value, axis, [(i, i ^ step) for i in range(count)])  8.7 us
    pallas_call x1, Pallas kernels, back_weighted(): pl.pallas_call(functools.partial(_back_body, span=span, rows=rows, blocks...  7.8 us
    ppermute x1, waiting for transfers between devices, with_halo(): after = lax.ppermute(first, axis, down)  3.77 us
    ppermute x1, starting transfers between devices, band_halo(): before = lax.ppermute(last, 'band', up)  3.04 us
    gather x4, local copies, waits for them, and re-layouts, tap_rows(): taps = kernels.astype(jnp.float32)[:, :, jnp.clip(idx, 0, span - 1)]  2.01 us
  transfers between devices with their start and end apart: 8, of which 5 were waited for; matrix products, arithmetic and copies ran while one was open for 5% of the time, Pallas kernels for 0%

profile of v8, /device:TPU:0, one launch (start us, length us, event | category | flops | bytes accessed | tf_op | source)
XLA Modules:
  0.0 95.2 jit_solution(4190586873965690674)
XLA Ops:
  0.7 0.8 fusion.52
  1.5 1.0 %multiply_convert_fusion = bf16[8,64,256]{2,1,0:T(8,128)(2,1)S(1)} fusion(bf16[8,64,256]{2,1,0:T(8,128)(2,1)} %w_ref.1, f32[64,256]{1,0:T(8,128)} %param.10), kind=kLoop, calls=%fused_computation.22 | loop fusion | flops 393216 | bytes 589824 | tf_op jit(solution)/shard_map/convert_element_type | solution.py:268
  2.6 1.3 %collective-permute-start.1 = (bf16[9,32,256]{2,1,0:T(8,128)(2,1)S(1)}, bf16[9,32,256]{2,1,0:T(8,128)(2,1)S(1)}, u32[]{:S(2)}, u32[]{:S(2)}) collective-permute-start(bf16[9,32,256]{2,1,0:T(8,128)(2,1)S(1)} %pad_maximum_fusion.1), channel_id=1, source_target_pairs={{1,0},{2,1},{3,2},{4,3},{5,4},{6,5},{7,6},{9,8},{10,9},{11,10},{12... | collective-permute-start | bytes 442376 | tf_op jit(solution)/shard_map/ppermute | solution.py:56
  3.9 3.0 %collective-permute-start = (bf16[9,32,256]{2,1,0:T(8,128)(2,1)S(1)}, bf16[9,32,256]{2,1,0:T(8,128)(2,1)S(1)}, u32[]{:S(2)}, u32[]{:S(2)}) collective-permute-start(bf16[9,32,256]{2,1,0:T(8,128)(2,1)S(1)} %pad_maximum_fusion), channel_id=1, source_target_pairs={{0,1},{1,2},{2,3},{3,4},{4,5},{5,6},{6,7},{8,9},{9,10},{10,11},{11... | collective-permute-start | bytes 442376 | tf_op jit(solution)/shard_map/ppermute | solution.py:55
  7.0 1.1 %copy.12 = bf16[8,65,65]{1,0,2:T(8,128)(2,1)S(1)} copy(bf16[8,65,65]{2,0,1:T(8,128)(2,1)} %param.11) | data formatting | bytes 135200 | tf_op args[3]
  8.1 0.1 rev.3
  8.4 0.8 gather_fusion
  9.1 0.2 copy.13
  9.4 0.8 gather_fusion.1
  10.1 0.2 copy.15
  10.4 0.9 select_bitcast_fusion
  11.3 0.1 and_convert_fusion
  11.4 0.0 collective-permute-done
  11.4 1.5 %fusion.17.x_ref = f32[8,128,384]{2,1,0:T(8,128)} fusion(bf16[8,32,256]{2,1,0:T(8,128)(2,1)S(1)} %slice.169, bf16[8,64,256]{2,1,0:T(8,128)(2,1)S(1)} %multiply_convert_fusion, bf16[8,32,256]{2,1,0:T(8,128)(2,1)S(1)} %slice.167), kind=kLoop, calls=%fused_computation.19 | loop fusion | flops 4718592 | bytes 2097152 | tf_op jit(solution)/shard_map/jit(_pad)/pad | solution.py:273
  12.9 20.6 %shard_map.111 = f32[128,128]{1,0:T(8,128)} custom-call(f32[8,65,128]{2,1,0:T(8,128)} %get-tuple-element.32.g_ref, f32[8,128,384]{2,1,0:T(8,128)} %fusion.17.x_ref), custom_call_target="tpu_custom_call" | custom-call | tf_op jit(solution)/shard_map/pallas_call | solution.py:199
  33.5 0.8 fusion.66
  34.3 3.0 %collective-permute-start.2 = (f32[64,256]{1,0:T(8,128)S(1)}, f32[64,256]{1,0:T(8,128)S(1)}, u32[]{:S(2)}, u32[]{:S(2)}) collective-permute-start(f32[64,256]{1,0:T(8,128)S(1)} %pad_maximum_fusion.3), channel_id=1, source_target_pairs={{0,8},{8,0},{16,24},{24,16},{1,9},{9,1},{17,25},{25,17},{2,10},{10... | collective-permute-start | bytes 196616 | tf_op jit(solution)/shard_map/ppermute | solution.py:67
  37.4 2.3 %collective-permute-done.2 = f32[64,256]{1,0:T(8,128)S(1)} collective-permute-done((f32[64,256]{1,0:T(8,128)S(1)}, f32[64,256]{1,0:T(8,128)S(1)}, u32[]{:S(2)}, u32[]{:S(2)}) %collective-permute-start.2) | collective-permute-done | bytes 65568 | tf_op jit(solution)/shard_map/ppermute | solution.py:67
  39.6 2.6 %collective-permute-start.3 = (f32[64,256]{1,0:T(8,128)S(1)}, f32[64,256]{1,0:T(8,128)S(1)}, u32[]{:S(2)}, u32[]{:S(2)}) collective-permute-start(f32[64,256]{1,0:T(8,128)S(1)} %fusion.64), channel_id=1, source_target_pairs={{0,16},{8,24},{16,0},{24,8},{1,17},{9,25},{17,1},{25,9},{2,18},{10... | collective-permute-start | bytes 196616 | tf_op jit(solution)/shard_map/ppermute | solution.py:67
  42.2 2.4 %collective-permute-done.3 = f32[64,256]{1,0:T(8,128)S(1)} collective-permute-done((f32[64,256]{1,0:T(8,128)S(1)}, f32[64,256]{1,0:T(8,128)S(1)}, u32[]{:S(2)}, u32[]{:S(2)}) %collective-permute-start.3) | collective-permute-done | bytes 65568 | tf_op jit(solution)/shard_map/ppermute | solution.py:67
  44.6 1.4 %collective-permute-start.4 = (bf16[32,256]{1,0:T(8,128)(2,1)S(1)}, bf16[32,256]{1,0:T(8,128)(2,1)S(1)}, u32[]{:S(2)}, u32[]{:S(2)}) collective-permute-start(bf16[32,256]{1,0:T(8,128)(2,1)S(1)} %get-tuple-element.26), channel_id=1, source_target_pairs={{0,1},{1,2},{2,3},{3,4},{4,5},{5,6},{6,7},{8,9},{9,10},{10,11},{11... | collective-permute-start | bytes 49160 | tf_op jit(solution)/shard_map/ppermute | solution.py:22
  46.1 1.3 %collective-permute-start.5 = (bf16[32,256]{1,0:T(8,128)(2,1)S(1)}, bf16[32,256]{1,0:T(8,128)(2,1)S(1)}, u32[]{:S(2)}, u32[]{:S(2)}) collective-permute-start(bf16[32,256]{1,0:T(8,128)(2,1)S(1)} %get-tuple-element.27), channel_id=1, source_target_pairs={{1,0},{2,1},{3,2},{4,3},{5,4},{6,5},{7,6},{9,8},{10,9},{11,10},{12... | collective-permute-start | bytes 49160 | tf_op jit(solution)/shard_map/ppermute | solution.py:23
  47.4 3.8 %collective-permute-done.5 = bf16[32,256]{1,0:T(8,128)(2,1)S(1)} collective-permute-done((bf16[32,256]{1,0:T(8,128)(2,1)S(1)}, bf16[32,256]{1,0:T(8,128)(2,1)S(1)}, u32[]{:S(2)}, u32[]{:S(2)}) %collective-permute-start.5) | collective-permute-done | bytes 16416 | tf_op jit(solution)/shard_map/ppermute | solution.py:23
  51.2 0.8 fusion.26.e_ref
  51.9 7.8 %shard_map.112 = f32[64,256]{1,0:T(8,128)} custom-call(f32[8,65,128]{2,1,0:T(8,128)} %get-tuple-element.33.g_ref, f32[128,384]{1,0:T(8,128)} %fusion.26.e_ref, bf16[8,64,256]{2,1,0:T(8,128)(2,1)} %w_ref.1), custom_call_target="tpu_custom_call" | custom-call | tf_op jit(solution)/shard_map/pallas_call | solution.py:252
  59.7 1.5 %collective-permute-start.6 = (f32[64,256]{1,0:T(8,128)}, f32[64,256]{1,0:T(8,128)S(1)}, u32[]{:S(2)}, u32[]{:S(2)}) collective-permute-start(f32[64,256]{1,0:T(8,128)} %shard_map.112), channel_id=1, source_target_pairs={{0,8},{8,0},{16,24},{24,16},{1,9},{9,1},{17,25},{25,17},{2,10},{10... | collective-permute-start | bytes 196616 | tf_op jit(solution)/shard_map/ppermute | solution.py:67
  61.3 3.0 %collective-permute-done.6 = f32[64,256]{1,0:T(8,128)S(1)} collective-permute-done((f32[64,256]{1,0:T(8,128)}, f32[64,256]{1,0:T(8,128)S(1)}, u32[]{:S(2)}, u32[]{:S(2)}) %collective-permute-start.6) | collective-permute-done | bytes 65568 | tf_op jit(solution)/shard_map/ppermute | solution.py:67
  64.2 0.8 add.177
  65.1 1.6 %collective-permute-start.7 = (f32[64,256]{1,0:T(8,128)S(1)}, f32[64,256]{1,0:T(8,128)S(1)}, u32[]{:S(2)}, u32[]{:S(2)}) collective-permute-start(f32[64,256]{1,0:T(8,128)S(1)} %add.177), channel_id=1, source_target_pairs={{0,16},{8,24},{16,0},{24,8},{1,17},{9,25},{17,1},{25,9},{2,18},{10... | collective-permute-start | bytes 196616 | tf_op jit(solution)/shard_map/ppermute | solution.py:67
  66.7 3.1 %collective-permute-done.7 = f32[64,256]{1,0:T(8,128)S(1)} collective-permute-done((f32[64,256]{1,0:T(8,128)S(1)}, f32[64,256]{1,0:T(8,128)S(1)}, u32[]{:S(2)}, u32[]{:S(2)}) %collective-permute-start.7) | collective-permute-done | bytes 65568 | tf_op jit(solution)/shard_map/ppermute | solution.py:67
  69.7 0.6 multiply_reduce_fusion
  70.4 14.4 %all-reduce.5 = (f32[]{:T(128)}, f32[]{:T(128)}, f32[]{:T(128)}, f32[]{:T(128)}) all-reduce(f32[]{:T(128)} %get-tuple-element.6, f32[]{:T(128)} %get-tuple-element.7, f32[]{:T(128)} %get-tuple-element.5, f32[]{:T(128)} %get-tuple-element.4), channel_id=1, replica_groups=mesh['comp'=4,'band'=8] {'band'}, use_global_device_ids=true, to_apply=%region_1.2 | all-reduce | flops 4 | bytes 32 | tf_op jit(solution)/shard_map/psum | solution.py:281
  88.8 0.0 copy-start.6
  88.8 0.7 multiply_add_fusion
  89.5 0.3 dynamic_update_slice.3
  89.8 0.1 fusion.32
  89.9 0.1 fusion.34
  90.0 0.1 fusion.36
  90.1 0.1 fusion.38
  90.2 0.1 fusion.40
  90.3 0.1 fusion.42
  90.3 0.1 fusion.44
  90.4 0.1 fusion.46
  90.5 0.1 fusion.30
  90.6 1.9 %fusion.18 = f32[66,66,64]{1,2,0:T(8,128)S(1)} fusion(f32[64,9,1]{0,1,2:T(8,128)S(1)} %reshape.181, f32[9,66,66]{2,1,0:T(8,128)S(1)} %fusion.30), kind=kOutput, calls=%fused_computation.20 | convolution fusion | flops 30108672 | bytes 1274256 | tf_op jit(solution)/shard_map/ct,tij->cij/dot_general | solution.py:82
  92.5 1.5 %fusion.6 = f32[9,66,66]{2,0,1:T(8,128)S(1)} fusion(f32[64,9,1]{0,1,2:T(8,128)S(1)} %reshape.182, f32[66,66,64]{1,2,0:T(8,128)S(1)} %fusion.18, f32[66,66]{1,0:T(8,128)S(1)} %and_convert_fusion, f32[64]{0:T(128)S(1)} %copy-done.6), kind=kOutput, calls=%fused_computation.10 | convolution fusion | flops 30945024 | bytes 1291936 | tf_op jit(solution)/shard_map/ct,cij->tij/dot_general | solution.py:93
  94.0 0.5 slice_add_fusion
  94.5 0.7 fusion.47
  (47 shorter events, 0.4 us)
Async XLA Ops:
  0.6 7.7 %copy-start.4 = (f32[64,3,3]{0,2,1:T(4,128)S(1)}, f32[64,3,3]{0,2,1:T(4,128)}, u32[]{:S(2)}) copy-start(f32[64,3,3]{0,2,1:T(4,128)} %param.13) | copy-start | bytes 6916
  0.6 7.7 %copy-start.5 = (f32[64,3,3]{0,2,1:T(4,128)S(1)}, f32[64,3,3]{0,2,1:T(4,128)}, u32[]{:S(2)}) copy-start(f32[64,3,3]{0,2,1:T(4,128)} %param.15) | copy-start | bytes 6916
  2.6 8.8 %collective-permute-start.1 = (bf16[9,32,256]{2,1,0:T(8,128)(2,1)S(1)}, bf16[9,32,256]{2,1,0:T(8,128)(2,1)S(1)}, u32[]{:S(2)}, u32[]{:S(2)}) collective-permute-start(bf16[9,32,256]{2,1,0:T(8,128)(2,1)S(1)} %pad_maximum_fusion.1), channel_id=1, source_target_pairs={{1,0},{2,1},{3,2},{4,3},{5,4},{6,5},{7,6},{9,8},{10,9},{11,10},{12... | collective-permute-start | bytes 442376 | tf_op jit(solution)/shard_map/ppermute | solution.py:56
  3.9 7.5 %collective-permute-start = (bf16[9,32,256]{2,1,0:T(8,128)(2,1)S(1)}, bf16[9,32,256]{2,1,0:T(8,128)(2,1)S(1)}, u32[]{:S(2)}, u32[]{:S(2)}) collective-permute-start(bf16[9,32,256]{2,1,0:T(8,128)(2,1)S(1)} %pad_maximum_fusion), channel_id=1, source_target_pairs={{0,1},{1,2},{2,3},{3,4},{4,5},{5,6},{6,7},{8,9},{9,10},{10,11},{11... | collective-permute-start | bytes 442376 | tf_op jit(solution)/shard_map/ppermute | solution.py:55
  12.9 53.7 %copy-start = (f32[64,256]{1,0:T(8,128)S(1)}, f32[64,256]{1,0:T(8,128)}, u32[]{:S(2)}) copy-start(f32[64,256]{1,0:T(8,128)} %param.10) | copy-start | bytes 196612
  12.9 53.7 %copy-start.1 = (f32[64,256]{1,0:T(8,128)S(1)}, f32[64,256]{1,0:T(8,128)}, u32[]{:S(2)}) copy-start(f32[64,256]{1,0:T(8,128)} %param.8) | copy-start | bytes 196612
  12.9 56.8 %copy-start.2 = (f32[64,256]{1,0:T(8,128)S(1)}, f32[64,256]{1,0:T(8,128)}, u32[]{:S(2)}) copy-start(f32[64,256]{1,0:T(8,128)} %param.9) | copy-start | bytes 196612
  34.3 5.3 %collective-permute-start.2 = (f32[64,256]{1,0:T(8,128)S(1)}, f32[64,256]{1,0:T(8,128)S(1)}, u32[]{:S(2)}, u32[]{:S(2)}) collective-permute-start(f32[64,256]{1,0:T(8,128)S(1)} %pad_maximum_fusion.3), channel_id=1, source_target_pairs={{0,8},{8,0},{16,24},{24,16},{1,9},{9,1},{17,25},{25,17},{2,10},{10... | collective-permute-start | bytes 196616 | tf_op jit(solution)/shard_map/ppermute | solution.py:67
  39.6 5.0 %collective-permute-start.3 = (f32[64,256]{1,0:T(8,128)S(1)}, f32[64,256]{1,0:T(8,128)S(1)}, u32[]{:S(2)}, u32[]{:S(2)}) collective-permute-start(f32[64,256]{1,0:T(8,128)S(1)} %fusion.64), channel_id=1, source_target_pairs={{0,16},{8,24},{16,0},{24,8},{1,17},{9,25},{17,1},{25,9},{2,18},{10... | collective-permute-start | bytes 196616 | tf_op jit(solution)/shard_map/ppermute | solution.py:67
  44.6 2.8 %collective-permute-start.4 = (bf16[32,256]{1,0:T(8,128)(2,1)S(1)}, bf16[32,256]{1,0:T(8,128)(2,1)S(1)}, u32[]{:S(2)}, u32[]{:S(2)}) collective-permute-start(bf16[32,256]{1,0:T(8,128)(2,1)S(1)} %get-tuple-element.26), channel_id=1, source_target_pairs={{0,1},{1,2},{2,3},{3,4},{4,5},{5,6},{6,7},{8,9},{9,10},{10,11},{11... | collective-permute-start | bytes 49160 | tf_op jit(solution)/shard_map/ppermute | solution.py:22
  46.1 5.1 %collective-permute-start.5 = (bf16[32,256]{1,0:T(8,128)(2,1)S(1)}, bf16[32,256]{1,0:T(8,128)(2,1)S(1)}, u32[]{:S(2)}, u32[]{:S(2)}) collective-permute-start(bf16[32,256]{1,0:T(8,128)(2,1)S(1)} %get-tuple-element.27), channel_id=1, source_target_pairs={{1,0},{2,1},{3,2},{4,3},{5,4},{6,5},{7,6},{9,8},{10,9},{11,10},{12... | collective-permute-start | bytes 49160 | tf_op jit(solution)/shard_map/ppermute | solution.py:23
  59.7 4.5 %collective-permute-start.6 = (f32[64,256]{1,0:T(8,128)}, f32[64,256]{1,0:T(8,128)S(1)}, u32[]{:S(2)}, u32[]{:S(2)}) collective-permute-start(f32[64,256]{1,0:T(8,128)} %shard_map.112), channel_id=1, source_target_pairs={{0,8},{8,0},{16,24},{24,16},{1,9},{9,1},{17,25},{25,17},{2,10},{10... | collective-permute-start | bytes 196616 | tf_op jit(solution)/shard_map/ppermute | solution.py:67
  65.1 4.7 %collective-permute-start.7 = (f32[64,256]{1,0:T(8,128)S(1)}, f32[64,256]{1,0:T(8,128)S(1)}, u32[]{:S(2)}, u32[]{:S(2)}) collective-permute-start(f32[64,256]{1,0:T(8,128)S(1)} %add.177), channel_id=1, source_target_pairs={{0,16},{8,24},{16,0},{24,8},{1,17},{9,25},{17,1},{25,9},{2,18},{10... | collective-permute-start | bytes 196616 | tf_op jit(solution)/shard_map/ppermute | solution.py:67
  88.8 3.7 %copy-start.6 = (f32[64]{0:T(128)S(1)}, f32[64]{0:T(128)}, u32[]{:S(2)}) copy-start(f32[64]{0:T(128)} %param.14) | copy-start | bytes 772
  89.5 4.6 %copy-start.3 = (f32[64,256]{1,0:T(8,128)}, f32[64,256]{1,0:T(8,128)S(1)}, u32[]{:S(2)}) copy-start(f32[64,256]{1,0:T(8,128)S(1)} %get-tuple-element.23) | copy-start | bytes 196612

commit v9 on v8

--- a/solution.py
+++ b/solution.py
@@ -270,11 +270,11 @@
     padded, edge_before, edge_after = band_halo(shaped, edges, half, 2)
     framed_both = jnp.concatenate([edge_before, edges, edge_after], axis=1)
     framed_estimate, framed_direction = framed_both[0], framed_both[1]
-    framed = jnp.pad(padded.astype(jnp.float32), ((0, 0), (0, 0), (half, LANES - half)))
+    framed = jnp.pad(padded, ((0, 0), (0, 0), (half, LANES - half)))
     partial_value = blur(tap_rows(kernels), framed, rows)
     image = pair_sum(partial_value, "comp").astype(jnp.bfloat16)
     edged = with_halo(image, (("band", 0),), half)
-    edged = jnp.pad(edged.astype(jnp.float32), ((0, 0), (half, LANES - half)))
+    edged = jnp.pad(edged, ((0, 0), (half, LANES - half)))
     local_sum = back_weighted(tap_rows(kernels[:, ::-1, ::-1]), edged, weight_maps)
     normal = pair_sum(local_sum, "comp")
     curved = normal + damping * direction

time: 95.7 us -> 95.1 us (level)
    pad x2 -> x0, other arithmetic: 2.29 us -> none  [the longest x1 1.52 us: per_device(): jnp.pad(padded.astype(jnp.float32), ((0, 0), (0, 0), (half, LANES - half)))]
    concatenate x0 -> x2, other arithmetic: none -> 1.98 us  [the longest x1 1.25 us: band_halo(): padded = jnp.concatenate([before[:nk], shaped, after[:nk]], axis=1)]
where the time goes in v9:
time: 95.1 us; the launch traced here: 94.6 us
  Pallas kernels  28.1 us (30%)
  starting transfers between devices  15.8 us (17%)
  waiting for transfers between devices  14.4 us (15%)
  blocking collectives  14.4 us (15%)
  other arithmetic  8.28 us (9%)
  local copies, waits for them, and re-layouts  5.32 us (6%)
  between operations  4.98 us (5%)
  matrix products  3.38 us (4%)
    pallas_call x1, Pallas kernels, blur(): pl.pallas_call(functools.partial(_blur_body, span=span, rows=rows, blocks...  20.4 us
    psum x1, blocking collectives, per_device(): lax.psum((jnp.sum(residual * residual), jnp.sum(direction * curved), jnp....  14.4 us
    ppermute x4, waiting for transfers between devices, pair_sum(): lax.ppermute(value, axis, [(i, i ^ step) for i in range(count)])  10.6 us
    ppermute x4, starting transfers between devices, pair_sum(): lax.ppermute(value, axis, [(i, i ^ step) for i in range(count)])  8.69 us
    pallas_call x1, Pallas kernels, back_weighted(): pl.pallas_call(functools.partial(_back_body, span=span, rows=rows, blocks...  7.72 us
    ppermute x1, waiting for transfers between devices, with_halo(): after = lax.ppermute(first, axis, down)  3.77 us
    ppermute x1, starting transfers between devices, band_halo(): before = lax.ppermute(last, 'band', up)  3.04 us
    gather x4, local copies, waits for them, and re-layouts, tap_rows(): taps = kernels.astype(jnp.float32)[:, :, jnp.clip(idx, 0, span - 1)]  2.01 us
  transfers between devices with their start and end apart: 8, of which 5 were waited for; matrix products, arithmetic and copies ran while one was open for 5% of the time, Pallas kernels for 0%

profile of v9, /device:TPU:0, one launch (start us, length us, event | category | flops | bytes accessed | tf_op | source)
XLA Modules:
  0.0 94.6 jit_solution(3741599196767668981)
XLA Ops:
  0.7 0.8 fusion.50
  1.5 1.0 %multiply_convert_fusion = bf16[8,64,256]{2,1,0:T(8,128)(2,1)S(1)} fusion(bf16[8,64,256]{2,1,0:T(8,128)(2,1)} %w_ref.1, f32[64,256]{1,0:T(8,128)} %param.10), kind=kLoop, calls=%fused_computation.21 | loop fusion | flops 393216 | bytes 589824 | tf_op jit(solution)/shard_map/convert_element_type | solution.py:268
  2.6 1.3 %collective-permute-start.1 = (bf16[9,32,256]{2,1,0:T(8,128)(2,1)S(1)}, bf16[9,32,256]{2,1,0:T(8,128)(2,1)S(1)}, u32[]{:S(2)}, u32[]{:S(2)}) collective-permute-start(bf16[9,32,256]{2,1,0:T(8,128)(2,1)S(1)} %pad_maximum_fusion.1), channel_id=1, source_target_pairs={{1,0},{2,1},{3,2},{4,3},{5,4},{6,5},{7,6},{9,8},{10,9},{11,10},{12... | collective-permute-start | bytes 442376 | tf_op jit(solution)/shard_map/ppermute | solution.py:56
  3.9 3.0 %collective-permute-start = (bf16[9,32,256]{2,1,0:T(8,128)(2,1)S(1)}, bf16[9,32,256]{2,1,0:T(8,128)(2,1)S(1)}, u32[]{:S(2)}, u32[]{:S(2)}) collective-permute-start(bf16[9,32,256]{2,1,0:T(8,128)(2,1)S(1)} %pad_maximum_fusion), channel_id=1, source_target_pairs={{0,1},{1,2},{2,3},{3,4},{4,5},{5,6},{6,7},{8,9},{9,10},{10,11},{11... | collective-permute-start | bytes 442376 | tf_op jit(solution)/shard_map/ppermute | solution.py:55
  7.0 1.1 %copy.12 = bf16[8,65,65]{1,0,2:T(8,128)(2,1)S(1)} copy(bf16[8,65,65]{2,0,1:T(8,128)(2,1)} %param.11) | data formatting | bytes 135200 | tf_op args[3]
  8.1 0.1 rev.3
  8.4 0.8 gather_fusion
  9.1 0.2 copy.13
  9.4 0.8 gather_fusion.1
  10.1 0.2 copy.15
  10.4 0.9 select_bitcast_fusion
  11.3 0.1 and_convert_fusion
  11.4 0.0 copy-start
  11.4 0.0 copy-start.2
  11.4 1.3 %fusion.16.x_ref = bf16[8,128,384]{2,1,0:T(8,128)(2,1)} fusion(bf16[8,32,256]{2,1,0:T(8,128)(2,1)S(1)} %slice.169, bf16[8,64,256]{2,1,0:T(8,128)(2,1)S(1)} %multiply_convert_fusion, bf16[8,32,256]{2,1,0:T(8,128)(2,1)S(1)} %slice.167), kind=kLoop, calls=%fused_computation.18 | loop fusion | flops 4718592 | bytes 1310720 | tf_op jit(solution)/shard_map/concatenate | solution.py:59
  12.7 20.4 %shard_map.111 = f32[128,128]{1,0:T(8,128)} custom-call(f32[8,65,128]{2,1,0:T(8,128)} %get-tuple-element.32.g_ref, bf16[8,128,384]{2,1,0:T(8,128)(2,1)} %fusion.16.x_ref), custom_call_target="tpu_custom_call" | custom-call | tf_op jit(solution)/shard_map/pallas_call | solution.py:199
  33.1 0.8 fusion.64
  33.9 3.0 %collective-permute-start.2 = (f32[64,256]{1,0:T(8,128)S(1)}, f32[64,256]{1,0:T(8,128)S(1)}, u32[]{:S(2)}, u32[]{:S(2)}) collective-permute-start(f32[64,256]{1,0:T(8,128)S(1)} %pad_maximum_fusion.3), channel_id=1, source_target_pairs={{0,8},{8,0},{16,24},{24,16},{1,9},{9,1},{17,25},{25,17},{2,10},{10... | collective-permute-start | bytes 196616 | tf_op jit(solution)/shard_map/ppermute | solution.py:67
  36.9 2.3 %collective-permute-done.2 = f32[64,256]{1,0:T(8,128)S(1)} collective-permute-done((f32[64,256]{1,0:T(8,128)S(1)}, f32[64,256]{1,0:T(8,128)S(1)}, u32[]{:S(2)}, u32[]{:S(2)}) %collective-permute-start.2) | collective-permute-done | bytes 65568 | tf_op jit(solution)/shard_map/ppermute | solution.py:67
  39.2 2.6 %collective-permute-start.3 = (f32[64,256]{1,0:T(8,128)S(1)}, f32[64,256]{1,0:T(8,128)S(1)}, u32[]{:S(2)}, u32[]{:S(2)}) collective-permute-start(f32[64,256]{1,0:T(8,128)S(1)} %fusion.62), channel_id=1, source_target_pairs={{0,16},{8,24},{16,0},{24,8},{1,17},{9,25},{17,1},{25,9},{2,18},{10... | collective-permute-start | bytes 196616 | tf_op jit(solution)/shard_map/ppermute | solution.py:67
  41.8 2.4 %collective-permute-done.3 = f32[64,256]{1,0:T(8,128)S(1)} collective-permute-done((f32[64,256]{1,0:T(8,128)S(1)}, f32[64,256]{1,0:T(8,128)S(1)}, u32[]{:S(2)}, u32[]{:S(2)}) %collective-permute-start.3) | collective-permute-done | bytes 65568 | tf_op jit(solution)/shard_map/ppermute | solution.py:67
  44.2 1.4 %collective-permute-start.4 = (bf16[32,256]{1,0:T(8,128)(2,1)S(1)}, bf16[32,256]{1,0:T(8,128)(2,1)S(1)}, u32[]{:S(2)}, u32[]{:S(2)}) collective-permute-start(bf16[32,256]{1,0:T(8,128)(2,1)S(1)} %get-tuple-element.26), channel_id=1, source_target_pairs={{0,1},{1,2},{2,3},{3,4},{4,5},{5,6},{6,7},{8,9},{9,10},{10,11},{11... | collective-permute-start | bytes 49160 | tf_op jit(solution)/shard_map/ppermute | solution.py:22
  45.6 1.3 %collective-permute-start.5 = (bf16[32,256]{1,0:T(8,128)(2,1)S(1)}, bf16[32,256]{1,0:T(8,128)(2,1)S(1)}, u32[]{:S(2)}, u32[]{:S(2)}) collective-permute-start(bf16[32,256]{1,0:T(8,128)(2,1)S(1)} %get-tuple-element.27), channel_id=1, source_target_pairs={{1,0},{2,1},{3,2},{4,3},{5,4},{6,5},{7,6},{9,8},{10,9},{11,10},{12... | collective-permute-start | bytes 49160 | tf_op jit(solution)/shard_map/ppermute | solution.py:23
  46.9 3.8 %collective-permute-done.5 = bf16[32,256]{1,0:T(8,128)(2,1)S(1)} collective-permute-done((bf16[32,256]{1,0:T(8,128)(2,1)S(1)}, bf16[32,256]{1,0:T(8,128)(2,1)S(1)}, u32[]{:S(2)}, u32[]{:S(2)}) %collective-permute-start.5) | collective-permute-done | bytes 16416 | tf_op jit(solution)/shard_map/ppermute | solution.py:23
  50.7 0.7 fusion.24.e_ref
  51.4 7.7 %shard_map.112 = f32[64,256]{1,0:T(8,128)} custom-call(f32[8,65,128]{2,1,0:T(8,128)} %get-tuple-element.33.g_ref, bf16[128,384]{1,0:T(8,128)(2,1)} %fusion.24.e_ref, bf16[8,64,256]{2,1,0:T(8,128)(2,1)} %w_ref.1), custom_call_target="tpu_custom_call" | custom-call | tf_op jit(solution)/shard_map/pallas_call | solution.py:252
  59.1 1.5 %collective-permute-start.6 = (f32[64,256]{1,0:T(8,128)}, f32[64,256]{1,0:T(8,128)S(1)}, u32[]{:S(2)}, u32[]{:S(2)}) collective-permute-start(f32[64,256]{1,0:T(8,128)} %shard_map.112), channel_id=1, source_target_pairs={{0,8},{8,0},{16,24},{24,16},{1,9},{9,1},{17,25},{25,17},{2,10},{10... | collective-permute-start | bytes 196616 | tf_op jit(solution)/shard_map/ppermute | solution.py:67
  60.7 3.0 %collective-permute-done.6 = f32[64,256]{1,0:T(8,128)S(1)} collective-permute-done((f32[64,256]{1,0:T(8,128)}, f32[64,256]{1,0:T(8,128)S(1)}, u32[]{:S(2)}, u32[]{:S(2)}) %collective-permute-start.6) | collective-permute-done | bytes 65568 | tf_op jit(solution)/shard_map/ppermute | solution.py:67
  63.6 0.8 add.177
  64.5 1.6 %collective-permute-start.7 = (f32[64,256]{1,0:T(8,128)S(1)}, f32[64,256]{1,0:T(8,128)S(1)}, u32[]{:S(2)}, u32[]{:S(2)}) collective-permute-start(f32[64,256]{1,0:T(8,128)S(1)} %add.177), channel_id=1, source_target_pairs={{0,16},{8,24},{16,0},{24,8},{1,17},{9,25},{17,1},{25,9},{2,18},{10... | collective-permute-start | bytes 196616 | tf_op jit(solution)/shard_map/ppermute | solution.py:67
  66.1 3.1 %collective-permute-done.7 = f32[64,256]{1,0:T(8,128)S(1)} collective-permute-done((f32[64,256]{1,0:T(8,128)S(1)}, f32[64,256]{1,0:T(8,128)S(1)}, u32[]{:S(2)}, u32[]{:S(2)}) %collective-permute-start.7) | collective-permute-done | bytes 65568 | tf_op jit(solution)/shard_map/ppermute | solution.py:67
  69.1 0.6 multiply_reduce_fusion
  69.8 14.4 %all-reduce.5 = (f32[]{:T(128)}, f32[]{:T(128)}, f32[]{:T(128)}, f32[]{:T(128)}) all-reduce(f32[]{:T(128)} %get-tuple-element.6, f32[]{:T(128)} %get-tuple-element.7, f32[]{:T(128)} %get-tuple-element.5, f32[]{:T(128)} %get-tuple-element.4), channel_id=1, replica_groups=mesh['comp'=4,'band'=8] {'band'}, use_global_device_ids=true, to_apply=%region_1.2 | all-reduce | flops 4 | bytes 32 | tf_op jit(solution)/shard_map/psum | solution.py:281
  88.2 0.7 multiply_add_fusion
  88.9 0.3 dynamic_update_slice.3
  89.2 0.1 fusion.30
  89.3 0.1 fusion.32
  89.4 0.1 fusion.34
  89.5 0.1 fusion.36
  89.6 0.1 fusion.38
  89.7 0.1 fusion.40
  89.7 0.1 fusion.42
  89.8 0.1 fusion.44
  89.9 0.1 fusion.28
  90.0 1.9 %fusion.17 = f32[66,66,64]{1,2,0:T(8,128)S(1)} fusion(f32[64,9,1]{0,1,2:T(8,128)S(1)} %reshape.181, f32[9,66,66]{2,1,0:T(8,128)S(1)} %fusion.28), kind=kOutput, calls=%fused_computation.19 | convolution fusion | flops 30108672 | bytes 1274256 | tf_op jit(solution)/shard_map/ct,tij->cij/dot_general | solution.py:82
  91.9 1.5 %fusion.6 = f32[9,66,66]{2,0,1:T(8,128)S(1)} fusion(f32[64,9,1]{0,1,2:T(8,128)S(1)} %reshape.182, f32[66,66,64]{1,2,0:T(8,128)S(1)} %fusion.17, f32[66,66]{1,0:T(8,128)S(1)} %and_convert_fusion, f32[64]{0:T(128)S(1)} %copy-done.6), kind=kOutput, calls=%fused_computation.10 | convolution fusion | flops 30945024 | bytes 1291936 | tf_op jit(solution)/shard_map/ct,cij->tij/dot_general | solution.py:93
  93.4 0.5 slice_add_fusion
  93.9 0.7 fusion.45
  (47 shorter events, 0.4 us)
Async XLA Ops:
  0.6 7.7 %copy-start.4 = (f32[64,3,3]{0,2,1:T(4,128)S(1)}, f32[64,3,3]{0,2,1:T(4,128)}, u32[]{:S(2)}) copy-start(f32[64,3,3]{0,2,1:T(4,128)} %param.13) | copy-start | bytes 6916
  0.6 7.7 %copy-start.5 = (f32[64,3,3]{0,2,1:T(4,128)S(1)}, f32[64,3,3]{0,2,1:T(4,128)}, u32[]{:S(2)}) copy-start(f32[64,3,3]{0,2,1:T(4,128)} %param.15) | copy-start | bytes 6916
  2.6 8.8 %collective-permute-start.1 = (bf16[9,32,256]{2,1,0:T(8,128)(2,1)S(1)}, bf16[9,32,256]{2,1,0:T(8,128)(2,1)S(1)}, u32[]{:S(2)}, u32[]{:S(2)}) collective-permute-start(bf16[9,32,256]{2,1,0:T(8,128)(2,1)S(1)} %pad_maximum_fusion.1), channel_id=1, source_target_pairs={{1,0},{2,1},{3,2},{4,3},{5,4},{6,5},{7,6},{9,8},{10,9},{11,10},{12... | collective-permute-start | bytes 442376 | tf_op jit(solution)/shard_map/ppermute | solution.py:56
  3.9 7.5 %collective-permute-start = (bf16[9,32,256]{2,1,0:T(8,128)(2,1)S(1)}, bf16[9,32,256]{2,1,0:T(8,128)(2,1)S(1)}, u32[]{:S(2)}, u32[]{:S(2)}) collective-permute-start(bf16[9,32,256]{2,1,0:T(8,128)(2,1)S(1)} %pad_maximum_fusion), channel_id=1, source_target_pairs={{0,1},{1,2},{2,3},{3,4},{4,5},{5,6},{6,7},{8,9},{9,10},{10,11},{11... | collective-permute-start | bytes 442376 | tf_op jit(solution)/shard_map/ppermute | solution.py:55
  11.4 54.7 %copy-start = (f32[64,256]{1,0:T(8,128)S(1)}, f32[64,256]{1,0:T(8,128)}, u32[]{:S(2)}) copy-start(f32[64,256]{1,0:T(8,128)} %param.10) | copy-start | bytes 196612
  11.4 54.6 %copy-start.1 = (f32[64,256]{1,0:T(8,128)S(1)}, f32[64,256]{1,0:T(8,128)}, u32[]{:S(2)}) copy-start(f32[64,256]{1,0:T(8,128)} %param.8) | copy-start | bytes 196612
  11.4 57.7 %copy-start.2 = (f32[64,256]{1,0:T(8,128)S(1)}, f32[64,256]{1,0:T(8,128)}, u32[]{:S(2)}) copy-start(f32[64,256]{1,0:T(8,128)} %param.9) | copy-start | bytes 196612
  33.9 5.3 %collective-permute-start.2 = (f32[64,256]{1,0:T(8,128)S(1)}, f32[64,256]{1,0:T(8,128)S(1)}, u32[]{:S(2)}, u32[]{:S(2)}) collective-permute-start(f32[64,256]{1,0:T(8,128)S(1)} %pad_maximum_fusion.3), channel_id=1, source_target_pairs={{0,8},{8,0},{16,24},{24,16},{1,9},{9,1},{17,25},{25,17},{2,10},{10... | collective-permute-start | bytes 196616 | tf_op jit(solution)/shard_map/ppermute | solution.py:67
  39.2 4.9 %collective-permute-start.3 = (f32[64,256]{1,0:T(8,128)S(1)}, f32[64,256]{1,0:T(8,128)S(1)}, u32[]{:S(2)}, u32[]{:S(2)}) collective-permute-start(f32[64,256]{1,0:T(8,128)S(1)} %fusion.62), channel_id=1, source_target_pairs={{0,16},{8,24},{16,0},{24,8},{1,17},{9,25},{17,1},{25,9},{2,18},{10... | collective-permute-start | bytes 196616 | tf_op jit(solution)/shard_map/ppermute | solution.py:67
  44.2 2.8 %collective-permute-start.4 = (bf16[32,256]{1,0:T(8,128)(2,1)S(1)}, bf16[32,256]{1,0:T(8,128)(2,1)S(1)}, u32[]{:S(2)}, u32[]{:S(2)}) collective-permute-start(bf16[32,256]{1,0:T(8,128)(2,1)S(1)} %get-tuple-element.26), channel_id=1, source_target_pairs={{0,1},{1,2},{2,3},{3,4},{4,5},{5,6},{6,7},{8,9},{9,10},{10,11},{11... | collective-permute-start | bytes 49160 | tf_op jit(solution)/shard_map/ppermute | solution.py:22
  45.6 5.1 %collective-permute-start.5 = (bf16[32,256]{1,0:T(8,128)(2,1)S(1)}, bf16[32,256]{1,0:T(8,128)(2,1)S(1)}, u32[]{:S(2)}, u32[]{:S(2)}) collective-permute-start(bf16[32,256]{1,0:T(8,128)(2,1)S(1)} %get-tuple-element.27), channel_id=1, source_target_pairs={{1,0},{2,1},{3,2},{4,3},{5,4},{6,5},{7,6},{9,8},{10,9},{11,10},{12... | collective-permute-start | bytes 49160 | tf_op jit(solution)/shard_map/ppermute | solution.py:23
  59.1 4.5 %collective-permute-start.6 = (f32[64,256]{1,0:T(8,128)}, f32[64,256]{1,0:T(8,128)S(1)}, u32[]{:S(2)}, u32[]{:S(2)}) collective-permute-start(f32[64,256]{1,0:T(8,128)} %shard_map.112), channel_id=1, source_target_pairs={{0,8},{8,0},{16,24},{24,16},{1,9},{9,1},{17,25},{25,17},{2,10},{10... | collective-permute-start | bytes 196616 | tf_op jit(solution)/shard_map/ppermute | solution.py:67
  64.5 4.7 %collective-permute-start.7 = (f32[64,256]{1,0:T(8,128)S(1)}, f32[64,256]{1,0:T(8,128)S(1)}, u32[]{:S(2)}, u32[]{:S(2)}) collective-permute-start(f32[64,256]{1,0:T(8,128)S(1)} %add.177), channel_id=1, source_target_pairs={{0,16},{8,24},{16,0},{24,8},{1,17},{9,25},{17,1},{25,9},{2,18},{10... | collective-permute-start | bytes 196616 | tf_op jit(solution)/shard_map/ppermute | solution.py:67
  88.2 3.7 %copy-start.6 = (f32[64]{0:T(128)S(1)}, f32[64]{0:T(128)}, u32[]{:S(2)}) copy-start(f32[64]{0:T(128)} %param.14) | copy-start | bytes 772
  88.9 4.6 %copy-start.3 = (f32[64,256]{1,0:T(8,128)}, f32[64,256]{1,0:T(8,128)S(1)}, u32[]{:S(2)}) copy-start(f32[64,256]{1,0:T(8,128)S(1)} %get-tuple-element.23) | copy-start | bytes 196612

commit v10 on v9

--- a/solution.py
+++ b/solution.py
@@ -271,11 +271,13 @@
     framed_both = jnp.concatenate([edge_before, edges, edge_after], axis=1)
     framed_estimate, framed_direction = framed_both[0], framed_both[1]
     framed = jnp.pad(padded, ((0, 0), (0, 0), (half, LANES - half)))
-    partial_value = blur(tap_rows(kernels), framed, rows)
+    both_taps = tap_rows(jnp.concatenate([kernels, kernels[:, ::-1, ::-1]]))
+    nk = kernels.shape[0]
+    partial_value = blur(both_taps[:nk], framed, rows)
     image = pair_sum(partial_value, "comp").astype(jnp.bfloat16)
     edged = with_halo(image, (("band", 0),), half)
     edged = jnp.pad(edged, ((0, 0), (half, LANES - half)))
-    local_sum = back_weighted(tap_rows(kernels[:, ::-1, ::-1]), edged, weight_maps)
+    local_sum = back_weighted(both_taps[nk:], edged, weight_maps)
     normal = pair_sum(local_sum, "comp")
     curved = normal + damping * direction
     old, product, cross, square = lax.psum(

time: 95.1 us -> 94.9 us (level)
    gather x4 -> x2, local copies, waits for them, and re-layouts: 2.01 us -> 1.21 us  [tap_rows(): taps = kernels.astype(jnp.float32)[:, :, jnp.clip(idx, 0, span - 1)]]
  transfers between devices with their start and end apart: 8 -> 8, of which waited for: 5 -> 5; matrix products, arithmetic and copies ran while one was open for 5% -> 4% of each run, Pallas kernels for 0% -> 0%
where the time goes in v10:
time: 94.9 us; the launch traced here: 94.3 us
  Pallas kernels  28.1 us (30%)
  starting transfers between devices  15.8 us (17%)
  waiting for transfers between devices  14.4 us (15%)
  blocking collectives  14.4 us (15%)
  other arithmetic  7.48 us (8%)
  local copies, waits for them, and re-layouts  5.89 us (6%)
  between operations  4.93 us (5%)
  matrix products  3.38 us (4%)
    pallas_call x1, Pallas kernels, blur(): pl.pallas_call(functools.partial(_blur_body, span=span, rows=rows, blocks...  20.4 us
    psum x1, blocking collectives, per_device(): lax.psum((jnp.sum(residual * residual), jnp.sum(direction * curved), jnp....  14.4 us
    ppermute x4, waiting for transfers between devices, pair_sum(): lax.ppermute(value, axis, [(i, i ^ step) for i in range(count)])  10.6 us
    ppermute x4, starting transfers between devices, pair_sum(): lax.ppermute(value, axis, [(i, i ^ step) for i in range(count)])  8.71 us
    pallas_call x1, Pallas kernels, back_weighted(): pl.pallas_call(functools.partial(_back_body, span=span, rows=rows, blocks...  7.72 us
    ppermute x1, waiting for transfers between devices, with_halo(): after = lax.ppermute(first, axis, down)  3.77 us
    ppermute x1, starting transfers between devices, band_halo(): before = lax.ppermute(last, 'band', up)  3.04 us
  transfers between devices with their start and end apart: 8, of which 5 were waited for; matrix products, arithmetic and copies ran while one was open for 4% of the time, Pallas kernels for 0%

profile of v10, /device:TPU:0, one launch (start us, length us, event | category | flops | bytes accessed | tf_op | source)
XLA Modules:
  0.0 94.3 jit_solution(17313139273155642241)
XLA Ops:
  0.6 0.8 fusion.50
  1.5 1.0 %multiply_convert_fusion = bf16[8,64,256]{2,1,0:T(8,128)(2,1)S(1)} fusion(bf16[8,64,256]{2,1,0:T(8,128)(2,1)} %w_ref.1, f32[64,256]{1,0:T(8,128)} %param.10), kind=kLoop, calls=%fused_computation.21 | loop fusion | flops 393216 | bytes 589824 | tf_op jit(solution)/shard_map/convert_element_type | solution.py:268
  2.6 1.3 %collective-permute-start.1 = (bf16[9,32,256]{2,1,0:T(8,128)(2,1)S(1)}, bf16[9,32,256]{2,1,0:T(8,128)(2,1)S(1)}, u32[]{:S(2)}, u32[]{:S(2)}) collective-permute-start(bf16[9,32,256]{2,1,0:T(8,128)(2,1)S(1)} %pad_maximum_fusion.1), channel_id=1, source_target_pairs={{1,0},{2,1},{3,2},{4,3},{5,4},{6,5},{7,6},{9,8},{10,9},{11,10},{12... | collective-permute-start | bytes 442376 | tf_op jit(solution)/shard_map/ppermute | solution.py:56
  3.9 3.0 %collective-permute-start = (bf16[9,32,256]{2,1,0:T(8,128)(2,1)S(1)}, bf16[9,32,256]{2,1,0:T(8,128)(2,1)S(1)}, u32[]{:S(2)}, u32[]{:S(2)}) collective-permute-start(bf16[9,32,256]{2,1,0:T(8,128)(2,1)S(1)} %pad_maximum_fusion), channel_id=1, source_target_pairs={{0,1},{1,2},{2,3},{3,4},{4,5},{5,6},{6,7},{8,9},{9,10},{10,11},{11... | collective-permute-start | bytes 442376 | tf_op jit(solution)/shard_map/ppermute | solution.py:55
  7.0 0.7 reshape.173
  7.7 0.7 reshape.174
  8.4 0.2 copy.13
  8.6 0.1 rev.3
  8.8 0.8 gather_fusion
  9.6 0.5 copy.14
  10.1 0.9 fusion.63
  11.0 0.1 and_convert_fusion
  11.1 0.0 copy-start
  11.1 0.0 copy-start.2
  11.2 1.3 %fusion.16.x_ref = bf16[8,128,384]{2,1,0:T(8,128)(2,1)} fusion(bf16[8,32,256]{2,1,0:T(8,128)(2,1)S(1)} %slice.177, bf16[8,64,256]{2,1,0:T(8,128)(2,1)S(1)} %multiply_convert_fusion, bf16[8,32,256]{2,1,0:T(8,128)(2,1)S(1)} %slice.175), kind=kLoop, calls=%fused_computation.17 | loop fusion | flops 4718592 | bytes 1310720 | tf_op jit(solution)/shard_map/concatenate | solution.py:59
  12.4 20.4 %shard_map.111 = f32[128,128]{1,0:T(8,128)} custom-call(f32[8,65,128]{2,1,0:T(8,128)} %get-tuple-element.19.g_ref, bf16[8,128,384]{2,1,0:T(8,128)(2,1)} %fusion.16.x_ref), custom_call_target="tpu_custom_call" | custom-call | tf_op jit(solution)/shard_map/pallas_call | solution.py:199
  32.8 0.8 fusion.65
  33.6 3.0 %collective-permute-start.2 = (f32[64,256]{1,0:T(8,128)S(1)}, f32[64,256]{1,0:T(8,128)S(1)}, u32[]{:S(2)}, u32[]{:S(2)}) collective-permute-start(f32[64,256]{1,0:T(8,128)S(1)} %pad_maximum_fusion.3), channel_id=1, source_target_pairs={{0,8},{8,0},{16,24},{24,16},{1,9},{9,1},{17,25},{25,17},{2,10},{10... | collective-permute-start | bytes 196616 | tf_op jit(solution)/shard_map/ppermute | solution.py:67
  36.6 2.3 %collective-permute-done.2 = f32[64,256]{1,0:T(8,128)S(1)} collective-permute-done((f32[64,256]{1,0:T(8,128)S(1)}, f32[64,256]{1,0:T(8,128)S(1)}, u32[]{:S(2)}, u32[]{:S(2)}) %collective-permute-start.2) | collective-permute-done | bytes 65568 | tf_op jit(solution)/shard_map/ppermute | solution.py:67
  38.9 2.6 %collective-permute-start.3 = (f32[64,256]{1,0:T(8,128)S(1)}, f32[64,256]{1,0:T(8,128)S(1)}, u32[]{:S(2)}, u32[]{:S(2)}) collective-permute-start(f32[64,256]{1,0:T(8,128)S(1)} %fusion.62), channel_id=1, source_target_pairs={{0,16},{8,24},{16,0},{24,8},{1,17},{9,25},{17,1},{25,9},{2,18},{10... | collective-permute-start | bytes 196616 | tf_op jit(solution)/shard_map/ppermute | solution.py:67
  41.5 2.4 %collective-permute-done.3 = f32[64,256]{1,0:T(8,128)S(1)} collective-permute-done((f32[64,256]{1,0:T(8,128)S(1)}, f32[64,256]{1,0:T(8,128)S(1)}, u32[]{:S(2)}, u32[]{:S(2)}) %collective-permute-start.3) | collective-permute-done | bytes 65568 | tf_op jit(solution)/shard_map/ppermute | solution.py:67
  43.9 1.4 %collective-permute-start.4 = (bf16[32,256]{1,0:T(8,128)(2,1)S(1)}, bf16[32,256]{1,0:T(8,128)(2,1)S(1)}, u32[]{:S(2)}, u32[]{:S(2)}) collective-permute-start(bf16[32,256]{1,0:T(8,128)(2,1)S(1)} %get-tuple-element.28), channel_id=1, source_target_pairs={{0,1},{1,2},{2,3},{3,4},{4,5},{5,6},{6,7},{8,9},{9,10},{10,11},{11... | collective-permute-start | bytes 49160 | tf_op jit(solution)/shard_map/ppermute | solution.py:22
  45.3 1.3 %collective-permute-start.5 = (bf16[32,256]{1,0:T(8,128)(2,1)S(1)}, bf16[32,256]{1,0:T(8,128)(2,1)S(1)}, u32[]{:S(2)}, u32[]{:S(2)}) collective-permute-start(bf16[32,256]{1,0:T(8,128)(2,1)S(1)} %get-tuple-element.29), channel_id=1, source_target_pairs={{1,0},{2,1},{3,2},{4,3},{5,4},{6,5},{7,6},{9,8},{10,9},{11,10},{12... | collective-permute-start | bytes 49160 | tf_op jit(solution)/shard_map/ppermute | solution.py:23
  46.6 3.8 %collective-permute-done.5 = bf16[32,256]{1,0:T(8,128)(2,1)S(1)} collective-permute-done((bf16[32,256]{1,0:T(8,128)(2,1)S(1)}, bf16[32,256]{1,0:T(8,128)(2,1)S(1)}, u32[]{:S(2)}, u32[]{:S(2)}) %collective-permute-start.5) | collective-permute-done | bytes 16416 | tf_op jit(solution)/shard_map/ppermute | solution.py:23
  50.4 0.7 fusion.24.e_ref
  51.1 7.7 %shard_map.112 = f32[64,256]{1,0:T(8,128)} custom-call(f32[8,65,128]{2,1,0:T(8,128)} %get-tuple-element.20.g_ref, bf16[128,384]{1,0:T(8,128)(2,1)} %fusion.24.e_ref, bf16[8,64,256]{2,1,0:T(8,128)(2,1)} %w_ref.1), custom_call_target="tpu_custom_call" | custom-call | tf_op jit(solution)/shard_map/pallas_call | solution.py:252
  58.8 1.5 %collective-permute-start.6 = (f32[64,256]{1,0:T(8,128)}, f32[64,256]{1,0:T(8,128)S(1)}, u32[]{:S(2)}, u32[]{:S(2)}) collective-permute-start(f32[64,256]{1,0:T(8,128)} %shard_map.112), channel_id=1, source_target_pairs={{0,8},{8,0},{16,24},{24,16},{1,9},{9,1},{17,25},{25,17},{2,10},{10... | collective-permute-start | bytes 196616 | tf_op jit(solution)/shard_map/ppermute | solution.py:67
  60.4 2.9 %collective-permute-done.6 = f32[64,256]{1,0:T(8,128)S(1)} collective-permute-done((f32[64,256]{1,0:T(8,128)}, f32[64,256]{1,0:T(8,128)S(1)}, u32[]{:S(2)}, u32[]{:S(2)}) %collective-permute-start.6) | collective-permute-done | bytes 65568 | tf_op jit(solution)/shard_map/ppermute | solution.py:67
  63.3 0.8 add.168
  64.2 1.6 %collective-permute-start.7 = (f32[64,256]{1,0:T(8,128)S(1)}, f32[64,256]{1,0:T(8,128)S(1)}, u32[]{:S(2)}, u32[]{:S(2)}) collective-permute-start(f32[64,256]{1,0:T(8,128)S(1)} %add.168), channel_id=1, source_target_pairs={{0,16},{8,24},{16,0},{24,8},{1,17},{9,25},{17,1},{25,9},{2,18},{10... | collective-permute-start | bytes 196616 | tf_op jit(solution)/shard_map/ppermute | solution.py:67
  65.8 3.0 %collective-permute-done.7 = f32[64,256]{1,0:T(8,128)S(1)} collective-permute-done((f32[64,256]{1,0:T(8,128)S(1)}, f32[64,256]{1,0:T(8,128)S(1)}, u32[]{:S(2)}, u32[]{:S(2)}) %collective-permute-start.7) | collective-permute-done | bytes 65568 | tf_op jit(solution)/shard_map/ppermute | solution.py:67
  68.9 0.6 multiply_reduce_fusion
  69.5 14.4 %all-reduce.5 = (f32[]{:T(128)}, f32[]{:T(128)}, f32[]{:T(128)}, f32[]{:T(128)}) all-reduce(f32[]{:T(128)} %get-tuple-element.6, f32[]{:T(128)} %get-tuple-element.7, f32[]{:T(128)} %get-tuple-element.5, f32[]{:T(128)} %get-tuple-element.4), channel_id=1, replica_groups=mesh['comp'=4,'band'=8] {'band'}, use_global_device_ids=true, to_apply=%region_1.2 | all-reduce | flops 4 | bytes 32 | tf_op jit(solution)/shard_map/psum | solution.py:283
  87.9 0.7 multiply_add_fusion
  88.6 0.3 dynamic_update_slice.3
  88.9 0.1 fusion.30
  89.0 0.1 fusion.32
  89.1 0.1 fusion.34
  89.2 0.1 fusion.36
  89.3 0.1 fusion.38
  89.4 0.1 fusion.40
  89.5 0.1 fusion.42
  89.5 0.1 fusion.44
  89.6 0.1 fusion.28
  89.7 1.9 %fusion.17 = f32[66,66,64]{1,2,0:T(8,128)S(1)} fusion(f32[64,9,1]{0,1,2:T(8,128)S(1)} %reshape.173, f32[9,66,66]{2,1,0:T(8,128)S(1)} %fusion.28), kind=kOutput, calls=%fused_computation.19 | convolution fusion | flops 30108672 | bytes 1274256 | tf_op jit(solution)/shard_map/ct,tij->cij/dot_general | solution.py:82
  91.6 1.5 %fusion.6 = f32[9,66,66]{2,0,1:T(8,128)S(1)} fusion(f32[64,9,1]{0,1,2:T(8,128)S(1)} %reshape.174, f32[66,66,64]{1,2,0:T(8,128)S(1)} %fusion.17, f32[66,66]{1,0:T(8,128)S(1)} %and_convert_fusion, f32[64]{0:T(128)S(1)} %copy-done.5), kind=kOutput, calls=%fused_computation.9 | convolution fusion | flops 30945024 | bytes 1291936 | tf_op jit(solution)/shard_map/ct,cij->tij/dot_general | solution.py:93
  93.1 0.5 slice_add_fusion
  93.6 0.7 fusion.45
  (43 shorter events, 0.4 us)
Async XLA Ops:
  0.6 7.8 %copy-start.4 = (bf16[8,65,65]{2,0,1:T(8,128)(2,1)S(1)}, bf16[8,65,65]{2,0,1:T(8,128)(2,1)}, u32[]{:S(2)}) copy-start(bf16[8,65,65]{2,0,1:T(8,128)(2,1)} %param.11) | copy-start | bytes 202804
  2.6 8.5 %collective-permute-start.1 = (bf16[9,32,256]{2,1,0:T(8,128)(2,1)S(1)}, bf16[9,32,256]{2,1,0:T(8,128)(2,1)S(1)}, u32[]{:S(2)}, u32[]{:S(2)}) collective-permute-start(bf16[9,32,256]{2,1,0:T(8,128)(2,1)S(1)} %pad_maximum_fusion.1), channel_id=1, source_target_pairs={{1,0},{2,1},{3,2},{4,3},{5,4},{6,5},{7,6},{9,8},{10,9},{11,10},{12... | collective-permute-start | bytes 442376 | tf_op jit(solution)/shard_map/ppermute | solution.py:56
  3.9 7.2 %collective-permute-start = (bf16[9,32,256]{2,1,0:T(8,128)(2,1)S(1)}, bf16[9,32,256]{2,1,0:T(8,128)(2,1)S(1)}, u32[]{:S(2)}, u32[]{:S(2)}) collective-permute-start(bf16[9,32,256]{2,1,0:T(8,128)(2,1)S(1)} %pad_maximum_fusion), channel_id=1, source_target_pairs={{0,1},{1,2},{2,3},{3,4},{4,5},{5,6},{6,7},{8,9},{9,10},{10,11},{11... | collective-permute-start | bytes 442376 | tf_op jit(solution)/shard_map/ppermute | solution.py:55
  11.1 54.7 %copy-start = (f32[64,256]{1,0:T(8,128)S(1)}, f32[64,256]{1,0:T(8,128)}, u32[]{:S(2)}) copy-start(f32[64,256]{1,0:T(8,128)} %param.10) | copy-start | bytes 196612
  11.1 54.7 %copy-start.1 = (f32[64,256]{1,0:T(8,128)S(1)}, f32[64,256]{1,0:T(8,128)}, u32[]{:S(2)}) copy-start(f32[64,256]{1,0:T(8,128)} %param.8) | copy-start | bytes 196612
  11.1 57.7 %copy-start.2 = (f32[64,256]{1,0:T(8,128)S(1)}, f32[64,256]{1,0:T(8,128)}, u32[]{:S(2)}) copy-start(f32[64,256]{1,0:T(8,128)} %param.9) | copy-start | bytes 196612
  33.6 5.3 %collective-permute-start.2 = (f32[64,256]{1,0:T(8,128)S(1)}, f32[64,256]{1,0:T(8,128)S(1)}, u32[]{:S(2)}, u32[]{:S(2)}) collective-permute-start(f32[64,256]{1,0:T(8,128)S(1)} %pad_maximum_fusion.3), channel_id=1, source_target_pairs={{0,8},{8,0},{16,24},{24,16},{1,9},{9,1},{17,25},{25,17},{2,10},{10... | collective-permute-start | bytes 196616 | tf_op jit(solution)/shard_map/ppermute | solution.py:67
  38.9 4.9 %collective-permute-start.3 = (f32[64,256]{1,0:T(8,128)S(1)}, f32[64,256]{1,0:T(8,128)S(1)}, u32[]{:S(2)}, u32[]{:S(2)}) collective-permute-start(f32[64,256]{1,0:T(8,128)S(1)} %fusion.62), channel_id=1, source_target_pairs={{0,16},{8,24},{16,0},{24,8},{1,17},{9,25},{17,1},{25,9},{2,18},{10... | collective-permute-start | bytes 196616 | tf_op jit(solution)/shard_map/ppermute | solution.py:67
  43.9 2.8 %collective-permute-start.4 = (bf16[32,256]{1,0:T(8,128)(2,1)S(1)}, bf16[32,256]{1,0:T(8,128)(2,1)S(1)}, u32[]{:S(2)}, u32[]{:S(2)}) collective-permute-start(bf16[32,256]{1,0:T(8,128)(2,1)S(1)} %get-tuple-element.28), channel_id=1, source_target_pairs={{0,1},{1,2},{2,3},{3,4},{4,5},{5,6},{6,7},{8,9},{9,10},{10,11},{11... | collective-permute-start | bytes 49160 | tf_op jit(solution)/shard_map/ppermute | solution.py:22
  45.3 5.1 %collective-permute-start.5 = (bf16[32,256]{1,0:T(8,128)(2,1)S(1)}, bf16[32,256]{1,0:T(8,128)(2,1)S(1)}, u32[]{:S(2)}, u32[]{:S(2)}) collective-permute-start(bf16[32,256]{1,0:T(8,128)(2,1)S(1)} %get-tuple-element.29), channel_id=1, source_target_pairs={{1,0},{2,1},{3,2},{4,3},{5,4},{6,5},{7,6},{9,8},{10,9},{11,10},{12... | collective-permute-start | bytes 49160 | tf_op jit(solution)/shard_map/ppermute | solution.py:23
  58.8 4.5 %collective-permute-start.6 = (f32[64,256]{1,0:T(8,128)}, f32[64,256]{1,0:T(8,128)S(1)}, u32[]{:S(2)}, u32[]{:S(2)}) collective-permute-start(f32[64,256]{1,0:T(8,128)} %shard_map.112), channel_id=1, source_target_pairs={{0,8},{8,0},{16,24},{24,16},{1,9},{9,1},{17,25},{25,17},{2,10},{10... | collective-permute-start | bytes 196616 | tf_op jit(solution)/shard_map/ppermute | solution.py:67
  64.2 4.7 %collective-permute-start.7 = (f32[64,256]{1,0:T(8,128)S(1)}, f32[64,256]{1,0:T(8,128)S(1)}, u32[]{:S(2)}, u32[]{:S(2)}) collective-permute-start(f32[64,256]{1,0:T(8,128)S(1)} %add.168), channel_id=1, source_target_pairs={{0,16},{8,24},{16,0},{24,8},{1,17},{9,25},{17,1},{25,9},{2,18},{10... | collective-permute-start | bytes 196616 | tf_op jit(solution)/shard_map/ppermute | solution.py:67
  87.9 3.7 %copy-start.5 = (f32[64]{0:T(128)S(1)}, f32[64]{0:T(128)}, u32[]{:S(2)}) copy-start(f32[64]{0:T(128)} %param.14) | copy-start | bytes 772
  88.6 4.6 %copy-start.3 = (f32[64,256]{1,0:T(8,128)}, f32[64,256]{1,0:T(8,128)S(1)}, u32[]{:S(2)}) copy-start(f32[64,256]{1,0:T(8,128)S(1)} %get-tuple-element.25) | copy-start | bytes 196612
